TPU v7x, 32 devices: a whole 2x2x4 slice. The times are simulated.
32 devices in a mesh: grp: 2 (over y), seq: 4 (over z), head: 2 (over x), sub: 2 (over core).
Axes of the slice: x: 2, y: 2, z: 4, core: 2. Of those that a mesh axis runs over, the one named last changes fastest.
Arguments:
- query_rows: bfloat16 [3072, 1024], P(('grp', 'seq', 'sub'), 'head'), parts along dimension 0, may hold values from -8 to 8
- key_rows: bfloat16 [3072, 1024], P(('grp', 'seq', 'sub'), 'head'), parts along dimension 0, may hold values from -8 to 8
- value_rows: bfloat16 [3072, 1024], P(('grp', 'seq', 'sub'), 'head'), parts along dimension 0, may hold values from -8 to 8
- clip_lengths: int32 [12], P('grp'), parts along dimension 0, may hold values from 1 to 768, 1536 in all
- block_mask: int32 [48, 24], P(('grp', 'seq')), parts along dimension 0, may hold values from 0 to 1, as said below
- out_weight: bfloat16 [1024, 1024], replicated
- norm_gain: bfloat16 [1024], P('head'), may hold values from 0.099609375 to 1.8984375
Outputs:
- layer_output: bfloat16 [3072, 1024], P(('grp', 'seq', 'sub'), 'head'), parts along dimension 0
There are 2 independent parts, one for each index of `grp`. A program takes and returns all parts, laid end to end along the dimension named above; an argument that names none is the same for every part. Nothing has to cross between parts.
Inputs may be any that keep to these rules, and one draw needn't show every extreme that they name: `clip_lengths`: 6 clip lengths that sum to 1536; the longest is exactly 768. block_mask[i, i] = 1 for every block i.
All inputs are finite; a program needn't handle non-finite values.
Results may differ from a plain program's by a relative error of at most 0.01.
Values may be sent and summed in bfloat16 or wider, within the bound.
No kernel may reach another device: no remote copies, remote signals or barrier semaphores. Data moves between devices by JAX's collectives and lax.ppermute only.
A program may use at most 64 MiB of HBM per device.

v0:
```python
import functools
import math

import jax
import jax.numpy as jnp
from jax.experimental import pallas as pl
from jax.experimental.pallas import tpu as pltpu
from jax import lax
from jax.sharding import PartitionSpec as P

HD = 64
BLK = 64
F = 64


def clip_index(positions, clip_ends):
    return jnp.sum((clip_ends[None, :] <= positions[:, None]).astype(jnp.int32), axis=1)


def shifted(x, axis, count, step):
    pairs = [(i + step, i) for i in range(count) if 0 <= i + step < count]
    return lax.ppermute(x, axis, pairs)


def rotated(x, axis, count, step):
    return lax.ppermute(x, axis, [(i, (i + step) % count) for i in range(count)])


def chunk_kernel(sources, has_state, final, flags_ref, q_ref, code_ref, qclip_ref, *refs):
    n_in = max(src for src, _ in sources) + 1
    kv_refs = refs[:n_in]
    rest = refs[n_in:]
    if has_state:
        m_in, l_in, acc_in = rest[:3]
        rest = rest[3:]
    if final:
        out_ref, m_ref, l_ref, acc_ref = rest
    else:
        m_ref, l_ref, acc_ref = rest
    row_count, col_count = acc_ref.shape
    sub_rows = code_ref.shape[1]
    piece = row_count // sub_rows
    pair = 2 * HD
    scale = 1.0 / math.sqrt(HD)
    if has_state:
        m_ref[...] = m_in[...]
        l_ref[...] = l_in[...]
        acc_ref[...] = acc_in[...]
    else:
        m_ref[...] = jnp.full(m_ref.shape, -1e30, jnp.float32)
        l_ref[...] = jnp.zeros(l_ref.shape, jnp.float32)
        acc_ref[...] = jnp.zeros(acc_ref.shape, jnp.float32)
    qclip = qclip_ref[...]
    low = lax.broadcasted_iota(jnp.int32, (row_count, pair), 1) < HD
    for b, (src, idx) in enumerate(sources):

        @pl.when(flags_ref[b] > 0)
        def _():
            code = code_ref[b]
            allowed = jnp.concatenate(
                [
                    jnp.broadcast_to(
                        qclip[i * piece : (i + 1) * piece] == code[i : i + 1, :],
                        (piece, code.shape[1]),
                    )
                    for i in range(sub_rows)
                ],
                axis=0,
            )
            bias = jnp.where(allowed, 0.0, -1e30).astype(jnp.float32)
            for hp in range(col_count // pair):
                cols = slice(hp * pair, (hp + 1) * pair)
                k_p = kv_refs[src][idx, 0, :, cols]
                v_p = kv_refs[src][idx, 1, :, cols]
                m_p = m_ref[:, cols]
                halves = []
                for e in range(2):
                    q_e = q_ref[e, :, cols]
                    s = lax.dot_general(
                        q_e, k_p, (((1,), (1,)), ((), ())), preferred_element_type=jnp.float32
                    )
                    s = s * scale + bias
                    m_old = m_p[:, e * HD : e * HD + 1]
                    m_new = jnp.maximum(m_old, jnp.max(s, axis=1, keepdims=True))
                    alpha = jnp.exp(m_old - m_new)
                    p = jnp.exp(s - m_new)
                    total = jnp.sum(p, axis=1, keepdims=True)
                    pv = jnp.dot(p.astype(jnp.bfloat16), v_p, preferred_element_type=jnp.float32)
                    halves.append((m_new, alpha, total, pv))
                (m0, a0, t0, pv0), (m1, a1, t1, pv1) = halves
                alpha = jnp.where(low, a0, a1)
                m_ref[:, cols] = jnp.where(low, m0, m1)
                l_ref[:, cols] = alpha * l_ref[:, cols] + jnp.where(low, t0, t1)
                acc_ref[:, cols] = alpha * acc_ref[:, cols] + jnp.where(low, pv0, pv1)

    if final:
        out_ref[...] = (acc_ref[...] / l_ref[...]).astype(out_ref.dtype)


def attend_chunk(state_now, q_split, query_clip, mask_rows, clip_ends, total, inputs, blocks):
    block_total = mask_rows.shape[1]
    sub_rows = mask_rows.shape[0]
    key_pos = jnp.stack([pos for _, _, pos in blocks])
    key_block = key_pos // BLK
    valid = (key_pos >= 0) & (key_pos < total)
    live = jnp.take(mask_rows, jnp.clip(key_block, 0, block_total - 1), axis=1)
    live = (live == 1) & valid[None]
    key_clip = clip_index(key_pos.reshape(-1), clip_ends).reshape(key_pos.shape)
    code = jnp.where(live, key_clip[None], -1).transpose(1, 0, 2)
    query_sub = query_clip.reshape(sub_rows, -1)
    flags = jnp.any(
        query_sub[None, :, :, None] == code[:, :, None, :], axis=(1, 2, 3)
    ).astype(jnp.int32)
    sources = tuple((src, idx) for src, idx, _ in blocks)
    n_in = len(inputs)
    has_state = state_now is not None
    final = not has_state
    row_count, col_count = q_split.shape[1:]
    state_shape = jax.ShapeDtypeStruct((row_count, col_count), jnp.float32)
    if final:
        out_shape = jax.ShapeDtypeStruct((row_count, col_count), jnp.bfloat16)
        out_specs = pl.BlockSpec(memory_space=pltpu.VMEM)
        scratch = [pltpu.VMEM((row_count, col_count), jnp.float32)] * 3
        aliases = {}
        extra = ()
    else:
        out_shape = (state_shape,) * 3
        out_specs = [pl.BlockSpec(memory_space=pltpu.VMEM)] * 3
        scratch = []
        aliases = {4 + n_in: 0, 5 + n_in: 1, 6 + n_in: 2}
        extra = tuple(state_now)
    return pl.pallas_call(
        functools.partial(chunk_kernel, sources, has_state, final),
        out_shape=out_shape,
        in_specs=[pl.BlockSpec(memory_space=pltpu.SMEM)]
        + [pl.BlockSpec(memory_space=pltpu.VMEM)] * (3 + n_in + len(extra)),
        out_specs=out_specs,
        scratch_shapes=scratch,
        input_output_aliases=aliases,
        cost_estimate=pl.CostEstimate(
            flops=len(blocks) * 8 * row_count**2 * col_count,
            transcendentals=len(blocks) * 2 * row_count**2 * col_count // HD,
            bytes_accessed=sum(x.size * x.dtype.itemsize for x in inputs) + 8 * q_split.size,
        ),
    )(flags, q_split, code, query_clip[:, None], *inputs, *extra)


def body(query_rows, key_rows, value_rows, clip_lengths, block_mask, out_weight, norm_gain):
    row_count, col_count = query_rows.shape
    head_count = col_count // HD
    n_seq = lax.axis_size("seq")
    n_sub = lax.axis_size("sub")
    n_head = lax.axis_size("head")
    seq_i = lax.axis_index("seq")
    sub_i = lax.axis_index("sub")
    head_i = lax.axis_index("head")
    chip_rows = row_count * n_sub
    total = chip_rows * n_seq
    longest = total // 2
    reach = min(n_seq - 1, 1 + (longest - 2) // chip_rows)

    clip_ends = jnp.cumsum(clip_lengths)
    token_first = (seq_i * n_sub + sub_i) * row_count
    mask_height = row_count // BLK
    mask_rows = lax.dynamic_slice_in_dim(block_mask, sub_i * mask_height, mask_height, 0)
    query_clip = clip_index(token_first + jnp.arange(row_count, dtype=jnp.int32), clip_ends)
    local_pos = jnp.arange(row_count, dtype=jnp.int32)

    def block_pos(seq_off, sub_src):
        return ((seq_i + seq_off) * n_sub + sub_src) * row_count + local_pos

    lane = lax.broadcasted_iota(jnp.int32, (1, col_count), 1) % (2 * HD)
    q_split = jnp.stack(
        [jnp.where(lane < HD, query_rows, 0), jnp.where(lane >= HD, query_rows, 0)]
    ).astype(jnp.bfloat16)

    def fold(state_now, mine, theirs):
        inputs = [kv[None] for kv, _ in mine]
        blocks = [(n, 0, block_pos(off, sub_i)) for n, (_, off) in enumerate(mine)]
        for got, offs, src in theirs:
            blocks += [(len(inputs), b, block_pos(off, src)) for b, off in enumerate(offs)]
            inputs.append(got)
        return attend_chunk(
            state_now, q_split, query_clip, mask_rows, clip_ends, total, inputs, blocks
        )

    def to_partner(mine):
        offs = [jnp.asarray(off, jnp.int32) for _, off in mine]
        return [
            (jnp.stack([rotated(kv, "sub", n_sub, j) for kv, _ in mine]), offs, (sub_i - j) % n_sub)
            for j in range(1, n_sub)
        ]

    own = jnp.stack([key_rows, value_rows])
    if reach <= 4:
        mine = [(own, 0)]
        theirs = to_partner(mine)
        left = own
        right = own
        for step in range(1, reach + 1):
            right = shifted(right, "seq", n_seq, 1)
            left = shifted(left, "seq", n_seq, -1)
            near = [(left, -step), (right, step)]
            mine += near
            theirs += to_partner(near)
        attended = fold(None, mine, theirs)
    else:
        state = (
            jnp.full((row_count, col_count), -1e30, jnp.float32),
            jnp.zeros((row_count, col_count), jnp.float32),
            jnp.zeros((row_count, col_count), jnp.float32),
        )
        state = fold(state, [(own, 0)], [])
        pending = to_partner([(own, 0)])

        def seq_step(step, carry):
            state_now, left, right, pending_now = carry
            right = shifted(right, "seq", n_seq, 1)
            left = shifted(left, "seq", n_seq, -1)
            near = [(left, -step), (right, step)]
            state_now = fold(state_now, near, pending_now)
            return (state_now, left, right, to_partner(near))

        carry = seq_step(1, (state, own, own, pending))
        carry = lax.fori_loop(2, reach + 1, seq_step, carry)
        state = fold(carry[0], [], carry[3])
        row_max, running, weighted = state
        attended = (weighted / running).astype(jnp.bfloat16)

    n_dev = n_seq * n_sub

    def flat(dev, head):
        return ((dev // n_sub) * n_head + head) * n_sub + dev % n_sub

    pieces = {-1: attended[row_count - F :], 0: attended, 1: attended[:F]}
    width = out_weight.shape[1]
    projected = jnp.zeros((row_count + 2 * F, width), jnp.float32)
    for j in range(n_head):
        parts = []
        for d in (-1, 0, 1):
            if j == 0 and d == 0:
                parts.append(attended)
                continue
            pairs = [
                (flat(i + d, (h + j) % n_head), flat(i, h))
                for i in range(n_dev)
                for h in range(n_head)
                if 0 <= i + d < n_dev
            ]
            parts.append(lax.ppermute(pieces[d], ("seq", "head", "sub"), pairs))
        src = (head_i + j) % n_head
        projected = projected + jnp.dot(
            jnp.concatenate(parts, axis=0),
            lax.dynamic_slice_in_dim(out_weight, src * col_count, col_count, 0),
            preferred_element_type=jnp.float32,
        )

    positions = token_first + jnp.arange(row_count, dtype=jnp.int32)
    clip_here = clip_index(positions, clip_ends)
    earlier = jnp.where(
        (clip_index(positions - F, clip_ends) == clip_here)[:, None], projected[:row_count], 0.0
    )
    later = jnp.where(
        (clip_index(positions + F, clip_ends) == clip_here)[:, None], projected[2 * F :], 0.0
    )
    blended = projected[F : F + row_count] + 0.5 * (earlier + later)
    squares = jnp.sum(blended * blended, axis=1)
    scale = lax.rsqrt(squares / width + 1e-06)
    own_cols = lax.dynamic_slice_in_dim(blended, head_i * col_count, col_count, 1)
    return (own_cols * scale[:, None] * norm_gain.astype(jnp.float32)).astype(jnp.bfloat16)


def solution(mesh):
    placed = (
        P(("grp", "seq", "sub"), "head"),
        P(("grp", "seq", "sub"), "head"),
        P(("grp", "seq", "sub"), "head"),
        P("grp"),
        P(("grp", "seq"), None),
        P(),
        P("head"),
    )
    return jax.shard_map(
        body,
        mesh=mesh,
        in_specs=placed,
        out_specs=P(("grp", "seq", "sub"), "head"),
        check_vma=False,
    )
```

profile of v0, /device:TPU:20, one launch (start us, length us, event | category | flops | bytes accessed | tf_op | source)
XLA Modules:
  0.0 78.7 jit_solution(463040836801444759)
XLA Ops:
  0.0 0.0 copy-start
  0.0 2.0 %pad_maximum_fusion.3 = (bf16[2,192,512]{2,1,0:T(8,128)(2,1)S(1)}, bf16[1,2,192,512]{3,2,1,0:T(8,128)(2,1)}) fusion(bf16[1,192,512]{2,1,0:T(8,128)(2,1)} %bitcast.45, bf16[1,192,512]{2,1,0:T(8,128)(2,1)} %bitcast.46), kind=kLoop, calls=%fused_computation.15 | loop fusion | flops 196608 | bytes 1179648 | tf_op jit(solution)/shard_map/stack | solution.py:194
  2.0 3.5 %collective-permute-start = (bf16[2,192,512]{2,1,0:T(8,128)(2,1)S(1)}, bf16[2,192,512]{2,1,0:T(8,128)(2,1)}, u32[]{:S(2)}, u32[]{:S(2)}) collective-permute-start(bf16[2,192,512]{2,1,0:T(8,128)(2,1)S(1)} %get-tuple-element.10), channel_id=1, source_target_pairs={{0,4},{4,8},{8,12},{1,5},{5,9},{9,13},{2,6},{6,10},{10,14},{3,7},{... | collective-permute-start | bytes 1179656 | tf_op jit(solution)/shard_map/ppermute | solution.py:22
  5.5 2.4 %collective-permute-start.1 = (bf16[2,192,512]{2,1,0:T(8,128)(2,1)S(1)}, bf16[2,192,512]{2,1,0:T(8,128)(2,1)}, u32[]{:S(2)}, u32[]{:S(2)}) collective-permute-start(bf16[2,192,512]{2,1,0:T(8,128)(2,1)S(1)} %get-tuple-element.10), channel_id=1, source_target_pairs={{4,0},{8,4},{12,8},{5,1},{9,5},{13,9},{6,2},{10,6},{14,10},{7,3},{... | collective-permute-start | bytes 1179656 | tf_op jit(solution)/shard_map/ppermute | solution.py:22
  7.8 0.1 collective-permute-start.4
  8.1 0.1 stack.74
  8.1 0.1 le.36
  8.3 0.1 fusion.20
  8.4 0.1 reshape.622
  8.5 0.8 %reduce-window.8 = s32[6,1]{0,1:T(1,128)S(1)} reduce-window(s32[6,1]{0,1:T(1,128)} %bitcast.50, s32[]{:T(128)} %constant.93.clone.1), window={size=6x1 pad=5_0x0_0}, to_apply=%region_0.0 | reduce-window | flops 30 | bytes 52 | tf_op jit(solution)/shard_map/reduce-window.3
  9.4 0.1 convert_reduce_fusion
  9.5 0.7 constant_dynamic-slice_fusion
  10.2 0.1 copy.19
  10.2 3.5 %gather_fusion = s32[1920,3]{1,0:T(8,128)S(1)} fusion(s32[3,24]{0,1:T(8,128)S(1)} %copy.19, s32[2048]{0:T(1024)S(1)} %pad_clamp_fusion), kind=kCustom, calls=%fused_computation | custom fusion | bytes 53760 | tf_op jit(solution)/shard_map/jit(_take)/gather | solution.py:106
  13.7 0.4 copy.15
  14.1 0.1 broadcast_in_dim.95
  14.2 0.0 copy-start.2
  14.3 0.6 collective-permute-done
  14.8 3.5 %collective-permute-start.2 = (bf16[2,192,512]{2,1,0:T(8,128)(2,1)}, bf16[2,192,512]{2,1,0:T(8,128)(2,1)}, u32[]{:S(2)}, u32[]{:S(2)}) collective-permute-start(bf16[2,192,512]{2,1,0:T(8,128)(2,1)} %collective-permute-done), channel_id=1, source_target_pairs={{0,4},{4,8},{8,12},{1,5},{5,9},{9,13},{2,6},{6,10},{10,14},{3,7},{... | collective-permute-start | bytes 1179656 | tf_op jit(solution)/shard_map/ppermute | solution.py:22
  18.4 0.0 collective-permute-done.1
  18.4 2.3 %collective-permute-start.3 = (bf16[2,192,512]{2,1,0:T(8,128)(2,1)}, bf16[2,192,512]{2,1,0:T(8,128)(2,1)}, u32[]{:S(2)}, u32[]{:S(2)}) collective-permute-start(bf16[2,192,512]{2,1,0:T(8,128)(2,1)} %collective-permute-done.1), channel_id=1, source_target_pairs={{4,0},{8,4},{12,8},{5,1},{9,5},{13,9},{6,2},{10,6},{14,10},{7,3},{... | collective-permute-start | bytes 1179656 | tf_op jit(solution)/shard_map/ppermute | solution.py:22
  20.7 1.0 %select_bitcast_fusion.1 = (bf16[1,192,512]{2,1,0:T(8,128)(2,1)S(1)}, bf16[1,192,512]{2,1,0:T(8,128)(2,1)S(1)}) fusion(bf16[192,512]{1,0:T(8,128)(2,1)} %param.7, pred[512]{0:T(512)(128)(4,1)S(1)} %get-tuple-element.33, pred[512]{0:T(512)(128)(4,1)S(1)} %get-tuple-element.32), kind=kLoop, calls=%fused_computation.28 | loop fusion | flops 196608 | bytes 590848 | tf_op jit(solution)/shard_map/stack | solution.py:173
  21.7 0.1 collective-permute-start.5
  21.7 0.5 collective-permute-start.6
  22.2 5.7 %collective-permute-done.2 = bf16[2,192,512]{2,1,0:T(8,128)(2,1)} collective-permute-done((bf16[2,192,512]{2,1,0:T(8,128)(2,1)}, bf16[2,192,512]{2,1,0:T(8,128)(2,1)}, u32[]{:S(2)}, u32[]{:S(2)}) %collective-permute-start.2) | collective-permute-done | bytes 393248 | tf_op jit(solution)/shard_map/ppermute | solution.py:22
  27.9 0.0 collective-permute-start.7
  27.9 3.9 %collective-permute-done.3 = bf16[2,192,512]{2,1,0:T(8,128)(2,1)} collective-permute-done((bf16[2,192,512]{2,1,0:T(8,128)(2,1)}, bf16[2,192,512]{2,1,0:T(8,128)(2,1)}, u32[]{:S(2)}, u32[]{:S(2)}) %collective-permute-start.3) | collective-permute-done | bytes 393248 | tf_op jit(solution)/shard_map/ppermute | solution.py:22
  31.8 0.0 collective-permute-start.8
  31.8 0.1 convert_reduce_fusion.2
  31.9 0.1 eq.45
  32.0 0.6 compare_reduce_fusion
  32.6 0.5 convert_element_type.27.flags_ref
  33.1 0.8 copy.16.qclip_ref
  33.8 0.8 pad_maximum_fusion.2.q_ref
  34.6 0.0 collective-permute-done.5
  34.6 0.0 collective-permute-done.6
  34.6 2.0 %pad_maximum_fusion.refs_6_ = bf16[2,2,192,512]{3,2,1,0:T(8,128)(2,1)} fusion(bf16[1,2,192,512]{3,2,1,0:T(8,128)(2,1)} %bitcast.26, bf16[1,2,192,512]{3,2,1,0:T(8,128)(2,1)S(1)} %bitcast.44), kind=kLoop, calls=%fused_computation.11 | loop fusion | flops 393216 | bytes 1572864 | tf_op jit(solution)/shard_map/stack | solution.py:190
  36.6 0.0 collective-permute-done.7
  36.6 0.0 collective-permute-done.8
  36.6 2.1 %pad_maximum_fusion.1.refs_7_ = bf16[2,2,192,512]{3,2,1,0:T(8,128)(2,1)} fusion(bf16[1,2,192,512]{3,2,1,0:T(8,128)(2,1)} %bitcast.28, bf16[1,2,192,512]{3,2,1,0:T(8,128)(2,1)} %bitcast.27), kind=kLoop, calls=%fused_computation.12 | loop fusion | flops 393216 | bytes 1572864 | tf_op jit(solution)/shard_map/stack | solution.py:190
  38.7 0.0 copy-done.2
  38.7 0.0 collective-permute-done.4
  38.7 0.0 copy-start.3
  38.7 19.4 %shard_map.73 = bf16[192,512]{1,0:T(8,128)(2,1)} custom-call(s32[10]{0:T(128)} %convert_element_type.27.flags_ref, bf16[2,192,512]{2,1,0:T(8,128)(2,1)} %pad_maximum_fusion.2.q_ref, s32[10,3,192]{2,1,0:T(4,128)} %copy-done.2, s32[192,1]{1,0:T(8,128)} %copy.16.qclip_ref, bf16[1,2,192,512]{3,2,1,0:T(8,128)(2,1)} %get-tuple-element.11.refs_0_, ...), custom_call_target="tpu_custom_call" | custom-call | flops 1509949440 | bytes 5505024 | tf_op jit(solution)/shard_map/pallas_call | solution.py:132
  58.1 0.0 copy-start.1
  58.1 0.9 %fusion.34 = (bf16[64,512]{1,0:T(8,128)(2,1)S(1)}, bf16[64,512]{1,0:T(8,128)(2,1)S(1)}) fusion(bf16[192,512]{1,0:T(8,128)(2,1)} %shard_map.73), kind=kLoop, calls=%fused_computation.91 | loop fusion | bytes 262144 | tf_op jit(solution)/shard_map/slice | solution.py:235
  59.0 1.6 %collective-permute-start.12 = (bf16[192,512]{1,0:T(8,128)(2,1)}, bf16[192,512]{1,0:T(8,128)(2,1)S(1)}, u32[]{:S(2)}, u32[]{:S(2)}) collective-permute-start(bf16[192,512]{1,0:T(8,128)(2,1)} %shard_map.73), channel_id=1, source_target_pairs={{2,0},{0,2},{3,1},{1,3},{6,4},{4,6},{7,5},{5,7},{10,8},{8,10},{11,... | collective-permute-start | bytes 589832 | tf_op jit(solution)/shard_map/ppermute | solution.py:250
  60.6 1.9 %collective-permute-start.11 = (bf16[64,512]{1,0:T(8,128)(2,1)S(1)}, bf16[64,512]{1,0:T(8,128)(2,1)S(1)}, u32[]{:S(2)}, u32[]{:S(2)}) collective-permute-start(bf16[64,512]{1,0:T(8,128)(2,1)S(1)} %get-tuple-element.12), channel_id=1, source_target_pairs={{2,1},{0,3},{3,4},{1,6},{6,5},{4,7},{7,8},{5,10},{10,9},{8,11},{11... | collective-permute-start | bytes 196616 | tf_op jit(solution)/shard_map/ppermute | solution.py:250
  62.5 5.2 %collective-permute-start.13 = (bf16[64,512]{1,0:T(8,128)(2,1)S(1)}, bf16[64,512]{1,0:T(8,128)(2,1)S(1)}, u32[]{:S(2)}, u32[]{:S(2)}) collective-permute-start(bf16[64,512]{1,0:T(8,128)(2,1)S(1)} %get-tuple-element.13), channel_id=1, source_target_pairs={{3,0},{1,2},{6,1},{4,3},{7,4},{5,6},{10,5},{8,7},{11,8},{9,10},{14... | collective-permute-start | bytes 196616 | tf_op jit(solution)/shard_map/ppermute | solution.py:250
  67.7 0.0 copy-done.3
  67.8 3.7 %collective-permute-start.10 = (bf16[64,512]{1,0:T(8,128)(2,1)S(1)}, bf16[64,512]{1,0:T(8,128)(2,1)S(1)}, u32[]{:S(2)}, u32[]{:S(2)}) collective-permute-start(bf16[64,512]{1,0:T(8,128)(2,1)S(1)} %get-tuple-element.13), channel_id=1, source_target_pairs={{1,0},{3,2},{4,1},{6,3},{5,4},{7,6},{8,5},{10,7},{9,8},{11,10},{12... | collective-permute-start | bytes 196616 | tf_op jit(solution)/shard_map/ppermute | solution.py:250
  71.4 1.9 %collective-permute-start.9 = (bf16[64,512]{1,0:T(8,128)(2,1)S(1)}, bf16[64,512]{1,0:T(8,128)(2,1)S(1)}, u32[]{:S(2)}, u32[]{:S(2)}) collective-permute-start(bf16[64,512]{1,0:T(8,128)(2,1)S(1)} %get-tuple-element.12), channel_id=1, source_target_pairs={{0,1},{2,3},{1,4},{3,6},{4,5},{6,7},{5,8},{7,10},{8,9},{10,11},{9,... | collective-permute-start | bytes 196616 | tf_op jit(solution)/shard_map/ppermute | solution.py:250
  73.4 0.0 collective-permute-done.11
  73.4 0.0 collective-permute-done.13
  73.4 0.0 collective-permute-done.12
  73.4 0.0 copy-done
  73.4 0.5 fusion
  73.9 0.0 collective-permute-done.10
  73.9 3.1 %collective-permute-done.9 = bf16[64,512]{1,0:T(8,128)(2,1)S(1)} collective-permute-done((bf16[64,512]{1,0:T(8,128)(2,1)S(1)}, bf16[64,512]{1,0:T(8,128)(2,1)S(1)}, u32[]{:S(2)}, u32[]{:S(2)}) %collective-permute-start.9) | collective-permute-done | bytes 65568 | tf_op jit(solution)/shard_map/ppermute | solution.py:250
  77.0 0.0 copy-done.1
  77.0 0.5 convolution_add_fusion
  77.5 0.4 multiply_reduce_fusion
  77.9 0.8 %multiply_convert_fusion = bf16[192,512]{1,0:T(8,128)(2,1)} fusion(f32[192,1024]{1,0:T(8,128)S(1)} %get-tuple-element.9, s32[]{:T(128)S(6)} %select_n.124, f32[512]{0:T(512)S(1)} %convert_element_type.30, f32[192]{0:T(256)S(1)} %add_rsqrt_fusion), kind=kLoop, calls=%fused_computation.16 | loop fusion | flops 294912 | bytes 592644 | tf_op jit(solution)/shard_map/convert_element_type | solution.py:270
  (24 shorter events, 0.3 us)
Async XLA Ops:
  0.0 73.4 %copy-start = (bf16[1024,1024]{1,0:T(8,128)(2,1)S(1)}, bf16[1024,1024]{1,0:T(8,128)(2,1)}, u32[]{:S(2)}) copy-start(bf16[1024,1024]{1,0:T(8,128)(2,1)} %param.12) | copy-start | bytes 6291460
  2.0 12.8 %collective-permute-start = (bf16[2,192,512]{2,1,0:T(8,128)(2,1)S(1)}, bf16[2,192,512]{2,1,0:T(8,128)(2,1)}, u32[]{:S(2)}, u32[]{:S(2)}) collective-permute-start(bf16[2,192,512]{2,1,0:T(8,128)(2,1)S(1)} %get-tuple-element.10), channel_id=1, source_target_pairs={{0,4},{4,8},{8,12},{1,5},{5,9},{9,13},{2,6},{6,10},{10,14},{3,7},{... | collective-permute-start | bytes 1179656 | tf_op jit(solution)/shard_map/ppermute | solution.py:22
  5.5 12.9 %collective-permute-start.1 = (bf16[2,192,512]{2,1,0:T(8,128)(2,1)S(1)}, bf16[2,192,512]{2,1,0:T(8,128)(2,1)}, u32[]{:S(2)}, u32[]{:S(2)}) collective-permute-start(bf16[2,192,512]{2,1,0:T(8,128)(2,1)S(1)} %get-tuple-element.10), channel_id=1, source_target_pairs={{4,0},{8,4},{12,8},{5,1},{9,5},{13,9},{6,2},{10,6},{14,10},{7,3},{... | collective-permute-start | bytes 1179656 | tf_op jit(solution)/shard_map/ppermute | solution.py:22
  7.8 30.9 %collective-permute-start.4 = (bf16[2,192,512]{2,1,0:T(8,128)(2,1)S(1)}, bf16[2,192,512]{2,1,0:T(8,128)(2,1)}, u32[]{:S(2)}, u32[]{:S(2)}) collective-permute-start(bf16[2,192,512]{2,1,0:T(8,128)(2,1)S(1)} %get-tuple-element.10), channel_id=1, source_target_pairs={{0,1},{1,0},{2,3},{3,2},{4,5},{5,4},{6,7},{7,6},{8,9},{9,8},{10,11... | collective-permute-start | bytes 1179656 | tf_op jit(solution)/shard_map/ppermute | solution.py:26
  14.2 24.4 %copy-start.2 = (s32[10,3,192]{2,1,0:T(4,128)}, s32[10,3,192]{2,1,0:T(4,128)S(1)}, u32[]{:S(2)}) copy-start(s32[10,3,192]{2,1,0:T(4,128)S(1)} %select_bitcast_fusion.2.code_ref) | copy-start | bytes 69124
  14.8 13.1 %collective-permute-start.2 = (bf16[2,192,512]{2,1,0:T(8,128)(2,1)}, bf16[2,192,512]{2,1,0:T(8,128)(2,1)}, u32[]{:S(2)}, u32[]{:S(2)}) collective-permute-start(bf16[2,192,512]{2,1,0:T(8,128)(2,1)} %collective-permute-done), channel_id=1, source_target_pairs={{0,4},{4,8},{8,12},{1,5},{5,9},{9,13},{2,6},{6,10},{10,14},{3,7},{... | collective-permute-start | bytes 1179656 | tf_op jit(solution)/shard_map/ppermute | solution.py:22
  18.4 13.5 %collective-permute-start.3 = (bf16[2,192,512]{2,1,0:T(8,128)(2,1)}, bf16[2,192,512]{2,1,0:T(8,128)(2,1)}, u32[]{:S(2)}, u32[]{:S(2)}) collective-permute-start(bf16[2,192,512]{2,1,0:T(8,128)(2,1)} %collective-permute-done.1), channel_id=1, source_target_pairs={{4,0},{8,4},{12,8},{5,1},{9,5},{13,9},{6,2},{10,6},{14,10},{7,3},{... | collective-permute-start | bytes 1179656 | tf_op jit(solution)/shard_map/ppermute | solution.py:22
  21.7 13.0 %collective-permute-start.5 = (bf16[2,192,512]{2,1,0:T(8,128)(2,1)}, bf16[2,192,512]{2,1,0:T(8,128)(2,1)S(1)}, u32[]{:S(2)}, u32[]{:S(2)}) collective-permute-start(bf16[2,192,512]{2,1,0:T(8,128)(2,1)} %collective-permute-done), channel_id=1, source_target_pairs={{0,1},{1,0},{2,3},{3,2},{4,5},{5,4},{6,7},{7,6},{8,9},{9,8},{10,11... | collective-permute-start | bytes 1179656 | tf_op jit(solution)/shard_map/ppermute | solution.py:26
  21.7 12.9 %collective-permute-start.6 = (bf16[2,192,512]{2,1,0:T(8,128)(2,1)}, bf16[2,192,512]{2,1,0:T(8,128)(2,1)}, u32[]{:S(2)}, u32[]{:S(2)}) collective-permute-start(bf16[2,192,512]{2,1,0:T(8,128)(2,1)} %collective-permute-done.1), channel_id=1, source_target_pairs={{0,1},{1,0},{2,3},{3,2},{4,5},{5,4},{6,7},{7,6},{8,9},{9,8},{10,11... | collective-permute-start | bytes 1179656 | tf_op jit(solution)/shard_map/ppermute | solution.py:26
  27.9 8.7 %collective-permute-start.7 = (bf16[2,192,512]{2,1,0:T(8,128)(2,1)}, bf16[2,192,512]{2,1,0:T(8,128)(2,1)}, u32[]{:S(2)}, u32[]{:S(2)}) collective-permute-start(bf16[2,192,512]{2,1,0:T(8,128)(2,1)} %collective-permute-done.2), channel_id=1, source_target_pairs={{0,1},{1,0},{2,3},{3,2},{4,5},{5,4},{6,7},{7,6},{8,9},{9,8},{10,11... | collective-permute-start | bytes 1179656 | tf_op jit(solution)/shard_map/ppermute | solution.py:26
  31.8 4.8 %collective-permute-start.8 = (bf16[2,192,512]{2,1,0:T(8,128)(2,1)}, bf16[2,192,512]{2,1,0:T(8,128)(2,1)}, u32[]{:S(2)}, u32[]{:S(2)}) collective-permute-start(bf16[2,192,512]{2,1,0:T(8,128)(2,1)} %collective-permute-done.3), channel_id=1, source_target_pairs={{0,1},{1,0},{2,3},{3,2},{4,5},{5,4},{6,7},{7,6},{8,9},{9,8},{10,11... | collective-permute-start | bytes 1179656 | tf_op jit(solution)/shard_map/ppermute | solution.py:26
  38.7 29.0 %copy-start.3 = (bf16[512]{0:T(512)(128)(2,1)S(1)}, bf16[512]{0:T(512)(128)(2,1)}, u32[]{:S(2)}) copy-start(bf16[512]{0:T(512)(128)(2,1)} %param.13) | copy-start | bytes 3076
  58.1 18.9 %copy-start.1 = (bf16[192,512]{1,0:T(8,128)(2,1)S(1)}, bf16[192,512]{1,0:T(8,128)(2,1)}, u32[]{:S(2)}) copy-start(bf16[192,512]{1,0:T(8,128)(2,1)} %shard_map.73) | copy-start | bytes 589828
  59.0 14.4 %collective-permute-start.12 = (bf16[192,512]{1,0:T(8,128)(2,1)}, bf16[192,512]{1,0:T(8,128)(2,1)S(1)}, u32[]{:S(2)}, u32[]{:S(2)}) collective-permute-start(bf16[192,512]{1,0:T(8,128)(2,1)} %shard_map.73), channel_id=1, source_target_pairs={{2,0},{0,2},{3,1},{1,3},{6,4},{4,6},{7,5},{5,7},{10,8},{8,10},{11,... | collective-permute-start | bytes 589832 | tf_op jit(solution)/shard_map/ppermute | solution.py:250
  60.6 12.8 %collective-permute-start.11 = (bf16[64,512]{1,0:T(8,128)(2,1)S(1)}, bf16[64,512]{1,0:T(8,128)(2,1)S(1)}, u32[]{:S(2)}, u32[]{:S(2)}) collective-permute-start(bf16[64,512]{1,0:T(8,128)(2,1)S(1)} %get-tuple-element.12), channel_id=1, source_target_pairs={{2,1},{0,3},{3,4},{1,6},{6,5},{4,7},{7,8},{5,10},{10,9},{8,11},{11... | collective-permute-start | bytes 196616 | tf_op jit(solution)/shard_map/ppermute | solution.py:250
  62.5 10.9 %collective-permute-start.13 = (bf16[64,512]{1,0:T(8,128)(2,1)S(1)}, bf16[64,512]{1,0:T(8,128)(2,1)S(1)}, u32[]{:S(2)}, u32[]{:S(2)}) collective-permute-start(bf16[64,512]{1,0:T(8,128)(2,1)S(1)} %get-tuple-element.13), channel_id=1, source_target_pairs={{3,0},{1,2},{6,1},{4,3},{7,4},{5,6},{10,5},{8,7},{11,8},{9,10},{14... | collective-permute-start | bytes 196616 | tf_op jit(solution)/shard_map/ppermute | solution.py:250
  67.8 6.2 %collective-permute-start.10 = (bf16[64,512]{1,0:T(8,128)(2,1)S(1)}, bf16[64,512]{1,0:T(8,128)(2,1)S(1)}, u32[]{:S(2)}, u32[]{:S(2)}) collective-permute-start(bf16[64,512]{1,0:T(8,128)(2,1)S(1)} %get-tuple-element.13), channel_id=1, source_target_pairs={{1,0},{3,2},{4,1},{6,3},{5,4},{7,6},{8,5},{10,7},{9,8},{11,10},{12... | collective-permute-start | bytes 196616 | tf_op jit(solution)/shard_map/ppermute | solution.py:250
  71.4 5.6 %collective-permute-start.9 = (bf16[64,512]{1,0:T(8,128)(2,1)S(1)}, bf16[64,512]{1,0:T(8,128)(2,1)S(1)}, u32[]{:S(2)}, u32[]{:S(2)}) collective-permute-start(bf16[64,512]{1,0:T(8,128)(2,1)S(1)} %get-tuple-element.12), channel_id=1, source_target_pairs={{0,1},{2,3},{1,4},{3,6},{4,5},{6,7},{5,8},{7,10},{8,9},{10,11},{9,... | collective-permute-start | bytes 196616 | tf_op jit(solution)/shard_map/ppermute | solution.py:250
where the time goes:
time: 78.3 us; the launch traced here: 78.7 us
  starting transfers between devices  26.5 us (34%)
  Pallas kernels  19.4 us (25%)
  waiting for transfers between devices  13.3 us (17%)
  other arithmetic  11.4 us (15%)
  local copies, waits for them, and re-layouts  6.71 us (9%)
  matrix products  1.02 us (1%)
    pallas_call x1, Pallas kernels, attend_chunk(): pl.pallas_call(functools.partial(chunk_kernel, sources, has_state, final)...  19.4 us
    ppermute x5, starting transfers between devices, body(): parts.append(lax.ppermute(pieces[d], ('seq', 'head', 'sub'), pairs))  14.2 us
    ppermute x4, starting transfers between devices, shifted(): return lax.ppermute(x, axis, pairs)  11.7 us
    ppermute x4, waiting for transfers between devices, shifted(): return lax.ppermute(x, axis, pairs)  10.1 us
    another operation x2, other arithmetic, to_partner(): jnp.stack([rotated(kv, 'sub', n_sub, j) for kv, _ in mine])  4.05 us
    gather x2, local copies, waits for them, and re-layouts, attend_chunk(): live = jnp.take(mask_rows, jnp.clip(key_block, 0, block_total - 1), axis=1)  3.87 us
    ppermute x5, waiting for transfers between devices, body(): parts.append(lax.ppermute(pieces[d], ('seq', 'head', 'sub'), pairs))  3.1 us
    another operation x1, other arithmetic, body(): own = jnp.stack([key_rows, value_rows])  1.97 us
  transfers between devices with their start and end apart: 14, of which 4 were waited for; matrix products, arithmetic and copies ran while one was open for 18% of the time, Pallas kernels for 0%

commit v1 on v0

--- a/solution.py
+++ b/solution.py
@@ -97,6 +97,79 @@
         out_ref[...] = (acc_ref[...] / l_ref[...]).astype(out_ref.dtype)
 
 
+def whole_kernel(sources, flags_ref, q_ref, code_ref, qclip_ref, *refs):
+    n_in = max(src for src, _ in sources) + 1
+    kv_refs = refs[:n_in]
+    out_ref, bias_ref, m_ref, l_ref, acc_ref = refs[n_in:]
+    row_count, col_count = out_ref.shape
+    sub_rows = code_ref.shape[1]
+    piece = row_count // sub_rows
+    pair = 2 * HD
+    qclip = qclip_ref[...]
+    low = lax.broadcasted_iota(jnp.int32, (row_count, pair), 1) < HD
+    for b in range(len(sources)):
+
+        @pl.when(flags_ref[b] > 0)
+        def _():
+            code = code_ref[b]
+            allowed = jnp.concatenate(
+                [
+                    jnp.broadcast_to(
+                        qclip[i * piece : (i + 1) * piece] == code[i : i + 1, :],
+                        (piece, code.shape[1]),
+                    )
+                    for i in range(sub_rows)
+                ],
+                axis=0,
+            )
+            bias_ref[b] = jnp.where(allowed, 0.0, -1e30).astype(jnp.float32)
+
+    m_ref[...] = jnp.full(m_ref.shape, -1e30, jnp.float32)
+    l_ref[...] = jnp.zeros(l_ref.shape, jnp.float32)
+    acc_ref[...] = jnp.zeros(acc_ref.shape, jnp.float32)
+
+    def scores(b, hp, e):
+        src, idx = sources[b]
+        cols = slice(hp * pair, (hp + 1) * pair)
+        k_p = kv_refs[src][idx, 0, :, cols]
+        s = lax.dot_general(
+            q_ref[e, :, cols], k_p, (((1,), (1,)), ((), ())), preferred_element_type=jnp.float32
+        )
+        return s + bias_ref[b]
+
+    for b in range(len(sources)):
+
+        @pl.when(flags_ref[b] > 0)
+        def _():
+            for hp in range(col_count // pair):
+                for e in range(2):
+                    h = 2 * hp + e
+                    m_ref[h] = jnp.maximum(m_ref[h], jnp.max(scores(b, hp, e), axis=1, keepdims=True))
+
+    for b in range(len(sources)):
+
+        @pl.when(flags_ref[b] > 0)
+        def _():
+            src, idx = sources[b]
+            for hp in range(col_count // pair):
+                cols = slice(hp * pair, (hp + 1) * pair)
+                v_p = kv_refs[src][idx, 1, :, cols]
+                pvs = []
+                for e in range(2):
+                    h = 2 * hp + e
+                    p = jnp.exp(scores(b, hp, e) - m_ref[h])
+                    l_ref[h] = l_ref[h] + jnp.sum(p, axis=1, keepdims=True)
+                    pvs.append(
+                        jnp.dot(p.astype(jnp.bfloat16), v_p, preferred_element_type=jnp.float32)
+                    )
+                acc_ref[:, cols] = acc_ref[:, cols] + jnp.where(low, pvs[0], pvs[1])
+
+    for hp in range(col_count // pair):
+        cols = slice(hp * pair, (hp + 1) * pair)
+        den = jnp.where(low, l_ref[2 * hp], l_ref[2 * hp + 1])
+        out_ref[:, cols] = (acc_ref[:, cols] / den).astype(out_ref.dtype)
+
+
 def attend_chunk(state_now, q_split, query_clip, mask_rows, clip_ends, total, inputs, blocks):
     block_total = mask_rows.shape[1]
     sub_rows = mask_rows.shape[0]
@@ -120,9 +193,16 @@
     if final:
         out_shape = jax.ShapeDtypeStruct((row_count, col_count), jnp.bfloat16)
         out_specs = pl.BlockSpec(memory_space=pltpu.VMEM)
-        scratch = [pltpu.VMEM((row_count, col_count), jnp.float32)] * 3
+        head_count = col_count // HD
+        scratch = [
+            pltpu.VMEM((len(blocks), row_count, row_count), jnp.float32),
+            pltpu.VMEM((head_count, row_count, 1), jnp.float32),
+            pltpu.VMEM((head_count, row_count, 1), jnp.float32),
+            pltpu.VMEM((row_count, col_count), jnp.float32),
+        ]
         aliases = {}
         extra = ()
+        q_split = (q_split.astype(jnp.float32) * (1.0 / math.sqrt(HD))).astype(jnp.bfloat16)
     else:
         out_shape = (state_shape,) * 3
         out_specs = [pl.BlockSpec(memory_space=pltpu.VMEM)] * 3
@@ -130,7 +210,9 @@
         aliases = {4 + n_in: 0, 5 + n_in: 1, 6 + n_in: 2}
         extra = tuple(state_now)
     return pl.pallas_call(
-        functools.partial(chunk_kernel, sources, has_state, final),
+        functools.partial(whole_kernel, sources)
+        if final
+        else functools.partial(chunk_kernel, sources, has_state, final),
         out_shape=out_shape,
         in_specs=[pl.BlockSpec(memory_space=pltpu.SMEM)]
         + [pl.BlockSpec(memory_space=pltpu.VMEM)] * (3 + n_in + len(extra)),

time: 78.3 us -> 69.9 us (0.89)
  the two profiles are of different devices: /device:TPU:20 before, /device:TPU:12 now
where the time goes in v1:
time: 69.9 us; the launch traced here: 69 us
  starting transfers between devices  27.3 us (39%)
  waiting for transfers between devices  11.6 us (17%)
  other arithmetic  11.4 us (16%)
  Pallas kernels  10.5 us (15%)
  local copies, waits for them, and re-layouts  6.71 us (10%)
  matrix products  1.02 us (1%)
    ppermute x5, starting transfers between devices, body(): parts.append(lax.ppermute(pieces[d], ('seq', 'head', 'sub'), pairs))  13.5 us
    ppermute x4, starting transfers between devices, shifted(): return lax.ppermute(x, axis, pairs)  13.1 us
    pallas_call x1, Pallas kernels, attend_chunk(): pl.pallas_call(functools.partial(whole_kernel, sources) if final else fun...  10.5 us
    ppermute x4, waiting for transfers between devices, shifted(): return lax.ppermute(x, axis, pairs)  8.5 us
    another operation x2, other arithmetic, to_partner(): jnp.stack([rotated(kv, 'sub', n_sub, j) for kv, _ in mine])  4.05 us
    gather x2, local copies, waits for them, and re-layouts, attend_chunk(): live = jnp.take(mask_rows, jnp.clip(key_block, 0, block_total - 1), axis=1)  3.87 us
    ppermute x5, waiting for transfers between devices, body(): parts.append(lax.ppermute(pieces[d], ('seq', 'head', 'sub'), pairs))  3.1 us
    another operation x1, other arithmetic, body(): own = jnp.stack([key_rows, value_rows])  1.97 us
  transfers between devices with their start and end apart: 14, of which 3 were waited for; matrix products, arithmetic and copies ran while one was open for 21% of the time, Pallas kernels for 0%

profile of v1, /device:TPU:12, one launch (start us, length us, event | category | flops | bytes accessed | tf_op | source)
XLA Modules:
  0.0 69.0 jit_solution(2282027805958768869)
XLA Ops:
  0.0 0.0 copy-start
  0.0 2.0 %pad_maximum_fusion.2 = (bf16[2,192,512]{2,1,0:T(8,128)(2,1)S(1)}, bf16[1,2,192,512]{3,2,1,0:T(8,128)(2,1)}) fusion(bf16[1,192,512]{2,1,0:T(8,128)(2,1)} %bitcast.45, bf16[1,192,512]{2,1,0:T(8,128)(2,1)} %bitcast.46), kind=kLoop, calls=%fused_computation.15 | loop fusion | flops 196608 | bytes 1179648 | tf_op jit(solution)/shard_map/stack | solution.py:276
  2.0 3.5 %collective-permute-start = (bf16[2,192,512]{2,1,0:T(8,128)(2,1)S(1)}, bf16[2,192,512]{2,1,0:T(8,128)(2,1)}, u32[]{:S(2)}, u32[]{:S(2)}) collective-permute-start(bf16[2,192,512]{2,1,0:T(8,128)(2,1)S(1)} %get-tuple-element.10), channel_id=1, source_target_pairs={{0,4},{4,8},{8,12},{1,5},{5,9},{9,13},{2,6},{6,10},{10,14},{3,7},{... | collective-permute-start | bytes 1179656 | tf_op jit(solution)/shard_map/ppermute | solution.py:22
  5.5 3.1 %collective-permute-start.1 = (bf16[2,192,512]{2,1,0:T(8,128)(2,1)S(1)}, bf16[2,192,512]{2,1,0:T(8,128)(2,1)}, u32[]{:S(2)}, u32[]{:S(2)}) collective-permute-start(bf16[2,192,512]{2,1,0:T(8,128)(2,1)S(1)} %get-tuple-element.10), channel_id=1, source_target_pairs={{4,0},{8,4},{12,8},{5,1},{9,5},{13,9},{6,2},{10,6},{14,10},{7,3},{... | collective-permute-start | bytes 1179656 | tf_op jit(solution)/shard_map/ppermute | solution.py:22
  8.6 0.1 collective-permute-start.4
  8.8 0.1 stack.74
  8.8 0.1 le.36
  9.1 0.1 fusion.20
  9.2 0.1 reshape.622
  9.3 0.8 %reduce-window.8 = s32[6,1]{0,1:T(1,128)S(1)} reduce-window(s32[6,1]{0,1:T(1,128)} %bitcast.50, s32[]{:T(128)} %constant.94.clone.1), window={size=6x1 pad=5_0x0_0}, to_apply=%region_0.0 | reduce-window | flops 30 | bytes 52 | tf_op jit(solution)/shard_map/reduce-window.3
  10.1 0.1 convert_reduce_fusion
  10.2 0.7 %constant_dynamic-slice_fusion = s32[3,24]{1,0:T(4,128)S(1)} fusion(s32[6,24]{1,0:T(8,128)} %param.11, s32[]{:T(128)S(6)} %select_n.109), kind=kLoop, calls=%fused_computation.85 | loop fusion | bytes 580 | tf_op jit(solution)/shard_map/dynamic_slice | solution.py:247
  10.9 0.1 copy.19
  11.0 3.5 %gather_fusion = s32[1920,3]{1,0:T(8,128)S(1)} fusion(s32[3,24]{0,1:T(8,128)S(1)} %copy.19, s32[2048]{0:T(1024)S(1)} %pad_clamp_fusion), kind=kCustom, calls=%fused_computation | custom fusion | bytes 53760 | tf_op jit(solution)/shard_map/jit(_take)/gather | solution.py:179
  14.5 0.4 copy.15
  14.9 0.1 broadcast_in_dim.95
  15.0 0.0 copy-start.2
  15.0 0.0 collective-permute-done
  15.0 3.3 %collective-permute-start.2 = (bf16[2,192,512]{2,1,0:T(8,128)(2,1)}, bf16[2,192,512]{2,1,0:T(8,128)(2,1)}, u32[]{:S(2)}, u32[]{:S(2)}) collective-permute-start(bf16[2,192,512]{2,1,0:T(8,128)(2,1)} %collective-permute-done), channel_id=1, source_target_pairs={{0,4},{4,8},{8,12},{1,5},{5,9},{9,13},{2,6},{6,10},{10,14},{3,7},{... | collective-permute-start | bytes 1179656 | tf_op jit(solution)/shard_map/ppermute | solution.py:22
  18.3 0.0 collective-permute-done.1
  18.3 3.3 %collective-permute-start.3 = (bf16[2,192,512]{2,1,0:T(8,128)(2,1)}, bf16[2,192,512]{2,1,0:T(8,128)(2,1)}, u32[]{:S(2)}, u32[]{:S(2)}) collective-permute-start(bf16[2,192,512]{2,1,0:T(8,128)(2,1)} %collective-permute-done.1), channel_id=1, source_target_pairs={{4,0},{8,4},{12,8},{5,1},{9,5},{13,9},{6,2},{10,6},{14,10},{7,3},{... | collective-permute-start | bytes 1179656 | tf_op jit(solution)/shard_map/ppermute | solution.py:22
  21.6 1.0 %select_bitcast_fusion.1 = (bf16[1,192,512]{2,1,0:T(8,128)(2,1)S(1)}, bf16[1,192,512]{2,1,0:T(8,128)(2,1)S(1)}) fusion(bf16[192,512]{1,0:T(8,128)(2,1)} %param.7, pred[512]{0:T(512)(128)(4,1)S(1)} %get-tuple-element.33, pred[512]{0:T(512)(128)(4,1)S(1)} %get-tuple-element.32), kind=kLoop, calls=%fused_computation.28 | loop fusion | flops 196608 | bytes 590848 | tf_op jit(solution)/shard_map/stack | solution.py:255
  22.6 0.1 collective-permute-start.5
  22.7 0.5 collective-permute-start.6
  23.2 5.5 %collective-permute-done.2 = bf16[2,192,512]{2,1,0:T(8,128)(2,1)} collective-permute-done((bf16[2,192,512]{2,1,0:T(8,128)(2,1)}, bf16[2,192,512]{2,1,0:T(8,128)(2,1)}, u32[]{:S(2)}, u32[]{:S(2)}) %collective-permute-start.2) | collective-permute-done | bytes 393248 | tf_op jit(solution)/shard_map/ppermute | solution.py:22
  28.7 0.0 collective-permute-start.7
  28.7 3.0 %collective-permute-done.3 = bf16[2,192,512]{2,1,0:T(8,128)(2,1)} collective-permute-done((bf16[2,192,512]{2,1,0:T(8,128)(2,1)}, bf16[2,192,512]{2,1,0:T(8,128)(2,1)}, u32[]{:S(2)}, u32[]{:S(2)}) %collective-permute-start.3) | collective-permute-done | bytes 393248 | tf_op jit(solution)/shard_map/ppermute | solution.py:22
  31.7 0.0 collective-permute-start.8
  31.7 0.1 convert_reduce_fusion.2
  31.8 0.1 eq.45
  31.8 0.6 compare_reduce_fusion
  32.4 0.5 convert_element_type.33.flags_ref
  32.9 0.8 %copy.16.qclip_ref = s32[192,1]{1,0:T(8,128)} copy(s32[192,1]{0,1:T(1,128)S(1)} %bitcast.47) | data formatting | bytes 1536 | tf_op jit(solution)/shard_map/broadcast_in_dim | solution.py:227
  33.7 0.8 %multiply_convert_fusion.q_ref = bf16[2,192,512]{2,1,0:T(8,128)(2,1)} fusion(bf16[1,192,512]{2,1,0:T(8,128)(2,1)S(1)} %get-tuple-element.15, bf16[1,192,512]{2,1,0:T(8,128)(2,1)S(1)} %get-tuple-element.14), kind=kLoop, calls=%fused_computation.14 | loop fusion | flops 786432 | bytes 786432 | tf_op jit(solution)/shard_map/convert_element_type | solution.py:205
  34.5 0.0 collective-permute-done.5
  34.5 0.0 collective-permute-done.6
  34.5 2.0 %pad_maximum_fusion.refs_6_ = bf16[2,2,192,512]{3,2,1,0:T(8,128)(2,1)} fusion(bf16[1,2,192,512]{3,2,1,0:T(8,128)(2,1)} %bitcast.26, bf16[1,2,192,512]{3,2,1,0:T(8,128)(2,1)S(1)} %bitcast.44), kind=kLoop, calls=%fused_computation.11 | loop fusion | flops 393216 | bytes 1572864 | tf_op jit(solution)/shard_map/stack | solution.py:272
  36.5 0.0 collective-permute-done.7
  36.5 0.0 collective-permute-done.8
  36.5 2.1 %pad_maximum_fusion.1.refs_7_ = bf16[2,2,192,512]{3,2,1,0:T(8,128)(2,1)} fusion(bf16[1,2,192,512]{3,2,1,0:T(8,128)(2,1)} %bitcast.28, bf16[1,2,192,512]{3,2,1,0:T(8,128)(2,1)} %bitcast.27), kind=kLoop, calls=%fused_computation.12 | loop fusion | flops 393216 | bytes 1572864 | tf_op jit(solution)/shard_map/stack | solution.py:272
  38.6 0.0 copy-done.2
  38.6 0.0 collective-permute-done.4
  38.6 0.0 copy-start.3
  38.6 10.5 %shard_map.73 = bf16[192,512]{1,0:T(8,128)(2,1)} custom-call(s32[10]{0:T(128)} %convert_element_type.33.flags_ref, bf16[2,192,512]{2,1,0:T(8,128)(2,1)} %multiply_convert_fusion.q_ref, s32[10,3,192]{2,1,0:T(4,128)} %copy-done.2, s32[192,1]{1,0:T(8,128)} %copy.16.qclip_ref, bf16[1,2,192,512]{3,2,1,0:T(8,128)(2,1)} %get-tuple-element.11.refs_0_, ...), custom_call_target="tpu_custom_call" | custom-call | flops 1509949440 | bytes 5505024 | tf_op jit(solution)/shard_map/pallas_call | solution.py:212
  49.1 0.0 copy-start.1
  49.1 0.9 %fusion.34 = (bf16[64,512]{1,0:T(8,128)(2,1)S(1)}, bf16[64,512]{1,0:T(8,128)(2,1)S(1)}) fusion(bf16[192,512]{1,0:T(8,128)(2,1)} %shard_map.73), kind=kLoop, calls=%fused_computation.91 | loop fusion | bytes 262144 | tf_op jit(solution)/shard_map/slice | solution.py:317
  50.0 1.5 %collective-permute-start.12 = (bf16[192,512]{1,0:T(8,128)(2,1)}, bf16[192,512]{1,0:T(8,128)(2,1)S(1)}, u32[]{:S(2)}, u32[]{:S(2)}) collective-permute-start(bf16[192,512]{1,0:T(8,128)(2,1)} %shard_map.73), channel_id=1, source_target_pairs={{2,0},{0,2},{3,1},{1,3},{6,4},{4,6},{7,5},{5,7},{10,8},{8,10},{11,... | collective-permute-start | bytes 589832 | tf_op jit(solution)/shard_map/ppermute | solution.py:332
  51.5 2.3 %collective-permute-start.11 = (bf16[64,512]{1,0:T(8,128)(2,1)S(1)}, bf16[64,512]{1,0:T(8,128)(2,1)S(1)}, u32[]{:S(2)}, u32[]{:S(2)}) collective-permute-start(bf16[64,512]{1,0:T(8,128)(2,1)S(1)} %get-tuple-element.12), channel_id=1, source_target_pairs={{2,1},{0,3},{3,4},{1,6},{6,5},{4,7},{7,8},{5,10},{10,9},{8,11},{11... | collective-permute-start | bytes 196616 | tf_op jit(solution)/shard_map/ppermute | solution.py:332
  53.8 4.2 %collective-permute-start.13 = (bf16[64,512]{1,0:T(8,128)(2,1)S(1)}, bf16[64,512]{1,0:T(8,128)(2,1)S(1)}, u32[]{:S(2)}, u32[]{:S(2)}) collective-permute-start(bf16[64,512]{1,0:T(8,128)(2,1)S(1)} %get-tuple-element.13), channel_id=1, source_target_pairs={{3,0},{1,2},{6,1},{4,3},{7,4},{5,6},{10,5},{8,7},{11,8},{9,10},{14... | collective-permute-start | bytes 196616 | tf_op jit(solution)/shard_map/ppermute | solution.py:332
  58.0 0.0 copy-done.3
  58.1 3.6 %collective-permute-start.10 = (bf16[64,512]{1,0:T(8,128)(2,1)S(1)}, bf16[64,512]{1,0:T(8,128)(2,1)S(1)}, u32[]{:S(2)}, u32[]{:S(2)}) collective-permute-start(bf16[64,512]{1,0:T(8,128)(2,1)S(1)} %get-tuple-element.13), channel_id=1, source_target_pairs={{1,0},{3,2},{4,1},{6,3},{5,4},{7,6},{8,5},{10,7},{9,8},{11,10},{12... | collective-permute-start | bytes 196616 | tf_op jit(solution)/shard_map/ppermute | solution.py:332
  61.7 1.9 %collective-permute-start.9 = (bf16[64,512]{1,0:T(8,128)(2,1)S(1)}, bf16[64,512]{1,0:T(8,128)(2,1)S(1)}, u32[]{:S(2)}, u32[]{:S(2)}) collective-permute-start(bf16[64,512]{1,0:T(8,128)(2,1)S(1)} %get-tuple-element.12), channel_id=1, source_target_pairs={{0,1},{2,3},{1,4},{3,6},{4,5},{6,7},{5,8},{7,10},{8,9},{10,11},{9,... | collective-permute-start | bytes 196616 | tf_op jit(solution)/shard_map/ppermute | solution.py:332
  63.6 0.0 collective-permute-done.11
  63.6 0.0 collective-permute-done.13
  63.6 0.0 collective-permute-done.12
  63.7 0.0 copy-done
  63.7 0.5 fusion
  64.2 0.0 collective-permute-done.10
  64.2 3.1 %collective-permute-done.9 = bf16[64,512]{1,0:T(8,128)(2,1)S(1)} collective-permute-done((bf16[64,512]{1,0:T(8,128)(2,1)S(1)}, bf16[64,512]{1,0:T(8,128)(2,1)S(1)}, u32[]{:S(2)}, u32[]{:S(2)}) %collective-permute-start.9) | collective-permute-done | bytes 65568 | tf_op jit(solution)/shard_map/ppermute | solution.py:332
  67.3 0.0 copy-done.1
  67.3 0.5 convolution_add_fusion
  67.8 0.4 multiply_reduce_fusion
  68.2 0.8 %multiply_convert_fusion.1 = bf16[192,512]{1,0:T(8,128)(2,1)} fusion(f32[192,1024]{1,0:T(8,128)S(1)} %get-tuple-element.9, s32[]{:T(128)S(6)} %select_n.124, f32[512]{0:T(512)S(1)} %convert_element_type.38, f32[192]{0:T(256)S(1)} %add_rsqrt_fusion), kind=kLoop, calls=%fused_computation.16 | loop fusion | flops 294912 | bytes 592644 | tf_op jit(solution)/shard_map/convert_element_type | solution.py:352
  (24 shorter events, 0.3 us)
Async XLA Ops:
  0.0 63.7 %copy-start = (bf16[1024,1024]{1,0:T(8,128)(2,1)S(1)}, bf16[1024,1024]{1,0:T(8,128)(2,1)}, u32[]{:S(2)}) copy-start(bf16[1024,1024]{1,0:T(8,128)(2,1)} %param.12) | copy-start | bytes 6291460
  2.0 13.0 %collective-permute-start = (bf16[2,192,512]{2,1,0:T(8,128)(2,1)S(1)}, bf16[2,192,512]{2,1,0:T(8,128)(2,1)}, u32[]{:S(2)}, u32[]{:S(2)}) collective-permute-start(bf16[2,192,512]{2,1,0:T(8,128)(2,1)S(1)} %get-tuple-element.10), channel_id=1, source_target_pairs={{0,4},{4,8},{8,12},{1,5},{5,9},{9,13},{2,6},{6,10},{10,14},{3,7},{... | collective-permute-start | bytes 1179656 | tf_op jit(solution)/shard_map/ppermute | solution.py:22
  5.5 12.8 %collective-permute-start.1 = (bf16[2,192,512]{2,1,0:T(8,128)(2,1)S(1)}, bf16[2,192,512]{2,1,0:T(8,128)(2,1)}, u32[]{:S(2)}, u32[]{:S(2)}) collective-permute-start(bf16[2,192,512]{2,1,0:T(8,128)(2,1)S(1)} %get-tuple-element.10), channel_id=1, source_target_pairs={{4,0},{8,4},{12,8},{5,1},{9,5},{13,9},{6,2},{10,6},{14,10},{7,3},{... | collective-permute-start | bytes 1179656 | tf_op jit(solution)/shard_map/ppermute | solution.py:22
  8.6 30.0 %collective-permute-start.4 = (bf16[2,192,512]{2,1,0:T(8,128)(2,1)S(1)}, bf16[2,192,512]{2,1,0:T(8,128)(2,1)}, u32[]{:S(2)}, u32[]{:S(2)}) collective-permute-start(bf16[2,192,512]{2,1,0:T(8,128)(2,1)S(1)} %get-tuple-element.10), channel_id=1, source_target_pairs={{0,1},{1,0},{2,3},{3,2},{4,5},{5,4},{6,7},{7,6},{8,9},{9,8},{10,11... | collective-permute-start | bytes 1179656 | tf_op jit(solution)/shard_map/ppermute | solution.py:26
  15.0 23.6 %copy-start.2 = (s32[10,3,192]{2,1,0:T(4,128)}, s32[10,3,192]{2,1,0:T(4,128)S(1)}, u32[]{:S(2)}) copy-start(s32[10,3,192]{2,1,0:T(4,128)S(1)} %select_bitcast_fusion.2.code_ref) | copy-start | bytes 69124
  15.0 13.7 %collective-permute-start.2 = (bf16[2,192,512]{2,1,0:T(8,128)(2,1)}, bf16[2,192,512]{2,1,0:T(8,128)(2,1)}, u32[]{:S(2)}, u32[]{:S(2)}) collective-permute-start(bf16[2,192,512]{2,1,0:T(8,128)(2,1)} %collective-permute-done), channel_id=1, source_target_pairs={{0,4},{4,8},{8,12},{1,5},{5,9},{9,13},{2,6},{6,10},{10,14},{3,7},{... | collective-permute-start | bytes 1179656 | tf_op jit(solution)/shard_map/ppermute | solution.py:22
  18.3 13.3 %collective-permute-start.3 = (bf16[2,192,512]{2,1,0:T(8,128)(2,1)}, bf16[2,192,512]{2,1,0:T(8,128)(2,1)}, u32[]{:S(2)}, u32[]{:S(2)}) collective-permute-start(bf16[2,192,512]{2,1,0:T(8,128)(2,1)} %collective-permute-done.1), channel_id=1, source_target_pairs={{4,0},{8,4},{12,8},{5,1},{9,5},{13,9},{6,2},{10,6},{14,10},{7,3},{... | collective-permute-start | bytes 1179656 | tf_op jit(solution)/shard_map/ppermute | solution.py:22
  22.6 11.9 %collective-permute-start.5 = (bf16[2,192,512]{2,1,0:T(8,128)(2,1)}, bf16[2,192,512]{2,1,0:T(8,128)(2,1)S(1)}, u32[]{:S(2)}, u32[]{:S(2)}) collective-permute-start(bf16[2,192,512]{2,1,0:T(8,128)(2,1)} %collective-permute-done), channel_id=1, source_target_pairs={{0,1},{1,0},{2,3},{3,2},{4,5},{5,4},{6,7},{7,6},{8,9},{9,8},{10,11... | collective-permute-start | bytes 1179656 | tf_op jit(solution)/shard_map/ppermute | solution.py:26
  22.7 11.8 %collective-permute-start.6 = (bf16[2,192,512]{2,1,0:T(8,128)(2,1)}, bf16[2,192,512]{2,1,0:T(8,128)(2,1)}, u32[]{:S(2)}, u32[]{:S(2)}) collective-permute-start(bf16[2,192,512]{2,1,0:T(8,128)(2,1)} %collective-permute-done.1), channel_id=1, source_target_pairs={{0,1},{1,0},{2,3},{3,2},{4,5},{5,4},{6,7},{7,6},{8,9},{9,8},{10,11... | collective-permute-start | bytes 1179656 | tf_op jit(solution)/shard_map/ppermute | solution.py:26
  28.7 7.8 %collective-permute-start.7 = (bf16[2,192,512]{2,1,0:T(8,128)(2,1)}, bf16[2,192,512]{2,1,0:T(8,128)(2,1)}, u32[]{:S(2)}, u32[]{:S(2)}) collective-permute-start(bf16[2,192,512]{2,1,0:T(8,128)(2,1)} %collective-permute-done.2), channel_id=1, source_target_pairs={{0,1},{1,0},{2,3},{3,2},{4,5},{5,4},{6,7},{7,6},{8,9},{9,8},{10,11... | collective-permute-start | bytes 1179656 | tf_op jit(solution)/shard_map/ppermute | solution.py:26
  31.7 4.8 %collective-permute-start.8 = (bf16[2,192,512]{2,1,0:T(8,128)(2,1)}, bf16[2,192,512]{2,1,0:T(8,128)(2,1)}, u32[]{:S(2)}, u32[]{:S(2)}) collective-permute-start(bf16[2,192,512]{2,1,0:T(8,128)(2,1)} %collective-permute-done.3), channel_id=1, source_target_pairs={{0,1},{1,0},{2,3},{3,2},{4,5},{5,4},{6,7},{7,6},{8,9},{9,8},{10,11... | collective-permute-start | bytes 1179656 | tf_op jit(solution)/shard_map/ppermute | solution.py:26
  38.6 19.5 %copy-start.3 = (bf16[512]{0:T(512)(128)(2,1)S(1)}, bf16[512]{0:T(512)(128)(2,1)}, u32[]{:S(2)}) copy-start(bf16[512]{0:T(512)(128)(2,1)} %param.13) | copy-start | bytes 3076
  49.1 18.2 %copy-start.1 = (bf16[192,512]{1,0:T(8,128)(2,1)S(1)}, bf16[192,512]{1,0:T(8,128)(2,1)}, u32[]{:S(2)}) copy-start(bf16[192,512]{1,0:T(8,128)(2,1)} %shard_map.73) | copy-start | bytes 589828
  50.0 13.7 %collective-permute-start.12 = (bf16[192,512]{1,0:T(8,128)(2,1)}, bf16[192,512]{1,0:T(8,128)(2,1)S(1)}, u32[]{:S(2)}, u32[]{:S(2)}) collective-permute-start(bf16[192,512]{1,0:T(8,128)(2,1)} %shard_map.73), channel_id=1, source_target_pairs={{2,0},{0,2},{3,1},{1,3},{6,4},{4,6},{7,5},{5,7},{10,8},{8,10},{11,... | collective-permute-start | bytes 589832 | tf_op jit(solution)/shard_map/ppermute | solution.py:332
  51.5 12.1 %collective-permute-start.11 = (bf16[64,512]{1,0:T(8,128)(2,1)S(1)}, bf16[64,512]{1,0:T(8,128)(2,1)S(1)}, u32[]{:S(2)}, u32[]{:S(2)}) collective-permute-start(bf16[64,512]{1,0:T(8,128)(2,1)S(1)} %get-tuple-element.12), channel_id=1, source_target_pairs={{2,1},{0,3},{3,4},{1,6},{6,5},{4,7},{7,8},{5,10},{10,9},{8,11},{11... | collective-permute-start | bytes 196616 | tf_op jit(solution)/shard_map/ppermute | solution.py:332
  53.8 9.8 %collective-permute-start.13 = (bf16[64,512]{1,0:T(8,128)(2,1)S(1)}, bf16[64,512]{1,0:T(8,128)(2,1)S(1)}, u32[]{:S(2)}, u32[]{:S(2)}) collective-permute-start(bf16[64,512]{1,0:T(8,128)(2,1)S(1)} %get-tuple-element.13), channel_id=1, source_target_pairs={{3,0},{1,2},{6,1},{4,3},{7,4},{5,6},{10,5},{8,7},{11,8},{9,10},{14... | collective-permute-start | bytes 196616 | tf_op jit(solution)/shard_map/ppermute | solution.py:332
  58.1 6.1 %collective-permute-start.10 = (bf16[64,512]{1,0:T(8,128)(2,1)S(1)}, bf16[64,512]{1,0:T(8,128)(2,1)S(1)}, u32[]{:S(2)}, u32[]{:S(2)}) collective-permute-start(bf16[64,512]{1,0:T(8,128)(2,1)S(1)} %get-tuple-element.13), channel_id=1, source_target_pairs={{1,0},{3,2},{4,1},{6,3},{5,4},{7,6},{8,5},{10,7},{9,8},{11,10},{12... | collective-permute-start | bytes 196616 | tf_op jit(solution)/shard_map/ppermute | solution.py:332
  61.7 5.6 %collective-permute-start.9 = (bf16[64,512]{1,0:T(8,128)(2,1)S(1)}, bf16[64,512]{1,0:T(8,128)(2,1)S(1)}, u32[]{:S(2)}, u32[]{:S(2)}) collective-permute-start(bf16[64,512]{1,0:T(8,128)(2,1)S(1)} %get-tuple-element.12), channel_id=1, source_target_pairs={{0,1},{2,3},{1,4},{3,6},{4,5},{6,7},{5,8},{7,10},{8,9},{10,11},{9,... | collective-permute-start | bytes 196616 | tf_op jit(solution)/shard_map/ppermute | solution.py:332

commit v2 on v1

--- a/solution.py
+++ b/solution.py
@@ -174,10 +174,10 @@
     block_total = mask_rows.shape[1]
     sub_rows = mask_rows.shape[0]
     key_pos = jnp.stack([pos for _, _, pos in blocks])
-    key_block = key_pos // BLK
-    valid = (key_pos >= 0) & (key_pos < total)
+    key_block = key_pos[:, ::BLK] // BLK
+    valid = (key_block >= 0) & (key_block < block_total)
     live = jnp.take(mask_rows, jnp.clip(key_block, 0, block_total - 1), axis=1)
-    live = (live == 1) & valid[None]
+    live = jnp.repeat((live == 1) & valid[None], BLK, axis=2)
     key_clip = clip_index(key_pos.reshape(-1), clip_ends).reshape(key_pos.shape)
     code = jnp.where(live, key_clip[None], -1).transpose(1, 0, 2)
     query_sub = query_clip.reshape(sub_rows, -1)
@@ -260,8 +260,13 @@
         inputs = [kv[None] for kv, _ in mine]
         blocks = [(n, 0, block_pos(off, sub_i)) for n, (_, off) in enumerate(mine)]
         for got, offs, src in theirs:
-            blocks += [(len(inputs), b, block_pos(off, src)) for b, off in enumerate(offs)]
-            inputs.append(got)
+            if isinstance(got, list):
+                for piece, off in zip(got, offs):
+                    blocks.append((len(inputs), 0, block_pos(off, src)))
+                    inputs.append(piece[None])
+            else:
+                blocks += [(len(inputs), b, block_pos(off, src)) for b, off in enumerate(offs)]
+                inputs.append(got)
         return attend_chunk(
             state_now, q_split, query_clip, mask_rows, clip_ends, total, inputs, blocks
         )
@@ -273,8 +278,16 @@
             for j in range(1, n_sub)
         ]
 
+    def to_partner_apart(mine):
+        offs = [off for _, off in mine]
+        return [
+            ([rotated(kv, "sub", n_sub, j) for kv, _ in mine], offs, (sub_i - j) % n_sub)
+            for j in range(1, n_sub)
+        ]
+
     own = jnp.stack([key_rows, value_rows])
     if reach <= 4:
+        to_partner = to_partner_apart
         mine = [(own, 0)]
         theirs = to_partner(mine)
         left = own

time: 69.9 us -> 61.8 us (0.88)
  the two profiles are of different devices: /device:TPU:12 before, /device:TPU:20 now
where the time goes in v2:
time: 61.8 us; the launch traced here: 61.4 us
  starting transfers between devices  23.7 us (38%)
  waiting for transfers between devices  14.4 us (23%)
  Pallas kernels  11.8 us (19%)
  other arithmetic  6.18 us (10%)
  local copies, waits for them, and re-layouts  3.87 us (6%)
  matrix products  1.02 us (2%)
    pallas_call x1, Pallas kernels, attend_chunk(): pl.pallas_call(functools.partial(whole_kernel, sources) if final else fun...  11.8 us
    ppermute x4, waiting for transfers between devices, shifted(): return lax.ppermute(x, axis, pairs)  11.8 us
    ppermute x4, starting transfers between devices, shifted(): return lax.ppermute(x, axis, pairs)  11.7 us
    ppermute x5, starting transfers between devices, body(): parts.append(lax.ppermute(pieces[d], ('seq', 'head', 'sub'), pairs))  11.4 us
    ppermute x5, waiting for transfers between devices, body(): parts.append(lax.ppermute(pieces[d], ('seq', 'head', 'sub'), pairs))  2.61 us
    another operation x1, other arithmetic, body(): own = jnp.stack([key_rows, value_rows])  1.98 us
  transfers between devices with their start and end apart: 14, of which 4 were waited for; matrix products, arithmetic and copies ran while one was open for 11% of the time, Pallas kernels for 0%

profile of v2, /device:TPU:20, one launch (start us, length us, event | category | flops | bytes accessed | tf_op | source)
XLA Modules:
  0.0 61.4 jit_solution(15137760984339854542)
XLA Ops:
  0.0 0.0 copy-start
  0.0 2.0 %pad_maximum_fusion = (bf16[2,192,512]{2,1,0:T(8,128)(2,1)S(1)}, bf16[1,2,192,512]{3,2,1,0:T(8,128)(2,1)}) fusion(bf16[1,192,512]{2,1,0:T(8,128)(2,1)} %bitcast.28, bf16[1,192,512]{2,1,0:T(8,128)(2,1)} %bitcast.29), kind=kLoop, calls=%fused_computation.13 | loop fusion | flops 196608 | bytes 1179648 | tf_op jit(solution)/shard_map/stack | solution.py:288
  2.0 3.5 %collective-permute-start = (bf16[2,192,512]{2,1,0:T(8,128)(2,1)S(1)}, bf16[2,192,512]{2,1,0:T(8,128)(2,1)S(1)}, u32[]{:S(2)}, u32[]{:S(2)}) collective-permute-start(bf16[2,192,512]{2,1,0:T(8,128)(2,1)S(1)} %get-tuple-element.12), channel_id=1, source_target_pairs={{0,4},{4,8},{8,12},{1,5},{5,9},{9,13},{2,6},{6,10},{10,14},{3,7},{... | collective-permute-start | bytes 1179656 | tf_op jit(solution)/shard_map/ppermute | solution.py:22
  5.5 2.4 %collective-permute-start.1 = (bf16[2,192,512]{2,1,0:T(8,128)(2,1)S(1)}, bf16[2,192,512]{2,1,0:T(8,128)(2,1)}, u32[]{:S(2)}, u32[]{:S(2)}) collective-permute-start(bf16[2,192,512]{2,1,0:T(8,128)(2,1)S(1)} %get-tuple-element.12), channel_id=1, source_target_pairs={{4,0},{8,4},{12,8},{5,1},{9,5},{13,9},{6,2},{10,6},{14,10},{7,3},{... | collective-permute-start | bytes 1179656 | tf_op jit(solution)/shard_map/ppermute | solution.py:22
  7.8 0.1 collective-permute-start.4
  8.1 0.1 stack.14
  8.1 0.1 slice.18
  8.2 0.1 reshape.158
  8.3 0.7 %constant_dynamic-slice_fusion = s32[3,24]{1,0:T(4,128)S(1)} fusion(s32[6,24]{1,0:T(8,128)} %param.11, s32[]{:T(128)S(6)} %select_n.81), kind=kLoop, calls=%fused_computation.67 | loop fusion | bytes 580 | tf_op jit(solution)/shard_map/dynamic_slice | solution.py:247
  9.0 0.1 le.32
  9.1 0.1 copy.19
  9.2 0.6 gather_fusion
  9.7 0.1 copy.16
  9.8 0.1 reshape.161
  9.9 0.8 %reduce-window.8 = s32[6,1]{0,1:T(1,128)S(1)} reduce-window(s32[6,1]{0,1:T(1,128)} %bitcast.34, s32[]{:T(128)} %constant.94.clone.1), window={size=6x1 pad=5_0x0_0}, to_apply=%region_0.0 | reduce-window | flops 30 | bytes 52 | tf_op jit(solution)/shard_map/reduce-window.3
  10.7 0.1 convert_reduce_fusion
  10.9 3.9 %collective-permute-done = bf16[2,192,512]{2,1,0:T(8,128)(2,1)S(1)} collective-permute-done((bf16[2,192,512]{2,1,0:T(8,128)(2,1)S(1)}, bf16[2,192,512]{2,1,0:T(8,128)(2,1)S(1)}, u32[]{:S(2)}, u32[]{:S(2)}) %collective-permute-start) | collective-permute-done | bytes 393248 | tf_op jit(solution)/shard_map/ppermute | solution.py:22
  14.7 3.5 %collective-permute-start.2 = (bf16[2,192,512]{2,1,0:T(8,128)(2,1)S(1)}, bf16[2,192,512]{2,1,0:T(8,128)(2,1)}, u32[]{:S(2)}, u32[]{:S(2)}) collective-permute-start(bf16[2,192,512]{2,1,0:T(8,128)(2,1)S(1)} %collective-permute-done), channel_id=1, source_target_pairs={{0,4},{4,8},{8,12},{1,5},{5,9},{9,13},{2,6},{6,10},{10,14},{3,7},{... | collective-permute-start | bytes 1179656 | tf_op jit(solution)/shard_map/ppermute | solution.py:22
  18.2 0.0 collective-permute-done.1
  18.2 2.4 %collective-permute-start.3 = (bf16[2,192,512]{2,1,0:T(8,128)(2,1)}, bf16[2,192,512]{2,1,0:T(8,128)(2,1)}, u32[]{:S(2)}, u32[]{:S(2)}) collective-permute-start(bf16[2,192,512]{2,1,0:T(8,128)(2,1)} %collective-permute-done.1), channel_id=1, source_target_pairs={{4,0},{8,4},{12,8},{5,1},{9,5},{13,9},{6,2},{10,6},{14,10},{7,3},{... | collective-permute-start | bytes 1179656 | tf_op jit(solution)/shard_map/ppermute | solution.py:22
  20.6 0.1 convert_reduce_fusion.2
  20.7 0.1 broadcast_in_dim.116
  20.8 0.1 reshape.155
  20.9 0.1 broadcast_in_dim.117
  21.0 0.1 eq.43
  21.1 0.0 copy-start.3
  21.1 0.6 compare_reduce_fusion
  21.6 0.1 collective-permute-start.5
  21.7 0.5 collective-permute-start.6
  22.2 4.6 %collective-permute-done.2 = bf16[2,192,512]{2,1,0:T(8,128)(2,1)} collective-permute-done((bf16[2,192,512]{2,1,0:T(8,128)(2,1)S(1)}, bf16[2,192,512]{2,1,0:T(8,128)(2,1)}, u32[]{:S(2)}, u32[]{:S(2)}) %collective-permute-start.2) | collective-permute-done | bytes 393248 | tf_op jit(solution)/shard_map/ppermute | solution.py:22
  26.8 0.0 collective-permute-start.7
  26.8 3.3 %collective-permute-done.3 = bf16[2,192,512]{2,1,0:T(8,128)(2,1)} collective-permute-done((bf16[2,192,512]{2,1,0:T(8,128)(2,1)}, bf16[2,192,512]{2,1,0:T(8,128)(2,1)}, u32[]{:S(2)}, u32[]{:S(2)}) %collective-permute-start.3) | collective-permute-done | bytes 393248 | tf_op jit(solution)/shard_map/ppermute | solution.py:22
  30.1 0.0 collective-permute-start.8
  30.1 0.5 convert_element_type.33.flags_ref
  30.6 0.8 %copy.18.qclip_ref = s32[192,1]{1,0:T(8,128)} copy(s32[192,1]{0,1:T(1,128)S(1)} %bitcast.30) | data formatting | bytes 1536 | tf_op jit(solution)/shard_map/broadcast_in_dim | solution.py:227
  31.4 0.0 copy-done.2
  31.4 0.8 %multiply_convert_fusion.q_ref = bf16[2,192,512]{2,1,0:T(8,128)(2,1)} fusion(bf16[1,192,512]{2,1,0:T(8,128)(2,1)S(1)} %get-tuple-element.17, bf16[1,192,512]{2,1,0:T(8,128)(2,1)S(1)} %get-tuple-element.16), kind=kLoop, calls=%fused_computation.12 | loop fusion | flops 786432 | bytes 786432 | tf_op jit(solution)/shard_map/convert_element_type | solution.py:205
  32.3 0.0 collective-permute-done.4
  32.3 0.0 collective-permute-done.5
  32.3 0.0 collective-permute-done.6
  32.3 0.0 collective-permute-done.7
  32.3 0.0 collective-permute-done.8
  32.3 0.0 copy-done.5
  32.3 0.0 copy-done.3
  32.3 0.0 copy-start.4
  32.3 11.8 %shard_map.73 = bf16[192,512]{1,0:T(8,128)(2,1)} custom-call(s32[10]{0:T(128)} %convert_element_type.33.flags_ref, bf16[2,192,512]{2,1,0:T(8,128)(2,1)} %multiply_convert_fusion.q_ref, s32[10,3,192]{2,1,0:T(4,128)} %copy-done.3, s32[192,1]{1,0:T(8,128)} %copy.18.qclip_ref, bf16[1,2,192,512]{3,2,1,0:T(8,128)(2,1)} %get-tuple-element.13.refs_0_, ...), custom_call_target="tpu_custom_call" | custom-call | flops 1509949440 | bytes 5505024 | tf_op jit(solution)/shard_map/pallas_call | solution.py:212
  44.1 0.9 %fusion.33 = (bf16[64,512]{1,0:T(8,128)(2,1)S(1)}, bf16[64,512]{1,0:T(8,128)(2,1)S(1)}) fusion(bf16[192,512]{1,0:T(8,128)(2,1)} %shard_map.73), kind=kLoop, calls=%fused_computation.73 | loop fusion | bytes 262144 | tf_op jit(solution)/shard_map/slice | solution.py:330
  45.1 1.6 %collective-permute-start.12 = (bf16[192,512]{1,0:T(8,128)(2,1)}, bf16[192,512]{1,0:T(8,128)(2,1)S(1)}, u32[]{:S(2)}, u32[]{:S(2)}) collective-permute-start(bf16[192,512]{1,0:T(8,128)(2,1)} %shard_map.73), channel_id=1, source_target_pairs={{2,0},{0,2},{3,1},{1,3},{6,4},{4,6},{7,5},{5,7},{10,8},{8,10},{11,... | collective-permute-start | bytes 589832 | tf_op jit(solution)/shard_map/ppermute | solution.py:345
  46.6 1.9 %collective-permute-start.13 = (bf16[64,512]{1,0:T(8,128)(2,1)S(1)}, bf16[64,512]{1,0:T(8,128)(2,1)S(1)}, u32[]{:S(2)}, u32[]{:S(2)}) collective-permute-start(bf16[64,512]{1,0:T(8,128)(2,1)S(1)} %get-tuple-element.15), channel_id=1, source_target_pairs={{3,0},{1,2},{6,1},{4,3},{7,4},{5,6},{10,5},{8,7},{11,8},{9,10},{14... | collective-permute-start | bytes 196616 | tf_op jit(solution)/shard_map/ppermute | solution.py:345
  48.5 3.6 %collective-permute-start.11 = (bf16[64,512]{1,0:T(8,128)(2,1)S(1)}, bf16[64,512]{1,0:T(8,128)(2,1)S(1)}, u32[]{:S(2)}, u32[]{:S(2)}) collective-permute-start(bf16[64,512]{1,0:T(8,128)(2,1)S(1)} %get-tuple-element.14), channel_id=1, source_target_pairs={{2,1},{0,3},{3,4},{1,6},{6,5},{4,7},{7,8},{5,10},{10,9},{8,11},{11... | collective-permute-start | bytes 196616 | tf_op jit(solution)/shard_map/ppermute | solution.py:345
  52.2 0.0 copy-done.4
  52.3 1.9 %collective-permute-start.10 = (bf16[64,512]{1,0:T(8,128)(2,1)S(1)}, bf16[64,512]{1,0:T(8,128)(2,1)S(1)}, u32[]{:S(2)}, u32[]{:S(2)}) collective-permute-start(bf16[64,512]{1,0:T(8,128)(2,1)S(1)} %get-tuple-element.15), channel_id=1, source_target_pairs={{1,0},{3,2},{4,1},{6,3},{5,4},{7,6},{8,5},{10,7},{9,8},{11,10},{12... | collective-permute-start | bytes 196616 | tf_op jit(solution)/shard_map/ppermute | solution.py:345
  54.2 2.4 %collective-permute-start.9 = (bf16[64,512]{1,0:T(8,128)(2,1)S(1)}, bf16[64,512]{1,0:T(8,128)(2,1)S(1)}, u32[]{:S(2)}, u32[]{:S(2)}) collective-permute-start(bf16[64,512]{1,0:T(8,128)(2,1)S(1)} %get-tuple-element.14), channel_id=1, source_target_pairs={{0,1},{2,3},{1,4},{3,6},{4,5},{6,7},{5,8},{7,10},{8,9},{10,11},{9,... | collective-permute-start | bytes 196616 | tf_op jit(solution)/shard_map/ppermute | solution.py:345
  56.6 0.0 collective-permute-done.13
  56.6 0.0 collective-permute-done.11
  56.6 0.0 collective-permute-done.12
  56.6 0.0 copy-done
  56.6 0.5 fusion
  57.2 0.0 collective-permute-done.10
  57.2 2.6 %collective-permute-done.9 = bf16[64,512]{1,0:T(8,128)(2,1)S(1)} collective-permute-done((bf16[64,512]{1,0:T(8,128)(2,1)S(1)}, bf16[64,512]{1,0:T(8,128)(2,1)S(1)}, u32[]{:S(2)}, u32[]{:S(2)}) %collective-permute-start.9) | collective-permute-done | bytes 65568 | tf_op jit(solution)/shard_map/ppermute | solution.py:345
  59.8 0.0 copy-done.1
  59.8 0.5 convolution_add_fusion
  60.3 0.4 multiply_reduce_fusion
  60.7 0.8 %multiply_convert_fusion.1 = bf16[192,512]{1,0:T(8,128)(2,1)} fusion(f32[192,1024]{1,0:T(8,128)S(1)} %get-tuple-element.9, s32[]{:T(128)S(6)} %select_n.93, f32[512]{0:T(512)S(1)} %convert_element_type.38, f32[192]{0:T(256)S(1)} %add_rsqrt_fusion), kind=kLoop, calls=%fused_computation.14 | loop fusion | flops 294912 | bytes 592644 | tf_op jit(solution)/shard_map/convert_element_type | solution.py:365
  (20 shorter events, 0.2 us)
Async XLA Ops:
  0.0 56.6 %copy-start = (bf16[1024,1024]{1,0:T(8,128)(2,1)S(1)}, bf16[1024,1024]{1,0:T(8,128)(2,1)}, u32[]{:S(2)}) copy-start(bf16[1024,1024]{1,0:T(8,128)(2,1)} %param.12) | copy-start | bytes 6291460
  0.0 31.4 %copy-start.2 = (bf16[192,512]{1,0:T(8,128)(2,1)S(1)}, bf16[192,512]{1,0:T(8,128)(2,1)}, u32[]{:S(2)}) copy-start(bf16[192,512]{1,0:T(8,128)(2,1)} %param.7) | copy-start | bytes 589828
  2.0 12.7 %collective-permute-start = (bf16[2,192,512]{2,1,0:T(8,128)(2,1)S(1)}, bf16[2,192,512]{2,1,0:T(8,128)(2,1)S(1)}, u32[]{:S(2)}, u32[]{:S(2)}) collective-permute-start(bf16[2,192,512]{2,1,0:T(8,128)(2,1)S(1)} %get-tuple-element.12), channel_id=1, source_target_pairs={{0,4},{4,8},{8,12},{1,5},{5,9},{9,13},{2,6},{6,10},{10,14},{3,7},{... | collective-permute-start | bytes 1179656 | tf_op jit(solution)/shard_map/ppermute | solution.py:22
  5.5 12.7 %collective-permute-start.1 = (bf16[2,192,512]{2,1,0:T(8,128)(2,1)S(1)}, bf16[2,192,512]{2,1,0:T(8,128)(2,1)}, u32[]{:S(2)}, u32[]{:S(2)}) collective-permute-start(bf16[2,192,512]{2,1,0:T(8,128)(2,1)S(1)} %get-tuple-element.12), channel_id=1, source_target_pairs={{4,0},{8,4},{12,8},{5,1},{9,5},{13,9},{6,2},{10,6},{14,10},{7,3},{... | collective-permute-start | bytes 1179656 | tf_op jit(solution)/shard_map/ppermute | solution.py:22
  7.8 24.4 %collective-permute-start.4 = (bf16[2,192,512]{2,1,0:T(8,128)(2,1)S(1)}, bf16[2,192,512]{2,1,0:T(8,128)(2,1)}, u32[]{:S(2)}, u32[]{:S(2)}) collective-permute-start(bf16[2,192,512]{2,1,0:T(8,128)(2,1)S(1)} %get-tuple-element.12), channel_id=1, source_target_pairs={{0,1},{1,0},{2,3},{3,2},{4,5},{5,4},{6,7},{7,6},{8,9},{9,8},{10,11... | collective-permute-start | bytes 1179656 | tf_op jit(solution)/shard_map/ppermute | solution.py:26
  14.7 17.6 %copy-start.5 = (bf16[2,192,512]{2,1,0:T(8,128)(2,1)}, bf16[2,192,512]{2,1,0:T(8,128)(2,1)S(1)}, u32[]{:S(2)}) copy-start(bf16[2,192,512]{2,1,0:T(8,128)(2,1)S(1)} %collective-permute-done) | copy-start | bytes 1179652
  14.7 12.1 %collective-permute-start.2 = (bf16[2,192,512]{2,1,0:T(8,128)(2,1)S(1)}, bf16[2,192,512]{2,1,0:T(8,128)(2,1)}, u32[]{:S(2)}, u32[]{:S(2)}) collective-permute-start(bf16[2,192,512]{2,1,0:T(8,128)(2,1)S(1)} %collective-permute-done), channel_id=1, source_target_pairs={{0,4},{4,8},{8,12},{1,5},{5,9},{9,13},{2,6},{6,10},{10,14},{3,7},{... | collective-permute-start | bytes 1179656 | tf_op jit(solution)/shard_map/ppermute | solution.py:22
  18.2 11.9 %collective-permute-start.3 = (bf16[2,192,512]{2,1,0:T(8,128)(2,1)}, bf16[2,192,512]{2,1,0:T(8,128)(2,1)}, u32[]{:S(2)}, u32[]{:S(2)}) collective-permute-start(bf16[2,192,512]{2,1,0:T(8,128)(2,1)} %collective-permute-done.1), channel_id=1, source_target_pairs={{4,0},{8,4},{12,8},{5,1},{9,5},{13,9},{6,2},{10,6},{14,10},{7,3},{... | collective-permute-start | bytes 1179656 | tf_op jit(solution)/shard_map/ppermute | solution.py:22
  21.1 11.2 %copy-start.3 = (s32[10,3,192]{2,1,0:T(4,128)}, s32[10,3,192]{2,1,0:T(4,128)S(1)}, u32[]{:S(2)}) copy-start(s32[10,3,192]{2,1,0:T(4,128)S(1)} %select_bitcast_fusion.2.code_ref) | copy-start | bytes 69124
  21.6 10.6 %collective-permute-start.5 = (bf16[2,192,512]{2,1,0:T(8,128)(2,1)S(1)}, bf16[2,192,512]{2,1,0:T(8,128)(2,1)}, u32[]{:S(2)}, u32[]{:S(2)}) collective-permute-start(bf16[2,192,512]{2,1,0:T(8,128)(2,1)S(1)} %collective-permute-done), channel_id=1, source_target_pairs={{0,1},{1,0},{2,3},{3,2},{4,5},{5,4},{6,7},{7,6},{8,9},{9,8},{10,11... | collective-permute-start | bytes 1179656 | tf_op jit(solution)/shard_map/ppermute | solution.py:26
  21.7 10.5 %collective-permute-start.6 = (bf16[2,192,512]{2,1,0:T(8,128)(2,1)}, bf16[2,192,512]{2,1,0:T(8,128)(2,1)}, u32[]{:S(2)}, u32[]{:S(2)}) collective-permute-start(bf16[2,192,512]{2,1,0:T(8,128)(2,1)} %collective-permute-done.1), channel_id=1, source_target_pairs={{0,1},{1,0},{2,3},{3,2},{4,5},{5,4},{6,7},{7,6},{8,9},{9,8},{10,11... | collective-permute-start | bytes 1179656 | tf_op jit(solution)/shard_map/ppermute | solution.py:26
  26.8 5.5 %collective-permute-start.7 = (bf16[2,192,512]{2,1,0:T(8,128)(2,1)}, bf16[2,192,512]{2,1,0:T(8,128)(2,1)}, u32[]{:S(2)}, u32[]{:S(2)}) collective-permute-start(bf16[2,192,512]{2,1,0:T(8,128)(2,1)} %collective-permute-done.2), channel_id=1, source_target_pairs={{0,1},{1,0},{2,3},{3,2},{4,5},{5,4},{6,7},{7,6},{8,9},{9,8},{10,11... | collective-permute-start | bytes 1179656 | tf_op jit(solution)/shard_map/ppermute | solution.py:26
  30.1 2.2 %collective-permute-start.8 = (bf16[2,192,512]{2,1,0:T(8,128)(2,1)}, bf16[2,192,512]{2,1,0:T(8,128)(2,1)}, u32[]{:S(2)}, u32[]{:S(2)}) collective-permute-start(bf16[2,192,512]{2,1,0:T(8,128)(2,1)} %collective-permute-done.3), channel_id=1, source_target_pairs={{0,1},{1,0},{2,3},{3,2},{4,5},{5,4},{6,7},{7,6},{8,9},{9,8},{10,11... | collective-permute-start | bytes 1179656 | tf_op jit(solution)/shard_map/ppermute | solution.py:26
  32.3 19.9 %copy-start.4 = (bf16[512]{0:T(512)(128)(2,1)S(1)}, bf16[512]{0:T(512)(128)(2,1)}, u32[]{:S(2)}) copy-start(bf16[512]{0:T(512)(128)(2,1)} %param.13) | copy-start | bytes 3076
  44.1 15.6 %copy-start.1 = (bf16[192,512]{1,0:T(8,128)(2,1)S(1)}, bf16[192,512]{1,0:T(8,128)(2,1)}, u32[]{:S(2)}) copy-start(bf16[192,512]{1,0:T(8,128)(2,1)} %shard_map.73) | copy-start | bytes 589828
  45.1 11.6 %collective-permute-start.12 = (bf16[192,512]{1,0:T(8,128)(2,1)}, bf16[192,512]{1,0:T(8,128)(2,1)S(1)}, u32[]{:S(2)}, u32[]{:S(2)}) collective-permute-start(bf16[192,512]{1,0:T(8,128)(2,1)} %shard_map.73), channel_id=1, source_target_pairs={{2,0},{0,2},{3,1},{1,3},{6,4},{4,6},{7,5},{5,7},{10,8},{8,10},{11,... | collective-permute-start | bytes 589832 | tf_op jit(solution)/shard_map/ppermute | solution.py:345
  46.6 10.0 %collective-permute-start.13 = (bf16[64,512]{1,0:T(8,128)(2,1)S(1)}, bf16[64,512]{1,0:T(8,128)(2,1)S(1)}, u32[]{:S(2)}, u32[]{:S(2)}) collective-permute-start(bf16[64,512]{1,0:T(8,128)(2,1)S(1)} %get-tuple-element.15), channel_id=1, source_target_pairs={{3,0},{1,2},{6,1},{4,3},{7,4},{5,6},{10,5},{8,7},{11,8},{9,10},{14... | collective-permute-start | bytes 196616 | tf_op jit(solution)/shard_map/ppermute | solution.py:345
  48.5 8.1 %collective-permute-start.11 = (bf16[64,512]{1,0:T(8,128)(2,1)S(1)}, bf16[64,512]{1,0:T(8,128)(2,1)S(1)}, u32[]{:S(2)}, u32[]{:S(2)}) collective-permute-start(bf16[64,512]{1,0:T(8,128)(2,1)S(1)} %get-tuple-element.14), channel_id=1, source_target_pairs={{2,1},{0,3},{3,4},{1,6},{6,5},{4,7},{7,8},{5,10},{10,9},{8,11},{11... | collective-permute-start | bytes 196616 | tf_op jit(solution)/shard_map/ppermute | solution.py:345
  52.3 4.9 %collective-permute-start.10 = (bf16[64,512]{1,0:T(8,128)(2,1)S(1)}, bf16[64,512]{1,0:T(8,128)(2,1)S(1)}, u32[]{:S(2)}, u32[]{:S(2)}) collective-permute-start(bf16[64,512]{1,0:T(8,128)(2,1)S(1)} %get-tuple-element.15), channel_id=1, source_target_pairs={{1,0},{3,2},{4,1},{6,3},{5,4},{7,6},{8,5},{10,7},{9,8},{11,10},{12... | collective-permute-start | bytes 196616 | tf_op jit(solution)/shard_map/ppermute | solution.py:345
  54.2 5.6 %collective-permute-start.9 = (bf16[64,512]{1,0:T(8,128)(2,1)S(1)}, bf16[64,512]{1,0:T(8,128)(2,1)S(1)}, u32[]{:S(2)}, u32[]{:S(2)}) collective-permute-start(bf16[64,512]{1,0:T(8,128)(2,1)S(1)} %get-tuple-element.14), channel_id=1, source_target_pairs={{0,1},{2,3},{1,4},{3,6},{4,5},{6,7},{5,8},{7,10},{8,9},{10,11},{9,... | collective-permute-start | bytes 196616 | tf_op jit(solution)/shard_map/ppermute | solution.py:345

commit v3 on v2

--- a/solution.py
+++ b/solution.py
@@ -100,7 +100,7 @@
 def whole_kernel(sources, flags_ref, q_ref, code_ref, qclip_ref, *refs):
     n_in = max(src for src, _ in sources) + 1
     kv_refs = refs[:n_in]
-    out_ref, bias_ref, m_ref, l_ref, acc_ref = refs[n_in:]
+    out_ref, bias_ref, m_ref, l_ref, acc_ref, s_ref = refs[n_in:]
     row_count, col_count = out_ref.shape
     sub_rows = code_ref.shape[1]
     piece = row_count // sub_rows
@@ -144,7 +144,9 @@
             for hp in range(col_count // pair):
                 for e in range(2):
                     h = 2 * hp + e
-                    m_ref[h] = jnp.maximum(m_ref[h], jnp.max(scores(b, hp, e), axis=1, keepdims=True))
+                    s_now = scores(b, hp, e)
+                    s_ref[b, h] = s_now
+                    m_ref[h] = jnp.maximum(m_ref[h], jnp.max(s_now, axis=1, keepdims=True))
 
     for b in range(len(sources)):
 
@@ -157,7 +159,7 @@
                 pvs = []
                 for e in range(2):
                     h = 2 * hp + e
-                    p = jnp.exp(scores(b, hp, e) - m_ref[h])
+                    p = jnp.exp(s_ref[b, h] - m_ref[h])
                     l_ref[h] = l_ref[h] + jnp.sum(p, axis=1, keepdims=True)
                     pvs.append(
                         jnp.dot(p.astype(jnp.bfloat16), v_p, preferred_element_type=jnp.float32)
@@ -199,6 +201,7 @@
             pltpu.VMEM((head_count, row_count, 1), jnp.float32),
             pltpu.VMEM((head_count, row_count, 1), jnp.float32),
             pltpu.VMEM((row_count, col_count), jnp.float32),
+            pltpu.VMEM((len(blocks), head_count, row_count, row_count), jnp.float32),
         ]
         aliases = {}
         extra = ()

time: 61.8 us -> 65.8 us (1.065)
  the two profiles are of different devices: /device:TPU:20 before, /device:TPU:1 now
where the time goes in v3:
time: 65.8 us; the launch traced here: 64.7 us
  starting transfers between devices  36.4 us (55%)
  Pallas kernels  9.1 us (14%)
  waiting for transfers between devices  7.84 us (12%)
  other arithmetic  6.17 us (9%)
  local copies, waits for them, and re-layouts  3.87 us (6%)
  matrix products  1.02 us (2%)
    ppermute x5, starting transfers between devices, body(): parts.append(lax.ppermute(pieces[d], ('seq', 'head', 'sub'), pairs))  16.9 us
    ppermute x4, starting transfers between devices, shifted(): return lax.ppermute(x, axis, pairs)  11.6 us
    pallas_call x1, Pallas kernels, attend_chunk(): pl.pallas_call(functools.partial(whole_kernel, sources) if final else fun...  9.1 us
    ppermute x5, starting transfers between devices, rotated(): lax.ppermute(x, axis, [(i, (i + step) % count) for i in range(count)])  7.89 us
    ppermute x4, waiting for transfers between devices, shifted(): return lax.ppermute(x, axis, pairs)  7.07 us
    another operation x1, other arithmetic, body(): own = jnp.stack([key_rows, value_rows])  1.98 us
  transfers between devices with their start and end apart: 14, of which 4 were waited for; matrix products, arithmetic and copies ran while one was open for 10% of the time, Pallas kernels for 0%

profile of v3, /device:TPU:1, one launch (start us, length us, event | category | flops | bytes accessed | tf_op | source)
XLA Modules:
  0.0 64.7 jit_solution(11968104803385886493)
XLA Ops:
  0.0 0.0 copy-start
  0.0 2.0 %pad_maximum_fusion = (bf16[2,192,512]{2,1,0:T(8,128)(2,1)S(1)}, bf16[1,2,192,512]{3,2,1,0:T(8,128)(2,1)}) fusion(bf16[1,192,512]{2,1,0:T(8,128)(2,1)} %bitcast.28, bf16[1,192,512]{2,1,0:T(8,128)(2,1)} %bitcast.29), kind=kLoop, calls=%fused_computation.13 | loop fusion | flops 196608 | bytes 1179648 | tf_op jit(solution)/shard_map/stack | solution.py:291
  2.0 4.0 %collective-permute-start = (bf16[2,192,512]{2,1,0:T(8,128)(2,1)S(1)}, bf16[2,192,512]{2,1,0:T(8,128)(2,1)S(1)}, u32[]{:S(2)}, u32[]{:S(2)}) collective-permute-start(bf16[2,192,512]{2,1,0:T(8,128)(2,1)S(1)} %get-tuple-element.12), channel_id=1, source_target_pairs={{0,4},{4,8},{8,12},{1,5},{5,9},{9,13},{2,6},{6,10},{10,14},{3,7},{... | collective-permute-start | bytes 1179656 | tf_op jit(solution)/shard_map/ppermute | solution.py:22
  6.0 1.3 %collective-permute-start.1 = (bf16[2,192,512]{2,1,0:T(8,128)(2,1)S(1)}, bf16[2,192,512]{2,1,0:T(8,128)(2,1)}, u32[]{:S(2)}, u32[]{:S(2)}) collective-permute-start(bf16[2,192,512]{2,1,0:T(8,128)(2,1)S(1)} %get-tuple-element.12), channel_id=1, source_target_pairs={{4,0},{8,4},{12,8},{5,1},{9,5},{13,9},{6,2},{10,6},{14,10},{7,3},{... | collective-permute-start | bytes 1179656 | tf_op jit(solution)/shard_map/ppermute | solution.py:22
  7.3 1.0 %collective-permute-start.4 = (bf16[2,192,512]{2,1,0:T(8,128)(2,1)S(1)}, bf16[2,192,512]{2,1,0:T(8,128)(2,1)}, u32[]{:S(2)}, u32[]{:S(2)}) collective-permute-start(bf16[2,192,512]{2,1,0:T(8,128)(2,1)S(1)} %get-tuple-element.12), channel_id=1, source_target_pairs={{0,1},{1,0},{2,3},{3,2},{4,5},{5,4},{6,7},{7,6},{8,9},{9,8},{10,11... | collective-permute-start | bytes 1179656 | tf_op jit(solution)/shard_map/ppermute | solution.py:26
  8.4 0.1 stack.14
  8.5 0.1 slice.18
  8.6 0.1 reshape.158
  8.7 0.7 %constant_dynamic-slice_fusion = s32[3,24]{1,0:T(4,128)S(1)} fusion(s32[6,24]{1,0:T(8,128)} %param.11, s32[]{:T(128)S(6)} %select_n.81), kind=kLoop, calls=%fused_computation.67 | loop fusion | bytes 580 | tf_op jit(solution)/shard_map/dynamic_slice | solution.py:250
  9.4 0.1 le.32
  9.4 0.1 copy.19
  9.5 0.6 gather_fusion
  10.1 0.1 copy.16
  10.2 0.1 reshape.161
  10.3 0.8 %reduce-window.8 = s32[6,1]{0,1:T(1,128)S(1)} reduce-window(s32[6,1]{0,1:T(1,128)} %bitcast.34, s32[]{:T(128)} %constant.94.clone.1), window={size=6x1 pad=5_0x0_0}, to_apply=%region_0.0 | reduce-window | flops 30 | bytes 52 | tf_op jit(solution)/shard_map/reduce-window.3
  11.1 0.1 convert_reduce_fusion
  11.2 2.6 %collective-permute-done = bf16[2,192,512]{2,1,0:T(8,128)(2,1)S(1)} collective-permute-done((bf16[2,192,512]{2,1,0:T(8,128)(2,1)S(1)}, bf16[2,192,512]{2,1,0:T(8,128)(2,1)S(1)}, u32[]{:S(2)}, u32[]{:S(2)}) %collective-permute-start) | collective-permute-done | bytes 393248 | tf_op jit(solution)/shard_map/ppermute | solution.py:22
  13.8 4.9 %collective-permute-start.2 = (bf16[2,192,512]{2,1,0:T(8,128)(2,1)S(1)}, bf16[2,192,512]{2,1,0:T(8,128)(2,1)}, u32[]{:S(2)}, u32[]{:S(2)}) collective-permute-start(bf16[2,192,512]{2,1,0:T(8,128)(2,1)S(1)} %collective-permute-done), channel_id=1, source_target_pairs={{0,4},{4,8},{8,12},{1,5},{5,9},{9,13},{2,6},{6,10},{10,14},{3,7},{... | collective-permute-start | bytes 1179656 | tf_op jit(solution)/shard_map/ppermute | solution.py:22
  18.7 0.0 collective-permute-done.1
  18.7 1.3 %collective-permute-start.3 = (bf16[2,192,512]{2,1,0:T(8,128)(2,1)}, bf16[2,192,512]{2,1,0:T(8,128)(2,1)}, u32[]{:S(2)}, u32[]{:S(2)}) collective-permute-start(bf16[2,192,512]{2,1,0:T(8,128)(2,1)} %collective-permute-done.1), channel_id=1, source_target_pairs={{4,0},{8,4},{12,8},{5,1},{9,5},{13,9},{6,2},{10,6},{14,10},{7,3},{... | collective-permute-start | bytes 1179656 | tf_op jit(solution)/shard_map/ppermute | solution.py:22
  20.0 0.1 convert_reduce_fusion.2
  20.1 0.1 broadcast_in_dim.116
  20.2 0.1 reshape.155
  20.3 0.1 broadcast_in_dim.117
  20.4 0.1 eq.43
  20.5 0.0 copy-start.3
  20.5 0.6 compare_reduce_fusion
  21.1 1.8 %collective-permute-start.5 = (bf16[2,192,512]{2,1,0:T(8,128)(2,1)S(1)}, bf16[2,192,512]{2,1,0:T(8,128)(2,1)}, u32[]{:S(2)}, u32[]{:S(2)}) collective-permute-start(bf16[2,192,512]{2,1,0:T(8,128)(2,1)S(1)} %collective-permute-done), channel_id=1, source_target_pairs={{0,1},{1,0},{2,3},{3,2},{4,5},{5,4},{6,7},{7,6},{8,9},{9,8},{10,11... | collective-permute-start | bytes 1179656 | tf_op jit(solution)/shard_map/ppermute | solution.py:26
  22.9 0.1 collective-permute-start.6
  22.9 2.0 %collective-permute-done.2 = bf16[2,192,512]{2,1,0:T(8,128)(2,1)} collective-permute-done((bf16[2,192,512]{2,1,0:T(8,128)(2,1)S(1)}, bf16[2,192,512]{2,1,0:T(8,128)(2,1)}, u32[]{:S(2)}, u32[]{:S(2)}) %collective-permute-start.2) | collective-permute-done | bytes 393248 | tf_op jit(solution)/shard_map/ppermute | solution.py:22
  24.9 2.4 %collective-permute-start.7 = (bf16[2,192,512]{2,1,0:T(8,128)(2,1)}, bf16[2,192,512]{2,1,0:T(8,128)(2,1)}, u32[]{:S(2)}, u32[]{:S(2)}) collective-permute-start(bf16[2,192,512]{2,1,0:T(8,128)(2,1)} %collective-permute-done.2), channel_id=1, source_target_pairs={{0,1},{1,0},{2,3},{3,2},{4,5},{5,4},{6,7},{7,6},{8,9},{9,8},{10,11... | collective-permute-start | bytes 1179656 | tf_op jit(solution)/shard_map/ppermute | solution.py:26
  27.3 2.5 %collective-permute-done.3 = bf16[2,192,512]{2,1,0:T(8,128)(2,1)} collective-permute-done((bf16[2,192,512]{2,1,0:T(8,128)(2,1)}, bf16[2,192,512]{2,1,0:T(8,128)(2,1)}, u32[]{:S(2)}, u32[]{:S(2)}) %collective-permute-start.3) | collective-permute-done | bytes 393248 | tf_op jit(solution)/shard_map/ppermute | solution.py:22
  29.8 2.6 %collective-permute-start.8 = (bf16[2,192,512]{2,1,0:T(8,128)(2,1)}, bf16[2,192,512]{2,1,0:T(8,128)(2,1)}, u32[]{:S(2)}, u32[]{:S(2)}) collective-permute-start(bf16[2,192,512]{2,1,0:T(8,128)(2,1)} %collective-permute-done.3), channel_id=1, source_target_pairs={{0,1},{1,0},{2,3},{3,2},{4,5},{5,4},{6,7},{7,6},{8,9},{9,8},{10,11... | collective-permute-start | bytes 1179656 | tf_op jit(solution)/shard_map/ppermute | solution.py:26
  32.5 0.5 convert_element_type.33.flags_ref
  33.0 0.8 %copy.18.qclip_ref = s32[192,1]{1,0:T(8,128)} copy(s32[192,1]{0,1:T(1,128)S(1)} %bitcast.30) | data formatting | bytes 1536 | tf_op jit(solution)/shard_map/broadcast_in_dim | solution.py:230
  33.7 0.0 copy-done.2
  33.8 0.8 %multiply_convert_fusion.q_ref = bf16[2,192,512]{2,1,0:T(8,128)(2,1)} fusion(bf16[1,192,512]{2,1,0:T(8,128)(2,1)S(1)} %get-tuple-element.17, bf16[1,192,512]{2,1,0:T(8,128)(2,1)S(1)} %get-tuple-element.16), kind=kLoop, calls=%fused_computation.12 | loop fusion | flops 786432 | bytes 786432 | tf_op jit(solution)/shard_map/convert_element_type | solution.py:208
  34.6 0.0 collective-permute-done.4
  34.6 0.0 collective-permute-done.5
  34.6 0.0 collective-permute-done.6
  34.6 0.0 collective-permute-done.7
  34.6 0.0 collective-permute-done.8
  34.6 0.0 copy-done.5
  34.6 0.0 copy-done.3
  34.6 0.0 copy-start.4
  34.6 9.1 %shard_map.73 = bf16[192,512]{1,0:T(8,128)(2,1)} custom-call(s32[10]{0:T(128)} %convert_element_type.33.flags_ref, bf16[2,192,512]{2,1,0:T(8,128)(2,1)} %multiply_convert_fusion.q_ref, s32[10,3,192]{2,1,0:T(4,128)} %copy-done.3, s32[192,1]{1,0:T(8,128)} %copy.18.qclip_ref, bf16[1,2,192,512]{3,2,1,0:T(8,128)(2,1)} %get-tuple-element.13.refs_0_, ...), custom_call_target="tpu_custom_call" | custom-call | flops 1509949440 | bytes 5505024 | tf_op jit(solution)/shard_map/pallas_call | solution.py:215
  43.7 0.9 %fusion.33 = (bf16[64,512]{1,0:T(8,128)(2,1)S(1)}, bf16[64,512]{1,0:T(8,128)(2,1)S(1)}) fusion(bf16[192,512]{1,0:T(8,128)(2,1)} %shard_map.73), kind=kLoop, calls=%fused_computation.73 | loop fusion | bytes 262144 | tf_op jit(solution)/shard_map/slice | solution.py:333
  44.7 1.3 %collective-permute-start.12 = (bf16[192,512]{1,0:T(8,128)(2,1)}, bf16[192,512]{1,0:T(8,128)(2,1)S(1)}, u32[]{:S(2)}, u32[]{:S(2)}) collective-permute-start(bf16[192,512]{1,0:T(8,128)(2,1)} %shard_map.73), channel_id=1, source_target_pairs={{2,0},{0,2},{3,1},{1,3},{6,4},{4,6},{7,5},{5,7},{10,8},{8,10},{11,... | collective-permute-start | bytes 589832 | tf_op jit(solution)/shard_map/ppermute | solution.py:348
  46.0 1.9 %collective-permute-start.13 = (bf16[64,512]{1,0:T(8,128)(2,1)S(1)}, bf16[64,512]{1,0:T(8,128)(2,1)S(1)}, u32[]{:S(2)}, u32[]{:S(2)}) collective-permute-start(bf16[64,512]{1,0:T(8,128)(2,1)S(1)} %get-tuple-element.15), channel_id=1, source_target_pairs={{3,0},{1,2},{6,1},{4,3},{7,4},{5,6},{10,5},{8,7},{11,8},{9,10},{14... | collective-permute-start | bytes 196616 | tf_op jit(solution)/shard_map/ppermute | solution.py:348
  47.9 8.1 %collective-permute-start.11 = (bf16[64,512]{1,0:T(8,128)(2,1)S(1)}, bf16[64,512]{1,0:T(8,128)(2,1)S(1)}, u32[]{:S(2)}, u32[]{:S(2)}) collective-permute-start(bf16[64,512]{1,0:T(8,128)(2,1)S(1)} %get-tuple-element.14), channel_id=1, source_target_pairs={{2,1},{0,3},{3,4},{1,6},{6,5},{4,7},{7,8},{5,10},{10,9},{8,11},{11... | collective-permute-start | bytes 196616 | tf_op jit(solution)/shard_map/ppermute | solution.py:348
  56.0 0.0 copy-done.4
  56.1 1.9 %collective-permute-start.10 = (bf16[64,512]{1,0:T(8,128)(2,1)S(1)}, bf16[64,512]{1,0:T(8,128)(2,1)S(1)}, u32[]{:S(2)}, u32[]{:S(2)}) collective-permute-start(bf16[64,512]{1,0:T(8,128)(2,1)S(1)} %get-tuple-element.15), channel_id=1, source_target_pairs={{1,0},{3,2},{4,1},{6,3},{5,4},{7,6},{8,5},{10,7},{9,8},{11,10},{12... | collective-permute-start | bytes 196616 | tf_op jit(solution)/shard_map/ppermute | solution.py:348
  58.0 3.7 %collective-permute-start.9 = (bf16[64,512]{1,0:T(8,128)(2,1)S(1)}, bf16[64,512]{1,0:T(8,128)(2,1)S(1)}, u32[]{:S(2)}, u32[]{:S(2)}) collective-permute-start(bf16[64,512]{1,0:T(8,128)(2,1)S(1)} %get-tuple-element.14), channel_id=1, source_target_pairs={{0,1},{2,3},{1,4},{3,6},{4,5},{6,7},{5,8},{7,10},{8,9},{10,11},{9,... | collective-permute-start | bytes 196616 | tf_op jit(solution)/shard_map/ppermute | solution.py:348
  61.7 0.0 collective-permute-done.13
  61.7 0.0 collective-permute-done.11
  61.7 0.0 collective-permute-done.12
  61.7 0.0 copy-done
  61.7 0.5 fusion
  62.2 0.0 collective-permute-done.10
  62.2 0.7 %collective-permute-done.9 = bf16[64,512]{1,0:T(8,128)(2,1)S(1)} collective-permute-done((bf16[64,512]{1,0:T(8,128)(2,1)S(1)}, bf16[64,512]{1,0:T(8,128)(2,1)S(1)}, u32[]{:S(2)}, u32[]{:S(2)}) %collective-permute-start.9) | collective-permute-done | bytes 65568 | tf_op jit(solution)/shard_map/ppermute | solution.py:348
  63.0 0.0 copy-done.1
  63.0 0.5 convolution_add_fusion
  63.5 0.4 multiply_reduce_fusion
  63.9 0.8 %multiply_convert_fusion.1 = bf16[192,512]{1,0:T(8,128)(2,1)} fusion(f32[192,1024]{1,0:T(8,128)S(1)} %get-tuple-element.9, s32[]{:T(128)S(6)} %select_n.93, f32[512]{0:T(512)S(1)} %convert_element_type.38, f32[192]{0:T(256)S(1)} %add_rsqrt_fusion), kind=kLoop, calls=%fused_computation.14 | loop fusion | flops 294912 | bytes 592644 | tf_op jit(solution)/shard_map/convert_element_type | solution.py:368
  (20 shorter events, 0.2 us)
Async XLA Ops:
  0.0 61.7 %copy-start = (bf16[1024,1024]{1,0:T(8,128)(2,1)S(1)}, bf16[1024,1024]{1,0:T(8,128)(2,1)}, u32[]{:S(2)}) copy-start(bf16[1024,1024]{1,0:T(8,128)(2,1)} %param.12) | copy-start | bytes 6291460
  0.0 33.7 %copy-start.2 = (bf16[192,512]{1,0:T(8,128)(2,1)S(1)}, bf16[192,512]{1,0:T(8,128)(2,1)}, u32[]{:S(2)}) copy-start(bf16[192,512]{1,0:T(8,128)(2,1)} %param.7) | copy-start | bytes 589828
  2.0 11.8 %collective-permute-start = (bf16[2,192,512]{2,1,0:T(8,128)(2,1)S(1)}, bf16[2,192,512]{2,1,0:T(8,128)(2,1)S(1)}, u32[]{:S(2)}, u32[]{:S(2)}) collective-permute-start(bf16[2,192,512]{2,1,0:T(8,128)(2,1)S(1)} %get-tuple-element.12), channel_id=1, source_target_pairs={{0,4},{4,8},{8,12},{1,5},{5,9},{9,13},{2,6},{6,10},{10,14},{3,7},{... | collective-permute-start | bytes 1179656 | tf_op jit(solution)/shard_map/ppermute | solution.py:22
  6.0 12.7 %collective-permute-start.1 = (bf16[2,192,512]{2,1,0:T(8,128)(2,1)S(1)}, bf16[2,192,512]{2,1,0:T(8,128)(2,1)}, u32[]{:S(2)}, u32[]{:S(2)}) collective-permute-start(bf16[2,192,512]{2,1,0:T(8,128)(2,1)S(1)} %get-tuple-element.12), channel_id=1, source_target_pairs={{4,0},{8,4},{12,8},{5,1},{9,5},{13,9},{6,2},{10,6},{14,10},{7,3},{... | collective-permute-start | bytes 1179656 | tf_op jit(solution)/shard_map/ppermute | solution.py:22
  7.3 27.2 %collective-permute-start.4 = (bf16[2,192,512]{2,1,0:T(8,128)(2,1)S(1)}, bf16[2,192,512]{2,1,0:T(8,128)(2,1)}, u32[]{:S(2)}, u32[]{:S(2)}) collective-permute-start(bf16[2,192,512]{2,1,0:T(8,128)(2,1)S(1)} %get-tuple-element.12), channel_id=1, source_target_pairs={{0,1},{1,0},{2,3},{3,2},{4,5},{5,4},{6,7},{7,6},{8,9},{9,8},{10,11... | collective-permute-start | bytes 1179656 | tf_op jit(solution)/shard_map/ppermute | solution.py:26
  13.8 20.8 %copy-start.5 = (bf16[2,192,512]{2,1,0:T(8,128)(2,1)}, bf16[2,192,512]{2,1,0:T(8,128)(2,1)S(1)}, u32[]{:S(2)}) copy-start(bf16[2,192,512]{2,1,0:T(8,128)(2,1)S(1)} %collective-permute-done) | copy-start | bytes 1179652
  13.8 11.2 %collective-permute-start.2 = (bf16[2,192,512]{2,1,0:T(8,128)(2,1)S(1)}, bf16[2,192,512]{2,1,0:T(8,128)(2,1)}, u32[]{:S(2)}, u32[]{:S(2)}) collective-permute-start(bf16[2,192,512]{2,1,0:T(8,128)(2,1)S(1)} %collective-permute-done), channel_id=1, source_target_pairs={{0,4},{4,8},{8,12},{1,5},{5,9},{9,13},{2,6},{6,10},{10,14},{3,7},{... | collective-permute-start | bytes 1179656 | tf_op jit(solution)/shard_map/ppermute | solution.py:22
  18.7 11.1 %collective-permute-start.3 = (bf16[2,192,512]{2,1,0:T(8,128)(2,1)}, bf16[2,192,512]{2,1,0:T(8,128)(2,1)}, u32[]{:S(2)}, u32[]{:S(2)}) collective-permute-start(bf16[2,192,512]{2,1,0:T(8,128)(2,1)} %collective-permute-done.1), channel_id=1, source_target_pairs={{4,0},{8,4},{12,8},{5,1},{9,5},{13,9},{6,2},{10,6},{14,10},{7,3},{... | collective-permute-start | bytes 1179656 | tf_op jit(solution)/shard_map/ppermute | solution.py:22
  20.5 14.1 %copy-start.3 = (s32[10,3,192]{2,1,0:T(4,128)}, s32[10,3,192]{2,1,0:T(4,128)S(1)}, u32[]{:S(2)}) copy-start(s32[10,3,192]{2,1,0:T(4,128)S(1)} %select_bitcast_fusion.2.code_ref) | copy-start | bytes 69124
  21.1 13.5 %collective-permute-start.5 = (bf16[2,192,512]{2,1,0:T(8,128)(2,1)S(1)}, bf16[2,192,512]{2,1,0:T(8,128)(2,1)}, u32[]{:S(2)}, u32[]{:S(2)}) collective-permute-start(bf16[2,192,512]{2,1,0:T(8,128)(2,1)S(1)} %collective-permute-done), channel_id=1, source_target_pairs={{0,1},{1,0},{2,3},{3,2},{4,5},{5,4},{6,7},{7,6},{8,9},{9,8},{10,11... | collective-permute-start | bytes 1179656 | tf_op jit(solution)/shard_map/ppermute | solution.py:26
  22.9 11.7 %collective-permute-start.6 = (bf16[2,192,512]{2,1,0:T(8,128)(2,1)}, bf16[2,192,512]{2,1,0:T(8,128)(2,1)}, u32[]{:S(2)}, u32[]{:S(2)}) collective-permute-start(bf16[2,192,512]{2,1,0:T(8,128)(2,1)} %collective-permute-done.1), channel_id=1, source_target_pairs={{0,1},{1,0},{2,3},{3,2},{4,5},{5,4},{6,7},{7,6},{8,9},{9,8},{10,11... | collective-permute-start | bytes 1179656 | tf_op jit(solution)/shard_map/ppermute | solution.py:26
  24.9 9.7 %collective-permute-start.7 = (bf16[2,192,512]{2,1,0:T(8,128)(2,1)}, bf16[2,192,512]{2,1,0:T(8,128)(2,1)}, u32[]{:S(2)}, u32[]{:S(2)}) collective-permute-start(bf16[2,192,512]{2,1,0:T(8,128)(2,1)} %collective-permute-done.2), channel_id=1, source_target_pairs={{0,1},{1,0},{2,3},{3,2},{4,5},{5,4},{6,7},{7,6},{8,9},{9,8},{10,11... | collective-permute-start | bytes 1179656 | tf_op jit(solution)/shard_map/ppermute | solution.py:26
  29.8 4.8 %collective-permute-start.8 = (bf16[2,192,512]{2,1,0:T(8,128)(2,1)}, bf16[2,192,512]{2,1,0:T(8,128)(2,1)}, u32[]{:S(2)}, u32[]{:S(2)}) collective-permute-start(bf16[2,192,512]{2,1,0:T(8,128)(2,1)} %collective-permute-done.3), channel_id=1, source_target_pairs={{0,1},{1,0},{2,3},{3,2},{4,5},{5,4},{6,7},{7,6},{8,9},{9,8},{10,11... | collective-permute-start | bytes 1179656 | tf_op jit(solution)/shard_map/ppermute | solution.py:26
  34.6 21.4 %copy-start.4 = (bf16[512]{0:T(512)(128)(2,1)S(1)}, bf16[512]{0:T(512)(128)(2,1)}, u32[]{:S(2)}) copy-start(bf16[512]{0:T(512)(128)(2,1)} %param.13) | copy-start | bytes 3076
  43.7 19.2 %copy-start.1 = (bf16[192,512]{1,0:T(8,128)(2,1)S(1)}, bf16[192,512]{1,0:T(8,128)(2,1)}, u32[]{:S(2)}) copy-start(bf16[192,512]{1,0:T(8,128)(2,1)} %shard_map.73) | copy-start | bytes 589828
  44.7 17.0 %collective-permute-start.12 = (bf16[192,512]{1,0:T(8,128)(2,1)}, bf16[192,512]{1,0:T(8,128)(2,1)S(1)}, u32[]{:S(2)}, u32[]{:S(2)}) collective-permute-start(bf16[192,512]{1,0:T(8,128)(2,1)} %shard_map.73), channel_id=1, source_target_pairs={{2,0},{0,2},{3,1},{1,3},{6,4},{4,6},{7,5},{5,7},{10,8},{8,10},{11,... | collective-permute-start | bytes 589832 | tf_op jit(solution)/shard_map/ppermute | solution.py:348
  46.0 15.7 %collective-permute-start.13 = (bf16[64,512]{1,0:T(8,128)(2,1)S(1)}, bf16[64,512]{1,0:T(8,128)(2,1)S(1)}, u32[]{:S(2)}, u32[]{:S(2)}) collective-permute-start(bf16[64,512]{1,0:T(8,128)(2,1)S(1)} %get-tuple-element.15), channel_id=1, source_target_pairs={{3,0},{1,2},{6,1},{4,3},{7,4},{5,6},{10,5},{8,7},{11,8},{9,10},{14... | collective-permute-start | bytes 196616 | tf_op jit(solution)/shard_map/ppermute | solution.py:348
  47.9 13.8 %collective-permute-start.11 = (bf16[64,512]{1,0:T(8,128)(2,1)S(1)}, bf16[64,512]{1,0:T(8,128)(2,1)S(1)}, u32[]{:S(2)}, u32[]{:S(2)}) collective-permute-start(bf16[64,512]{1,0:T(8,128)(2,1)S(1)} %get-tuple-element.14), channel_id=1, source_target_pairs={{2,1},{0,3},{3,4},{1,6},{6,5},{4,7},{7,8},{5,10},{10,9},{8,11},{11... | collective-permute-start | bytes 196616 | tf_op jit(solution)/shard_map/ppermute | solution.py:348
  56.1 6.2 %collective-permute-start.10 = (bf16[64,512]{1,0:T(8,128)(2,1)S(1)}, bf16[64,512]{1,0:T(8,128)(2,1)S(1)}, u32[]{:S(2)}, u32[]{:S(2)}) collective-permute-start(bf16[64,512]{1,0:T(8,128)(2,1)S(1)} %get-tuple-element.15), channel_id=1, source_target_pairs={{1,0},{3,2},{4,1},{6,3},{5,4},{7,6},{8,5},{10,7},{9,8},{11,10},{12... | collective-permute-start | bytes 196616 | tf_op jit(solution)/shard_map/ppermute | solution.py:348
  58.0 5.0 %collective-permute-start.9 = (bf16[64,512]{1,0:T(8,128)(2,1)S(1)}, bf16[64,512]{1,0:T(8,128)(2,1)S(1)}, u32[]{:S(2)}, u32[]{:S(2)}) collective-permute-start(bf16[64,512]{1,0:T(8,128)(2,1)S(1)} %get-tuple-element.14), channel_id=1, source_target_pairs={{0,1},{2,3},{1,4},{3,6},{4,5},{6,7},{5,8},{7,10},{8,9},{10,11},{9,... | collective-permute-start | bytes 196616 | tf_op jit(solution)/shard_map/ppermute | solution.py:348

commit v4 on v2

--- a/solution.py
+++ b/solution.py
@@ -99,14 +99,25 @@
 
 def whole_kernel(sources, flags_ref, q_ref, code_ref, qclip_ref, *refs):
     n_in = max(src for src, _ in sources) + 1
-    kv_refs = refs[:n_in]
-    out_ref, bias_ref, m_ref, l_ref, acc_ref = refs[n_in:]
+    kv_hbm = refs[:n_in]
+    out_ref, bias_ref, m_ref, l_ref, acc_ref, kv_buf, sems = refs[n_in:]
     row_count, col_count = out_ref.shape
     sub_rows = code_ref.shape[1]
     piece = row_count // sub_rows
     pair = 2 * HD
     qclip = qclip_ref[...]
     low = lax.broadcasted_iota(jnp.int32, (row_count, pair), 1) < HD
+
+    def fetch(b):
+        src, idx = sources[b]
+        return pltpu.make_async_copy(kv_hbm[src].at[idx], kv_buf.at[b], sems.at[b])
+
+    for b in range(len(sources)):
+
+        @pl.when(flags_ref[b] > 0)
+        def _():
+            fetch(b).start()
+
     for b in range(len(sources)):
 
         @pl.when(flags_ref[b] > 0)
@@ -129,9 +140,8 @@
     acc_ref[...] = jnp.zeros(acc_ref.shape, jnp.float32)
 
     def scores(b, hp, e):
-        src, idx = sources[b]
         cols = slice(hp * pair, (hp + 1) * pair)
-        k_p = kv_refs[src][idx, 0, :, cols]
+        k_p = kv_buf[b, 0, :, cols]
         s = lax.dot_general(
             q_ref[e, :, cols], k_p, (((1,), (1,)), ((), ())), preferred_element_type=jnp.float32
         )
@@ -141,6 +151,7 @@
 
         @pl.when(flags_ref[b] > 0)
         def _():
+            fetch(b).wait()
             for hp in range(col_count // pair):
                 for e in range(2):
                     h = 2 * hp + e
@@ -150,10 +161,9 @@
 
         @pl.when(flags_ref[b] > 0)
         def _():
-            src, idx = sources[b]
             for hp in range(col_count // pair):
                 cols = slice(hp * pair, (hp + 1) * pair)
-                v_p = kv_refs[src][idx, 1, :, cols]
+                v_p = kv_buf[b, 1, :, cols]
                 pvs = []
                 for e in range(2):
                     h = 2 * hp + e
@@ -199,6 +209,8 @@
             pltpu.VMEM((head_count, row_count, 1), jnp.float32),
             pltpu.VMEM((head_count, row_count, 1), jnp.float32),
             pltpu.VMEM((row_count, col_count), jnp.float32),
+            pltpu.VMEM((len(blocks),) + inputs[0].shape[1:], inputs[0].dtype),
+            pltpu.SemaphoreType.DMA((len(blocks),)),
         ]
         aliases = {}
         extra = ()
@@ -215,7 +227,9 @@
         else functools.partial(chunk_kernel, sources, has_state, final),
         out_shape=out_shape,
         in_specs=[pl.BlockSpec(memory_space=pltpu.SMEM)]
-        + [pl.BlockSpec(memory_space=pltpu.VMEM)] * (3 + n_in + len(extra)),
+        + [pl.BlockSpec(memory_space=pltpu.VMEM)] * 3
+        + [pl.BlockSpec(memory_space=pl.ANY if final else pltpu.VMEM)] * n_in
+        + [pl.BlockSpec(memory_space=pltpu.VMEM)] * len(extra),
         out_specs=out_specs,
         scratch_shapes=scratch,
         input_output_aliases=aliases,

time: 61.8 us -> 61.8 us (level)
  the two profiles are of different devices: /device:TPU:20 before, /device:TPU:24 now
where the time goes in v4:
time: 61.8 us; the launch traced here: 60.7 us
  starting transfers between devices  27.9 us (45%)
  waiting for transfers between devices  11.5 us (19%)
  Pallas kernels  9.85 us (16%)
  other arithmetic  6.17 us (10%)
  local copies, waits for them, and re-layouts  3.87 us (6%)
  matrix products  1.02 us (2%)
    ppermute x5, starting transfers between devices, body(): parts.append(lax.ppermute(pieces[d], ('seq', 'head', 'sub'), pairs))  14.1 us
    ppermute x4, starting transfers between devices, shifted(): return lax.ppermute(x, axis, pairs)  13.2 us
    pallas_call x1, Pallas kernels, attend_chunk(): pl.pallas_call(functools.partial(whole_kernel, sources) if final else fun...  9.85 us
    ppermute x4, waiting for transfers between devices, shifted(): return lax.ppermute(x, axis, pairs)  8.38 us
    ppermute x5, waiting for transfers between devices, body(): parts.append(lax.ppermute(pieces[d], ('seq', 'head', 'sub'), pairs))  3.1 us
    another operation x1, other arithmetic, body(): own = jnp.stack([key_rows, value_rows])  1.98 us
  transfers between devices with their start and end apart: 14, of which 4 were waited for; matrix products, arithmetic and copies ran while one was open for 11% of the time, Pallas kernels for 0%

profile of v4, /device:TPU:24, one launch (start us, length us, event | category | flops | bytes accessed | tf_op | source)
XLA Modules:
  0.0 60.7 jit_solution(419715714714758759)
XLA Ops:
  0.0 0.0 copy-start
  0.0 2.0 %pad_maximum_fusion = (bf16[2,192,512]{2,1,0:T(8,128)(2,1)S(1)}, bf16[1,2,192,512]{3,2,1,0:T(8,128)(2,1)}) fusion(bf16[1,192,512]{2,1,0:T(8,128)(2,1)} %bitcast.28, bf16[1,192,512]{2,1,0:T(8,128)(2,1)} %bitcast.29), kind=kLoop, calls=%fused_computation.13 | loop fusion | flops 196608 | bytes 1179648 | tf_op jit(solution)/shard_map/stack | solution.py:302
  2.0 1.3 %collective-permute-start = (bf16[2,192,512]{2,1,0:T(8,128)(2,1)S(1)}, bf16[2,192,512]{2,1,0:T(8,128)(2,1)S(1)}, u32[]{:S(2)}, u32[]{:S(2)}) collective-permute-start(bf16[2,192,512]{2,1,0:T(8,128)(2,1)S(1)} %get-tuple-element.12), channel_id=1, source_target_pairs={{0,4},{4,8},{8,12},{1,5},{5,9},{9,13},{2,6},{6,10},{10,14},{3,7},{... | collective-permute-start | bytes 1179656 | tf_op jit(solution)/shard_map/ppermute | solution.py:22
  3.3 5.3 %collective-permute-start.1 = (bf16[2,192,512]{2,1,0:T(8,128)(2,1)S(1)}, bf16[2,192,512]{2,1,0:T(8,128)(2,1)}, u32[]{:S(2)}, u32[]{:S(2)}) collective-permute-start(bf16[2,192,512]{2,1,0:T(8,128)(2,1)S(1)} %get-tuple-element.12), channel_id=1, source_target_pairs={{4,0},{8,4},{12,8},{5,1},{9,5},{13,9},{6,2},{10,6},{14,10},{7,3},{... | collective-permute-start | bytes 1179656 | tf_op jit(solution)/shard_map/ppermute | solution.py:22
  8.6 0.0 collective-permute-start.4
  8.7 0.1 stack.14
  8.7 0.1 slice.18
  8.8 0.1 reshape.158
  8.9 0.7 %constant_dynamic-slice_fusion = s32[3,24]{1,0:T(4,128)S(1)} fusion(s32[6,24]{1,0:T(8,128)} %param.11, s32[]{:T(128)S(6)} %select_n.81), kind=kLoop, calls=%fused_computation.67 | loop fusion | bytes 580 | tf_op jit(solution)/shard_map/dynamic_slice | solution.py:261
  9.6 0.1 le.32
  9.7 0.1 copy.19
  9.8 0.6 gather_fusion
  10.4 0.1 copy.16
  10.5 0.1 reshape.161
  10.5 0.8 %reduce-window.8 = s32[6,1]{0,1:T(1,128)S(1)} reduce-window(s32[6,1]{0,1:T(1,128)} %bitcast.34, s32[]{:T(128)} %constant.94.clone.1), window={size=6x1 pad=5_0x0_0}, to_apply=%region_0.0 | reduce-window | flops 30 | bytes 52 | tf_op jit(solution)/shard_map/reduce-window.3
  11.4 0.1 convert_reduce_fusion
  11.5 3.2 %collective-permute-done = bf16[2,192,512]{2,1,0:T(8,128)(2,1)S(1)} collective-permute-done((bf16[2,192,512]{2,1,0:T(8,128)(2,1)S(1)}, bf16[2,192,512]{2,1,0:T(8,128)(2,1)S(1)}, u32[]{:S(2)}, u32[]{:S(2)}) %collective-permute-start) | collective-permute-done | bytes 393248 | tf_op jit(solution)/shard_map/ppermute | solution.py:22
  14.7 1.3 %collective-permute-start.2 = (bf16[2,192,512]{2,1,0:T(8,128)(2,1)S(1)}, bf16[2,192,512]{2,1,0:T(8,128)(2,1)}, u32[]{:S(2)}, u32[]{:S(2)}) collective-permute-start(bf16[2,192,512]{2,1,0:T(8,128)(2,1)S(1)} %collective-permute-done), channel_id=1, source_target_pairs={{0,4},{4,8},{8,12},{1,5},{5,9},{9,13},{2,6},{6,10},{10,14},{3,7},{... | collective-permute-start | bytes 1179656 | tf_op jit(solution)/shard_map/ppermute | solution.py:22
  16.0 0.0 collective-permute-done.1
  16.0 5.3 %collective-permute-start.3 = (bf16[2,192,512]{2,1,0:T(8,128)(2,1)}, bf16[2,192,512]{2,1,0:T(8,128)(2,1)}, u32[]{:S(2)}, u32[]{:S(2)}) collective-permute-start(bf16[2,192,512]{2,1,0:T(8,128)(2,1)} %collective-permute-done.1), channel_id=1, source_target_pairs={{4,0},{8,4},{12,8},{5,1},{9,5},{13,9},{6,2},{10,6},{14,10},{7,3},{... | collective-permute-start | bytes 1179656 | tf_op jit(solution)/shard_map/ppermute | solution.py:22
  21.3 0.1 convert_reduce_fusion.2
  21.4 0.1 broadcast_in_dim.116
  21.5 0.1 reshape.155
  21.6 0.1 broadcast_in_dim.117
  21.7 0.1 eq.43
  21.8 0.0 copy-start.3
  21.8 0.6 compare_reduce_fusion
  22.4 0.1 collective-permute-start.5
  22.4 0.5 collective-permute-start.6
  22.9 3.8 %collective-permute-done.2 = bf16[2,192,512]{2,1,0:T(8,128)(2,1)} collective-permute-done((bf16[2,192,512]{2,1,0:T(8,128)(2,1)S(1)}, bf16[2,192,512]{2,1,0:T(8,128)(2,1)}, u32[]{:S(2)}, u32[]{:S(2)}) %collective-permute-start.2) | collective-permute-done | bytes 393248 | tf_op jit(solution)/shard_map/ppermute | solution.py:22
  26.7 0.0 collective-permute-start.7
  26.7 1.4 %collective-permute-done.3 = bf16[2,192,512]{2,1,0:T(8,128)(2,1)} collective-permute-done((bf16[2,192,512]{2,1,0:T(8,128)(2,1)}, bf16[2,192,512]{2,1,0:T(8,128)(2,1)}, u32[]{:S(2)}, u32[]{:S(2)}) %collective-permute-start.3) | collective-permute-done | bytes 393248 | tf_op jit(solution)/shard_map/ppermute | solution.py:22
  28.1 0.0 collective-permute-start.8
  28.1 0.5 convert_element_type.33.flags_ref
  28.6 0.8 %copy.18.qclip_ref = s32[192,1]{1,0:T(8,128)} copy(s32[192,1]{0,1:T(1,128)S(1)} %bitcast.30) | data formatting | bytes 1536 | tf_op jit(solution)/shard_map/broadcast_in_dim | solution.py:241
  29.4 0.0 copy-done.2
  29.4 0.8 %multiply_convert_fusion.q_ref = bf16[2,192,512]{2,1,0:T(8,128)(2,1)} fusion(bf16[1,192,512]{2,1,0:T(8,128)(2,1)S(1)} %get-tuple-element.17, bf16[1,192,512]{2,1,0:T(8,128)(2,1)S(1)} %get-tuple-element.16), kind=kLoop, calls=%fused_computation.12 | loop fusion | flops 786432 | bytes 786432 | tf_op jit(solution)/shard_map/convert_element_type | solution.py:217
  30.2 0.0 collective-permute-done.4
  30.2 0.0 collective-permute-done.5
  30.2 0.0 collective-permute-done.6
  30.2 0.0 collective-permute-done.7
  30.2 0.0 collective-permute-done.8
  30.3 0.0 copy-done.5
  30.3 0.0 copy-done.3
  30.3 0.0 copy-start.4
  30.3 9.8 %shard_map.73 = bf16[192,512]{1,0:T(8,128)(2,1)} custom-call(s32[10]{0:T(128)} %convert_element_type.33.flags_ref, bf16[2,192,512]{2,1,0:T(8,128)(2,1)} %multiply_convert_fusion.q_ref, s32[10,3,192]{2,1,0:T(4,128)} %copy-done.3, s32[192,1]{1,0:T(8,128)} %copy.18.qclip_ref, bf16[1,2,192,512]{3,2,1,0:T(8,128)(2,1)} %get-tuple-element.13.refs_0_, ...), custom_call_target="tpu_custom_call" | custom-call | flops 1509949440 | bytes 5505024 | tf_op jit(solution)/shard_map/pallas_call | solution.py:224
  40.1 0.0 copy-start.1
  40.2 0.9 %fusion.33 = (bf16[64,512]{1,0:T(8,128)(2,1)S(1)}, bf16[64,512]{1,0:T(8,128)(2,1)S(1)}) fusion(bf16[192,512]{1,0:T(8,128)(2,1)} %shard_map.73), kind=kLoop, calls=%fused_computation.73 | loop fusion | bytes 262144 | tf_op jit(solution)/shard_map/slice | solution.py:344
  41.1 1.5 %collective-permute-start.12 = (bf16[192,512]{1,0:T(8,128)(2,1)}, bf16[192,512]{1,0:T(8,128)(2,1)S(1)}, u32[]{:S(2)}, u32[]{:S(2)}) collective-permute-start(bf16[192,512]{1,0:T(8,128)(2,1)} %shard_map.73), channel_id=1, source_target_pairs={{2,0},{0,2},{3,1},{1,3},{6,4},{4,6},{7,5},{5,7},{10,8},{8,10},{11,... | collective-permute-start | bytes 589832 | tf_op jit(solution)/shard_map/ppermute | solution.py:359
  42.6 4.2 %collective-permute-start.13 = (bf16[64,512]{1,0:T(8,128)(2,1)S(1)}, bf16[64,512]{1,0:T(8,128)(2,1)S(1)}, u32[]{:S(2)}, u32[]{:S(2)}) collective-permute-start(bf16[64,512]{1,0:T(8,128)(2,1)S(1)} %get-tuple-element.15), channel_id=1, source_target_pairs={{3,0},{1,2},{6,1},{4,3},{7,4},{5,6},{10,5},{8,7},{11,8},{9,10},{14... | collective-permute-start | bytes 196616 | tf_op jit(solution)/shard_map/ppermute | solution.py:359
  46.8 1.9 %collective-permute-start.11 = (bf16[64,512]{1,0:T(8,128)(2,1)S(1)}, bf16[64,512]{1,0:T(8,128)(2,1)S(1)}, u32[]{:S(2)}, u32[]{:S(2)}) collective-permute-start(bf16[64,512]{1,0:T(8,128)(2,1)S(1)} %get-tuple-element.14), channel_id=1, source_target_pairs={{2,1},{0,3},{3,4},{1,6},{6,5},{4,7},{7,8},{5,10},{10,9},{8,11},{11... | collective-permute-start | bytes 196616 | tf_op jit(solution)/shard_map/ppermute | solution.py:359
  48.8 0.0 copy-done.4
  48.8 4.6 %collective-permute-start.10 = (bf16[64,512]{1,0:T(8,128)(2,1)S(1)}, bf16[64,512]{1,0:T(8,128)(2,1)S(1)}, u32[]{:S(2)}, u32[]{:S(2)}) collective-permute-start(bf16[64,512]{1,0:T(8,128)(2,1)S(1)} %get-tuple-element.15), channel_id=1, source_target_pairs={{1,0},{3,2},{4,1},{6,3},{5,4},{7,6},{8,5},{10,7},{9,8},{11,10},{12... | collective-permute-start | bytes 196616 | tf_op jit(solution)/shard_map/ppermute | solution.py:359
  53.4 1.9 %collective-permute-start.9 = (bf16[64,512]{1,0:T(8,128)(2,1)S(1)}, bf16[64,512]{1,0:T(8,128)(2,1)S(1)}, u32[]{:S(2)}, u32[]{:S(2)}) collective-permute-start(bf16[64,512]{1,0:T(8,128)(2,1)S(1)} %get-tuple-element.14), channel_id=1, source_target_pairs={{0,1},{2,3},{1,4},{3,6},{4,5},{6,7},{5,8},{7,10},{8,9},{10,11},{9,... | collective-permute-start | bytes 196616 | tf_op jit(solution)/shard_map/ppermute | solution.py:359
  55.3 0.0 collective-permute-done.13
  55.3 0.0 collective-permute-done.11
  55.3 0.0 collective-permute-done.12
  55.4 0.0 copy-done
  55.4 0.5 fusion
  55.9 0.0 collective-permute-done.10
  55.9 3.1 %collective-permute-done.9 = bf16[64,512]{1,0:T(8,128)(2,1)S(1)} collective-permute-done((bf16[64,512]{1,0:T(8,128)(2,1)S(1)}, bf16[64,512]{1,0:T(8,128)(2,1)S(1)}, u32[]{:S(2)}, u32[]{:S(2)}) %collective-permute-start.9) | collective-permute-done | bytes 65568 | tf_op jit(solution)/shard_map/ppermute | solution.py:359
  59.0 0.5 convolution_add_fusion
  59.5 0.4 multiply_reduce_fusion
  59.9 0.8 %multiply_convert_fusion.1 = bf16[192,512]{1,0:T(8,128)(2,1)} fusion(f32[192,1024]{1,0:T(8,128)S(1)} %get-tuple-element.9, s32[]{:T(128)S(6)} %select_n.93, f32[512]{0:T(512)S(1)} %convert_element_type.38, f32[192]{0:T(256)S(1)} %add_rsqrt_fusion), kind=kLoop, calls=%fused_computation.14 | loop fusion | flops 294912 | bytes 592644 | tf_op jit(solution)/shard_map/convert_element_type | solution.py:379
  (20 shorter events, 0.2 us)
Async XLA Ops:
  0.0 55.4 %copy-start = (bf16[1024,1024]{1,0:T(8,128)(2,1)S(1)}, bf16[1024,1024]{1,0:T(8,128)(2,1)}, u32[]{:S(2)}) copy-start(bf16[1024,1024]{1,0:T(8,128)(2,1)} %param.12) | copy-start | bytes 6291460
  0.0 29.4 %copy-start.2 = (bf16[192,512]{1,0:T(8,128)(2,1)S(1)}, bf16[192,512]{1,0:T(8,128)(2,1)}, u32[]{:S(2)}) copy-start(bf16[192,512]{1,0:T(8,128)(2,1)} %param.7) | copy-start | bytes 589828
  2.0 12.7 %collective-permute-start = (bf16[2,192,512]{2,1,0:T(8,128)(2,1)S(1)}, bf16[2,192,512]{2,1,0:T(8,128)(2,1)S(1)}, u32[]{:S(2)}, u32[]{:S(2)}) collective-permute-start(bf16[2,192,512]{2,1,0:T(8,128)(2,1)S(1)} %get-tuple-element.12), channel_id=1, source_target_pairs={{0,4},{4,8},{8,12},{1,5},{5,9},{9,13},{2,6},{6,10},{10,14},{3,7},{... | collective-permute-start | bytes 1179656 | tf_op jit(solution)/shard_map/ppermute | solution.py:22
  3.3 12.7 %collective-permute-start.1 = (bf16[2,192,512]{2,1,0:T(8,128)(2,1)S(1)}, bf16[2,192,512]{2,1,0:T(8,128)(2,1)}, u32[]{:S(2)}, u32[]{:S(2)}) collective-permute-start(bf16[2,192,512]{2,1,0:T(8,128)(2,1)S(1)} %get-tuple-element.12), channel_id=1, source_target_pairs={{4,0},{8,4},{12,8},{5,1},{9,5},{13,9},{6,2},{10,6},{14,10},{7,3},{... | collective-permute-start | bytes 1179656 | tf_op jit(solution)/shard_map/ppermute | solution.py:22
  8.6 21.6 %collective-permute-start.4 = (bf16[2,192,512]{2,1,0:T(8,128)(2,1)S(1)}, bf16[2,192,512]{2,1,0:T(8,128)(2,1)}, u32[]{:S(2)}, u32[]{:S(2)}) collective-permute-start(bf16[2,192,512]{2,1,0:T(8,128)(2,1)S(1)} %get-tuple-element.12), channel_id=1, source_target_pairs={{0,1},{1,0},{2,3},{3,2},{4,5},{5,4},{6,7},{7,6},{8,9},{9,8},{10,11... | collective-permute-start | bytes 1179656 | tf_op jit(solution)/shard_map/ppermute | solution.py:26
  14.7 15.5 %copy-start.5 = (bf16[2,192,512]{2,1,0:T(8,128)(2,1)}, bf16[2,192,512]{2,1,0:T(8,128)(2,1)S(1)}, u32[]{:S(2)}) copy-start(bf16[2,192,512]{2,1,0:T(8,128)(2,1)S(1)} %collective-permute-done) | copy-start | bytes 1179652
  14.7 12.0 %collective-permute-start.2 = (bf16[2,192,512]{2,1,0:T(8,128)(2,1)S(1)}, bf16[2,192,512]{2,1,0:T(8,128)(2,1)}, u32[]{:S(2)}, u32[]{:S(2)}) collective-permute-start(bf16[2,192,512]{2,1,0:T(8,128)(2,1)S(1)} %collective-permute-done), channel_id=1, source_target_pairs={{0,4},{4,8},{8,12},{1,5},{5,9},{9,13},{2,6},{6,10},{10,14},{3,7},{... | collective-permute-start | bytes 1179656 | tf_op jit(solution)/shard_map/ppermute | solution.py:22
  16.0 12.1 %collective-permute-start.3 = (bf16[2,192,512]{2,1,0:T(8,128)(2,1)}, bf16[2,192,512]{2,1,0:T(8,128)(2,1)}, u32[]{:S(2)}, u32[]{:S(2)}) collective-permute-start(bf16[2,192,512]{2,1,0:T(8,128)(2,1)} %collective-permute-done.1), channel_id=1, source_target_pairs={{4,0},{8,4},{12,8},{5,1},{9,5},{13,9},{6,2},{10,6},{14,10},{7,3},{... | collective-permute-start | bytes 1179656 | tf_op jit(solution)/shard_map/ppermute | solution.py:22
  21.8 8.5 %copy-start.3 = (s32[10,3,192]{2,1,0:T(4,128)}, s32[10,3,192]{2,1,0:T(4,128)S(1)}, u32[]{:S(2)}) copy-start(s32[10,3,192]{2,1,0:T(4,128)S(1)} %select_bitcast_fusion.2.code_ref) | copy-start | bytes 69124
  22.4 7.9 %collective-permute-start.5 = (bf16[2,192,512]{2,1,0:T(8,128)(2,1)S(1)}, bf16[2,192,512]{2,1,0:T(8,128)(2,1)}, u32[]{:S(2)}, u32[]{:S(2)}) collective-permute-start(bf16[2,192,512]{2,1,0:T(8,128)(2,1)S(1)} %collective-permute-done), channel_id=1, source_target_pairs={{0,1},{1,0},{2,3},{3,2},{4,5},{5,4},{6,7},{7,6},{8,9},{9,8},{10,11... | collective-permute-start | bytes 1179656 | tf_op jit(solution)/shard_map/ppermute | solution.py:26
  22.4 7.8 %collective-permute-start.6 = (bf16[2,192,512]{2,1,0:T(8,128)(2,1)}, bf16[2,192,512]{2,1,0:T(8,128)(2,1)}, u32[]{:S(2)}, u32[]{:S(2)}) collective-permute-start(bf16[2,192,512]{2,1,0:T(8,128)(2,1)} %collective-permute-done.1), channel_id=1, source_target_pairs={{0,1},{1,0},{2,3},{3,2},{4,5},{5,4},{6,7},{7,6},{8,9},{9,8},{10,11... | collective-permute-start | bytes 1179656 | tf_op jit(solution)/shard_map/ppermute | solution.py:26
  26.7 3.5 %collective-permute-start.7 = (bf16[2,192,512]{2,1,0:T(8,128)(2,1)}, bf16[2,192,512]{2,1,0:T(8,128)(2,1)}, u32[]{:S(2)}, u32[]{:S(2)}) collective-permute-start(bf16[2,192,512]{2,1,0:T(8,128)(2,1)} %collective-permute-done.2), channel_id=1, source_target_pairs={{0,1},{1,0},{2,3},{3,2},{4,5},{5,4},{6,7},{7,6},{8,9},{9,8},{10,11... | collective-permute-start | bytes 1179656 | tf_op jit(solution)/shard_map/ppermute | solution.py:26
  28.1 2.2 %collective-permute-start.8 = (bf16[2,192,512]{2,1,0:T(8,128)(2,1)}, bf16[2,192,512]{2,1,0:T(8,128)(2,1)}, u32[]{:S(2)}, u32[]{:S(2)}) collective-permute-start(bf16[2,192,512]{2,1,0:T(8,128)(2,1)} %collective-permute-done.3), channel_id=1, source_target_pairs={{0,1},{1,0},{2,3},{3,2},{4,5},{5,4},{6,7},{7,6},{8,9},{9,8},{10,11... | collective-permute-start | bytes 1179656 | tf_op jit(solution)/shard_map/ppermute | solution.py:26
  30.3 18.5 %copy-start.4 = (bf16[512]{0:T(512)(128)(2,1)S(1)}, bf16[512]{0:T(512)(128)(2,1)}, u32[]{:S(2)}) copy-start(bf16[512]{0:T(512)(128)(2,1)} %param.13) | copy-start | bytes 3076
  40.1 18.8 %copy-start.1 = (bf16[192,512]{1,0:T(8,128)(2,1)S(1)}, bf16[192,512]{1,0:T(8,128)(2,1)}, u32[]{:S(2)}) copy-start(bf16[192,512]{1,0:T(8,128)(2,1)} %shard_map.73) | copy-start | bytes 589828
  41.1 14.3 %collective-permute-start.12 = (bf16[192,512]{1,0:T(8,128)(2,1)}, bf16[192,512]{1,0:T(8,128)(2,1)S(1)}, u32[]{:S(2)}, u32[]{:S(2)}) collective-permute-start(bf16[192,512]{1,0:T(8,128)(2,1)} %shard_map.73), channel_id=1, source_target_pairs={{2,0},{0,2},{3,1},{1,3},{6,4},{4,6},{7,5},{5,7},{10,8},{8,10},{11,... | collective-permute-start | bytes 589832 | tf_op jit(solution)/shard_map/ppermute | solution.py:359
  42.6 12.7 %collective-permute-start.13 = (bf16[64,512]{1,0:T(8,128)(2,1)S(1)}, bf16[64,512]{1,0:T(8,128)(2,1)S(1)}, u32[]{:S(2)}, u32[]{:S(2)}) collective-permute-start(bf16[64,512]{1,0:T(8,128)(2,1)S(1)} %get-tuple-element.15), channel_id=1, source_target_pairs={{3,0},{1,2},{6,1},{4,3},{7,4},{5,6},{10,5},{8,7},{11,8},{9,10},{14... | collective-permute-start | bytes 196616 | tf_op jit(solution)/shard_map/ppermute | solution.py:359
  46.8 8.5 %collective-permute-start.11 = (bf16[64,512]{1,0:T(8,128)(2,1)S(1)}, bf16[64,512]{1,0:T(8,128)(2,1)S(1)}, u32[]{:S(2)}, u32[]{:S(2)}) collective-permute-start(bf16[64,512]{1,0:T(8,128)(2,1)S(1)} %get-tuple-element.14), channel_id=1, source_target_pairs={{2,1},{0,3},{3,4},{1,6},{6,5},{4,7},{7,8},{5,10},{10,9},{8,11},{11... | collective-permute-start | bytes 196616 | tf_op jit(solution)/shard_map/ppermute | solution.py:359
  48.8 7.0 %collective-permute-start.10 = (bf16[64,512]{1,0:T(8,128)(2,1)S(1)}, bf16[64,512]{1,0:T(8,128)(2,1)S(1)}, u32[]{:S(2)}, u32[]{:S(2)}) collective-permute-start(bf16[64,512]{1,0:T(8,128)(2,1)S(1)} %get-tuple-element.15), channel_id=1, source_target_pairs={{1,0},{3,2},{4,1},{6,3},{5,4},{7,6},{8,5},{10,7},{9,8},{11,10},{12... | collective-permute-start | bytes 196616 | tf_op jit(solution)/shard_map/ppermute | solution.py:359
  53.4 5.6 %collective-permute-start.9 = (bf16[64,512]{1,0:T(8,128)(2,1)S(1)}, bf16[64,512]{1,0:T(8,128)(2,1)S(1)}, u32[]{:S(2)}, u32[]{:S(2)}) collective-permute-start(bf16[64,512]{1,0:T(8,128)(2,1)S(1)} %get-tuple-element.14), channel_id=1, source_target_pairs={{0,1},{2,3},{1,4},{3,6},{4,5},{6,7},{5,8},{7,10},{8,9},{10,11},{9,... | collective-permute-start | bytes 196616 | tf_op jit(solution)/shard_map/ppermute | solution.py:359

commit v5 on v4

--- a/solution.py
+++ b/solution.py
@@ -337,32 +337,23 @@
         attended = (weighted / running).astype(jnp.bfloat16)
 
     n_dev = n_seq * n_sub
-
-    def flat(dev, head):
-        return ((dev // n_sub) * n_head + head) * n_sub + dev % n_sub
-
-    pieces = {-1: attended[row_count - F :], 0: attended, 1: attended[:F]}
     width = out_weight.shape[1]
-    projected = jnp.zeros((row_count + 2 * F, width), jnp.float32)
-    for j in range(n_head):
-        parts = []
-        for d in (-1, 0, 1):
-            if j == 0 and d == 0:
-                parts.append(attended)
-                continue
-            pairs = [
-                (flat(i + d, (h + j) % n_head), flat(i, h))
-                for i in range(n_dev)
-                for h in range(n_head)
-                if 0 <= i + d < n_dev
-            ]
-            parts.append(lax.ppermute(pieces[d], ("seq", "head", "sub"), pairs))
-        src = (head_i + j) % n_head
+    projected = jnp.dot(
+        attended,
+        lax.dynamic_slice_in_dim(out_weight, head_i * col_count, col_count, 0),
+        preferred_element_type=jnp.float32,
+    )
+    for j in range(1, n_head):
+        got = rotated(attended, "head", n_head, j)
+        src = (head_i - j) % n_head
         projected = projected + jnp.dot(
-            jnp.concatenate(parts, axis=0),
+            got,
             lax.dynamic_slice_in_dim(out_weight, src * col_count, col_count, 0),
             preferred_element_type=jnp.float32,
         )
+    prev_tail = shifted(projected[row_count - F :], ("seq", "sub"), n_dev, -1)
+    next_head = shifted(projected[:F], ("seq", "sub"), n_dev, 1)
+    projected = jnp.concatenate([prev_tail, projected, next_head], axis=0)
 
     positions = token_first + jnp.arange(row_count, dtype=jnp.int32)
     clip_here = clip_index(positions, clip_ends)

time: 61.8 us -> 61.4 us (level)
  the two profiles are of different devices: /device:TPU:24 before, /device:TPU:20 now
where the time goes in v5:
time: 61.4 us; the launch traced here: 60.6 us
  waiting for transfers between devices  23.2 us (38%)
  starting transfers between devices  19.8 us (32%)
  Pallas kernels  7.27 us (12%)
  other arithmetic  6.21 us (10%)
  local copies, waits for them, and re-layouts  2.99 us (5%)
  matrix products  0.77 us (1%)
    ppermute x6, starting transfers between devices, shifted(): return lax.ppermute(x, axis, pairs)  17.6 us
    ppermute x6, waiting for transfers between devices, shifted(): return lax.ppermute(x, axis, pairs)  17.5 us
    pallas_call x1, Pallas kernels, attend_chunk(): pl.pallas_call(functools.partial(whole_kernel, sources) if final else fun...  7.27 us
    ppermute x6, waiting for transfers between devices, rotated(): lax.ppermute(x, axis, [(i, (i + step) % count) for i in range(count)])  5.69 us
    ppermute x6, starting transfers between devices, rotated(): lax.ppermute(x, axis, [(i, (i + step) % count) for i in range(count)])  2.21 us
    another operation x1, other arithmetic, body(): own = jnp.stack([key_rows, value_rows])  1.98 us
  transfers between devices with their start and end apart: 12, of which 6 were waited for; matrix products, arithmetic and copies ran while one was open for 10% of the time, Pallas kernels for 0%

profile of v5, /device:TPU:20, one launch (start us, length us, event | category | flops | bytes accessed | tf_op | source)
XLA Modules:
  0.0 60.6 jit_solution(7675467852852307566)
XLA Ops:
  0.0 0.0 copy-start
  0.0 0.0 copy-start.2
  0.0 2.0 %pad_maximum_fusion.2 = (bf16[2,192,512]{2,1,0:T(8,128)(2,1)S(1)}, bf16[1,2,192,512]{3,2,1,0:T(8,128)(2,1)}) fusion(bf16[1,192,512]{2,1,0:T(8,128)(2,1)} %bitcast.30, bf16[1,192,512]{2,1,0:T(8,128)(2,1)} %bitcast.31), kind=kLoop, calls=%fused_computation.15 | loop fusion | flops 196608 | bytes 1179648 | tf_op jit(solution)/shard_map/stack | solution.py:302
  2.0 3.5 %collective-permute-start = (bf16[2,192,512]{2,1,0:T(8,128)(2,1)S(1)}, bf16[2,192,512]{2,1,0:T(8,128)(2,1)S(1)}, u32[]{:S(2)}, u32[]{:S(2)}) collective-permute-start(bf16[2,192,512]{2,1,0:T(8,128)(2,1)S(1)} %get-tuple-element.14), channel_id=1, source_target_pairs={{0,4},{4,8},{8,12},{1,5},{5,9},{9,13},{2,6},{6,10},{10,14},{3,7},{... | collective-permute-start | bytes 1179656 | tf_op jit(solution)/shard_map/ppermute | solution.py:22
  5.5 2.4 %collective-permute-start.1 = (bf16[2,192,512]{2,1,0:T(8,128)(2,1)S(1)}, bf16[2,192,512]{2,1,0:T(8,128)(2,1)}, u32[]{:S(2)}, u32[]{:S(2)}) collective-permute-start(bf16[2,192,512]{2,1,0:T(8,128)(2,1)S(1)} %get-tuple-element.14), channel_id=1, source_target_pairs={{4,0},{8,4},{12,8},{5,1},{9,5},{13,9},{6,2},{10,6},{14,10},{7,3},{... | collective-permute-start | bytes 1179656 | tf_op jit(solution)/shard_map/ppermute | solution.py:22
  7.8 0.1 collective-permute-start.4
  8.1 0.1 stack.14
  8.1 0.1 slice.17
  8.2 0.1 reshape.158
  8.3 0.7 %constant_dynamic-slice_fusion = s32[3,24]{1,0:T(4,128)S(1)} fusion(s32[6,24]{1,0:T(8,128)} %param.11, s32[]{:T(128)S(6)} %select_n.75), kind=kLoop, calls=%fused_computation.59 | loop fusion | bytes 580 | tf_op jit(solution)/shard_map/dynamic_slice | solution.py:261
  9.0 0.1 le.32
  9.1 0.1 copy.19
  9.2 0.6 gather_fusion
  9.7 0.1 copy.16
  9.8 0.1 reshape.161
  9.9 0.8 %reduce-window.8 = s32[6,1]{0,1:T(1,128)S(1)} reduce-window(s32[6,1]{0,1:T(1,128)} %bitcast.36, s32[]{:T(128)} %constant.91.clone.1), window={size=6x1 pad=5_0x0_0}, to_apply=%region_0.0 | reduce-window | flops 30 | bytes 52 | tf_op jit(solution)/shard_map/reduce-window.3
  10.7 0.1 convert_reduce_fusion
  10.9 3.9 %collective-permute-done = bf16[2,192,512]{2,1,0:T(8,128)(2,1)S(1)} collective-permute-done((bf16[2,192,512]{2,1,0:T(8,128)(2,1)S(1)}, bf16[2,192,512]{2,1,0:T(8,128)(2,1)S(1)}, u32[]{:S(2)}, u32[]{:S(2)}) %collective-permute-start) | collective-permute-done | bytes 393248 | tf_op jit(solution)/shard_map/ppermute | solution.py:22
  14.7 0.0 copy-start.5
  14.7 3.5 %collective-permute-start.2 = (bf16[2,192,512]{2,1,0:T(8,128)(2,1)S(1)}, bf16[2,192,512]{2,1,0:T(8,128)(2,1)}, u32[]{:S(2)}, u32[]{:S(2)}) collective-permute-start(bf16[2,192,512]{2,1,0:T(8,128)(2,1)S(1)} %collective-permute-done), channel_id=1, source_target_pairs={{0,4},{4,8},{8,12},{1,5},{5,9},{9,13},{2,6},{6,10},{10,14},{3,7},{... | collective-permute-start | bytes 1179656 | tf_op jit(solution)/shard_map/ppermute | solution.py:22
  18.2 0.0 collective-permute-done.1
  18.2 2.4 %collective-permute-start.3 = (bf16[2,192,512]{2,1,0:T(8,128)(2,1)}, bf16[2,192,512]{2,1,0:T(8,128)(2,1)}, u32[]{:S(2)}, u32[]{:S(2)}) collective-permute-start(bf16[2,192,512]{2,1,0:T(8,128)(2,1)} %collective-permute-done.1), channel_id=1, source_target_pairs={{4,0},{8,4},{12,8},{5,1},{9,5},{13,9},{6,2},{10,6},{14,10},{7,3},{... | collective-permute-start | bytes 1179656 | tf_op jit(solution)/shard_map/ppermute | solution.py:22
  20.6 0.1 convert_reduce_fusion.2
  20.7 0.1 broadcast_in_dim.116
  20.8 0.1 reshape.155
  20.9 0.1 broadcast_in_dim.117
  21.0 0.1 eq.42
  21.1 0.0 copy-start.3
  21.1 0.6 compare_reduce_fusion
  21.6 0.1 collective-permute-start.5
  21.7 0.5 collective-permute-start.6
  22.2 4.6 %collective-permute-done.2 = bf16[2,192,512]{2,1,0:T(8,128)(2,1)} collective-permute-done((bf16[2,192,512]{2,1,0:T(8,128)(2,1)S(1)}, bf16[2,192,512]{2,1,0:T(8,128)(2,1)}, u32[]{:S(2)}, u32[]{:S(2)}) %collective-permute-start.2) | collective-permute-done | bytes 393248 | tf_op jit(solution)/shard_map/ppermute | solution.py:22
  26.8 0.0 collective-permute-start.7
  26.8 3.3 %collective-permute-done.3 = bf16[2,192,512]{2,1,0:T(8,128)(2,1)} collective-permute-done((bf16[2,192,512]{2,1,0:T(8,128)(2,1)}, bf16[2,192,512]{2,1,0:T(8,128)(2,1)}, u32[]{:S(2)}, u32[]{:S(2)}) %collective-permute-start.3) | collective-permute-done | bytes 393248 | tf_op jit(solution)/shard_map/ppermute | solution.py:22
  30.1 0.0 collective-permute-start.8
  30.1 0.5 convert_element_type.33.flags_ref
  30.7 0.8 %copy.18.qclip_ref = s32[192,1]{1,0:T(8,128)} copy(s32[192,1]{0,1:T(1,128)S(1)} %bitcast.32) | data formatting | bytes 1536 | tf_op jit(solution)/shard_map/broadcast_in_dim | solution.py:241
  31.4 0.0 copy-done.2
  31.5 0.8 %multiply_convert_fusion.q_ref = bf16[2,192,512]{2,1,0:T(8,128)(2,1)} fusion(bf16[1,192,512]{2,1,0:T(8,128)(2,1)S(1)} %get-tuple-element.17, bf16[1,192,512]{2,1,0:T(8,128)(2,1)S(1)} %get-tuple-element.16), kind=kLoop, calls=%fused_computation.14 | loop fusion | flops 786432 | bytes 786432 | tf_op jit(solution)/shard_map/convert_element_type | solution.py:217
  32.3 0.0 collective-permute-done.4
  32.3 0.0 collective-permute-done.5
  32.3 0.0 collective-permute-done.6
  32.3 0.0 collective-permute-done.7
  32.3 0.0 collective-permute-done.8
  32.3 0.0 copy-done.5
  32.3 0.0 copy-done.3
  32.3 7.3 %shard_map.73 = bf16[192,512]{1,0:T(8,128)(2,1)} custom-call(s32[10]{0:T(128)} %convert_element_type.33.flags_ref, bf16[2,192,512]{2,1,0:T(8,128)(2,1)} %multiply_convert_fusion.q_ref, s32[10,3,192]{2,1,0:T(4,128)} %copy-done.3, s32[192,1]{1,0:T(8,128)} %copy.18.qclip_ref, bf16[1,2,192,512]{3,2,1,0:T(8,128)(2,1)} %get-tuple-element.15.refs_0_, ...), custom_call_target="tpu_custom_call" | custom-call | flops 1509949440 | bytes 5505024 | tf_op jit(solution)/shard_map/pallas_call | solution.py:224
  39.6 0.0 copy-start.1
  39.6 1.6 %collective-permute-start.9 = (bf16[192,512]{1,0:T(8,128)(2,1)}, bf16[192,512]{1,0:T(8,128)(2,1)S(1)}, u32[]{:S(2)}, u32[]{:S(2)}) collective-permute-start(bf16[192,512]{1,0:T(8,128)(2,1)} %shard_map.73), channel_id=1, source_target_pairs={{0,2},{2,0},{1,3},{3,1},{4,6},{6,4},{5,7},{7,5},{8,10},{10,8},{9,1... | collective-permute-start | bytes 589832 | tf_op jit(solution)/shard_map/ppermute | solution.py:26
  41.2 5.7 %collective-permute-done.9 = bf16[192,512]{1,0:T(8,128)(2,1)S(1)} collective-permute-done((bf16[192,512]{1,0:T(8,128)(2,1)}, bf16[192,512]{1,0:T(8,128)(2,1)S(1)}, u32[]{:S(2)}, u32[]{:S(2)}) %collective-permute-start.9) | collective-permute-done | bytes 196640 | tf_op jit(solution)/shard_map/ppermute | solution.py:26
  46.9 0.0 copy-done
  46.9 0.4 fusion
  47.3 0.0 copy-done.1
  47.3 0.0 copy-start.4
  47.3 0.4 convolution_add_fusion
  47.7 4.0 %collective-permute-start.11 = (f32[64,1024]{1,0:T(8,128)S(1)}, f32[64,1024]{1,0:T(8,128)S(1)}, u32[]{:S(2)}, u32[]{:S(2)}) collective-permute-start(f32[64,1024]{1,0:T(8,128)S(1)} %get-tuple-element.13), channel_id=1, source_target_pairs={{1,0},{4,1},{5,4},{8,5},{9,8},{12,9},{13,12},{3,2},{6,3},{7,6},{10... | collective-permute-start | bytes 786440 | tf_op jit(solution)/shard_map/ppermute | solution.py:22
  51.7 1.9 %collective-permute-start.10 = (f32[64,1024]{1,0:T(8,128)S(1)}, f32[64,1024]{1,0:T(8,128)S(1)}, u32[]{:S(2)}, u32[]{:S(2)}) collective-permute-start(f32[64,1024]{1,0:T(8,128)S(1)} %get-tuple-element.12), channel_id=1, source_target_pairs={{0,1},{1,4},{4,5},{5,8},{8,9},{9,12},{12,13},{2,3},{3,6},{6,7},{7,... | collective-permute-start | bytes 786440 | tf_op jit(solution)/shard_map/ppermute | solution.py:22
  53.6 0.0 copy-done.4
  53.7 1.9 %collective-permute-done.11 = f32[64,1024]{1,0:T(8,128)S(1)} collective-permute-done((f32[64,1024]{1,0:T(8,128)S(1)}, f32[64,1024]{1,0:T(8,128)S(1)}, u32[]{:S(2)}, u32[]{:S(2)}) %collective-permute-start.11) | collective-permute-done | bytes 262176 | tf_op jit(solution)/shard_map/ppermute | solution.py:22
  55.6 3.8 %collective-permute-done.10 = f32[64,1024]{1,0:T(8,128)S(1)} collective-permute-done((f32[64,1024]{1,0:T(8,128)S(1)}, f32[64,1024]{1,0:T(8,128)S(1)}, u32[]{:S(2)}, u32[]{:S(2)}) %collective-permute-start.10) | collective-permute-done | bytes 262176 | tf_op jit(solution)/shard_map/ppermute | solution.py:22
  59.4 0.4 multiply_reduce_fusion
  59.8 0.8 %multiply_convert_fusion.1 = bf16[192,512]{1,0:T(8,128)(2,1)} fusion(f32[192,1024]{1,0:T(8,128)S(1)} %get-tuple-element.9, s32[]{:T(128)S(6)} %select_n.81, f32[512]{0:T(512)S(1)} %convert_element_type.38, f32[192]{0:T(256)S(1)} %add_rsqrt_fusion), kind=kLoop, calls=%fused_computation.16 | loop fusion | flops 294912 | bytes 592644 | tf_op jit(solution)/shard_map/convert_element_type | solution.py:370
  (18 shorter events, 0.2 us)
Async XLA Ops:
  0.0 46.9 %copy-start = (bf16[1024,1024]{1,0:T(8,128)(2,1)S(1)}, bf16[1024,1024]{1,0:T(8,128)(2,1)}, u32[]{:S(2)}) copy-start(bf16[1024,1024]{1,0:T(8,128)(2,1)} %param.12) | copy-start | bytes 6291460
  0.0 31.4 %copy-start.2 = (bf16[192,512]{1,0:T(8,128)(2,1)S(1)}, bf16[192,512]{1,0:T(8,128)(2,1)}, u32[]{:S(2)}) copy-start(bf16[192,512]{1,0:T(8,128)(2,1)} %param.7) | copy-start | bytes 589828
  2.0 12.7 %collective-permute-start = (bf16[2,192,512]{2,1,0:T(8,128)(2,1)S(1)}, bf16[2,192,512]{2,1,0:T(8,128)(2,1)S(1)}, u32[]{:S(2)}, u32[]{:S(2)}) collective-permute-start(bf16[2,192,512]{2,1,0:T(8,128)(2,1)S(1)} %get-tuple-element.14), channel_id=1, source_target_pairs={{0,4},{4,8},{8,12},{1,5},{5,9},{9,13},{2,6},{6,10},{10,14},{3,7},{... | collective-permute-start | bytes 1179656 | tf_op jit(solution)/shard_map/ppermute | solution.py:22
  5.5 12.7 %collective-permute-start.1 = (bf16[2,192,512]{2,1,0:T(8,128)(2,1)S(1)}, bf16[2,192,512]{2,1,0:T(8,128)(2,1)}, u32[]{:S(2)}, u32[]{:S(2)}) collective-permute-start(bf16[2,192,512]{2,1,0:T(8,128)(2,1)S(1)} %get-tuple-element.14), channel_id=1, source_target_pairs={{4,0},{8,4},{12,8},{5,1},{9,5},{13,9},{6,2},{10,6},{14,10},{7,3},{... | collective-permute-start | bytes 1179656 | tf_op jit(solution)/shard_map/ppermute | solution.py:22
  7.8 24.5 %collective-permute-start.4 = (bf16[2,192,512]{2,1,0:T(8,128)(2,1)S(1)}, bf16[2,192,512]{2,1,0:T(8,128)(2,1)}, u32[]{:S(2)}, u32[]{:S(2)}) collective-permute-start(bf16[2,192,512]{2,1,0:T(8,128)(2,1)S(1)} %get-tuple-element.14), channel_id=1, source_target_pairs={{0,1},{1,0},{2,3},{3,2},{4,5},{5,4},{6,7},{7,6},{8,9},{9,8},{10,11... | collective-permute-start | bytes 1179656 | tf_op jit(solution)/shard_map/ppermute | solution.py:26
  14.7 17.6 %copy-start.5 = (bf16[2,192,512]{2,1,0:T(8,128)(2,1)}, bf16[2,192,512]{2,1,0:T(8,128)(2,1)S(1)}, u32[]{:S(2)}) copy-start(bf16[2,192,512]{2,1,0:T(8,128)(2,1)S(1)} %collective-permute-done) | copy-start | bytes 1179652
  14.7 12.1 %collective-permute-start.2 = (bf16[2,192,512]{2,1,0:T(8,128)(2,1)S(1)}, bf16[2,192,512]{2,1,0:T(8,128)(2,1)}, u32[]{:S(2)}, u32[]{:S(2)}) collective-permute-start(bf16[2,192,512]{2,1,0:T(8,128)(2,1)S(1)} %collective-permute-done), channel_id=1, source_target_pairs={{0,4},{4,8},{8,12},{1,5},{5,9},{9,13},{2,6},{6,10},{10,14},{3,7},{... | collective-permute-start | bytes 1179656 | tf_op jit(solution)/shard_map/ppermute | solution.py:22
  18.2 11.9 %collective-permute-start.3 = (bf16[2,192,512]{2,1,0:T(8,128)(2,1)}, bf16[2,192,512]{2,1,0:T(8,128)(2,1)}, u32[]{:S(2)}, u32[]{:S(2)}) collective-permute-start(bf16[2,192,512]{2,1,0:T(8,128)(2,1)} %collective-permute-done.1), channel_id=1, source_target_pairs={{4,0},{8,4},{12,8},{5,1},{9,5},{13,9},{6,2},{10,6},{14,10},{7,3},{... | collective-permute-start | bytes 1179656 | tf_op jit(solution)/shard_map/ppermute | solution.py:22
  21.1 11.3 %copy-start.3 = (s32[10,3,192]{2,1,0:T(4,128)}, s32[10,3,192]{2,1,0:T(4,128)S(1)}, u32[]{:S(2)}) copy-start(s32[10,3,192]{2,1,0:T(4,128)S(1)} %select_bitcast_fusion.2.code_ref) | copy-start | bytes 69124
  21.6 10.7 %collective-permute-start.5 = (bf16[2,192,512]{2,1,0:T(8,128)(2,1)S(1)}, bf16[2,192,512]{2,1,0:T(8,128)(2,1)}, u32[]{:S(2)}, u32[]{:S(2)}) collective-permute-start(bf16[2,192,512]{2,1,0:T(8,128)(2,1)S(1)} %collective-permute-done), channel_id=1, source_target_pairs={{0,1},{1,0},{2,3},{3,2},{4,5},{5,4},{6,7},{7,6},{8,9},{9,8},{10,11... | collective-permute-start | bytes 1179656 | tf_op jit(solution)/shard_map/ppermute | solution.py:26
  21.7 10.6 %collective-permute-start.6 = (bf16[2,192,512]{2,1,0:T(8,128)(2,1)}, bf16[2,192,512]{2,1,0:T(8,128)(2,1)}, u32[]{:S(2)}, u32[]{:S(2)}) collective-permute-start(bf16[2,192,512]{2,1,0:T(8,128)(2,1)} %collective-permute-done.1), channel_id=1, source_target_pairs={{0,1},{1,0},{2,3},{3,2},{4,5},{5,4},{6,7},{7,6},{8,9},{9,8},{10,11... | collective-permute-start | bytes 1179656 | tf_op jit(solution)/shard_map/ppermute | solution.py:26
  26.8 5.5 %collective-permute-start.7 = (bf16[2,192,512]{2,1,0:T(8,128)(2,1)}, bf16[2,192,512]{2,1,0:T(8,128)(2,1)}, u32[]{:S(2)}, u32[]{:S(2)}) collective-permute-start(bf16[2,192,512]{2,1,0:T(8,128)(2,1)} %collective-permute-done.2), channel_id=1, source_target_pairs={{0,1},{1,0},{2,3},{3,2},{4,5},{5,4},{6,7},{7,6},{8,9},{9,8},{10,11... | collective-permute-start | bytes 1179656 | tf_op jit(solution)/shard_map/ppermute | solution.py:26
  30.1 2.2 %collective-permute-start.8 = (bf16[2,192,512]{2,1,0:T(8,128)(2,1)}, bf16[2,192,512]{2,1,0:T(8,128)(2,1)}, u32[]{:S(2)}, u32[]{:S(2)}) collective-permute-start(bf16[2,192,512]{2,1,0:T(8,128)(2,1)} %collective-permute-done.3), channel_id=1, source_target_pairs={{0,1},{1,0},{2,3},{3,2},{4,5},{5,4},{6,7},{7,6},{8,9},{9,8},{10,11... | collective-permute-start | bytes 1179656 | tf_op jit(solution)/shard_map/ppermute | solution.py:26
  39.6 7.6 %copy-start.1 = (bf16[192,512]{1,0:T(8,128)(2,1)S(1)}, bf16[192,512]{1,0:T(8,128)(2,1)}, u32[]{:S(2)}) copy-start(bf16[192,512]{1,0:T(8,128)(2,1)} %shard_map.73) | copy-start | bytes 589828
  39.6 7.2 %collective-permute-start.9 = (bf16[192,512]{1,0:T(8,128)(2,1)}, bf16[192,512]{1,0:T(8,128)(2,1)S(1)}, u32[]{:S(2)}, u32[]{:S(2)}) collective-permute-start(bf16[192,512]{1,0:T(8,128)(2,1)} %shard_map.73), channel_id=1, source_target_pairs={{0,2},{2,0},{1,3},{3,1},{4,6},{6,4},{5,7},{7,5},{8,10},{10,8},{9,1... | collective-permute-start | bytes 589832 | tf_op jit(solution)/shard_map/ppermute | solution.py:26
  47.3 6.4 %copy-start.4 = (bf16[512]{0:T(512)(128)(2,1)S(1)}, bf16[512]{0:T(512)(128)(2,1)}, u32[]{:S(2)}) copy-start(bf16[512]{0:T(512)(128)(2,1)} %param.13) | copy-start | bytes 3076
  47.7 7.9 %collective-permute-start.11 = (f32[64,1024]{1,0:T(8,128)S(1)}, f32[64,1024]{1,0:T(8,128)S(1)}, u32[]{:S(2)}, u32[]{:S(2)}) collective-permute-start(f32[64,1024]{1,0:T(8,128)S(1)} %get-tuple-element.13), channel_id=1, source_target_pairs={{1,0},{4,1},{5,4},{8,5},{9,8},{12,9},{13,12},{3,2},{6,3},{7,6},{10... | collective-permute-start | bytes 786440 | tf_op jit(solution)/shard_map/ppermute | solution.py:22
  51.7 7.7 %collective-permute-start.10 = (f32[64,1024]{1,0:T(8,128)S(1)}, f32[64,1024]{1,0:T(8,128)S(1)}, u32[]{:S(2)}, u32[]{:S(2)}) collective-permute-start(f32[64,1024]{1,0:T(8,128)S(1)} %get-tuple-element.12), channel_id=1, source_target_pairs={{0,1},{1,4},{4,5},{5,8},{8,9},{9,12},{12,13},{2,3},{3,6},{6,7},{7,... | collective-permute-start | bytes 786440 | tf_op jit(solution)/shard_map/ppermute | solution.py:22

commit v6 on v5

--- a/solution.py
+++ b/solution.py
@@ -300,6 +300,7 @@
         ]
 
     own = jnp.stack([key_rows, value_rows])
+    dev_reach = 1 + (longest - 2) // row_count
     if reach <= 4:
         to_partner = to_partner_apart
         mine = [(own, 0)]
@@ -311,7 +312,12 @@
             left = shifted(left, "seq", n_seq, -1)
             near = [(left, -step), (right, step)]
             mine += near
-            theirs += to_partner(near)
+            if n_sub == 2 and 2 * step + 1 > dev_reach:
+                sent = jnp.where(sub_i == 0, right, left)
+                off = jnp.where(sub_i == 0, -step, step)
+                theirs.append(([rotated(sent, "sub", n_sub, 1)], [off], 1 - sub_i))
+            else:
+                theirs += to_partner(near)
         attended = fold(None, mine, theirs)
     else:
         state = (

time: 61.4 us -> 62.7 us (1.021)
  Pallas kernels: 7.27 us -> 9.83 us
  starting transfers between devices: 19.8 us -> 18.2 us
  other arithmetic: 6.21 us -> 7.04 us
    pallas_call x1, Pallas kernels: 7.27 us -> 9.83 us  [attend_chunk(): pl.pallas_call(functools.partial(whole_kernel, sources) if final else fun...]
    ppermute x6, starting transfers between devices: 17.6 us -> 16 us  [shifted(): return lax.ppermute(x, axis, pairs)]
    select_n x0 -> x1, other arithmetic: none -> 0.85 us  [body(): sent = jnp.where(sub_i == 0, right, left)]
    ppermute x6 -> x5, waiting for transfers between devices: 5.69 us -> 6.03 us  [rotated(): lax.ppermute(x, axis, [(i, (i + step) % count) for i in range(count)])]
    ppermute x6 -> x5, starting transfers between devices: 2.21 us -> 2.19 us  [rotated(): lax.ppermute(x, axis, [(i, (i + step) % count) for i in range(count)])]
  transfers between devices with their start and end apart: 12 -> 11, of which waited for: 6 -> 6; matrix products, arithmetic and copies ran while one was open for 10% -> 11% of each run, Pallas kernels for 0% -> 0%
where the time goes in v6:
time: 62.7 us; the launch traced here: 62.3 us
  waiting for transfers between devices  23.1 us (37%)
  starting transfers between devices  18.2 us (29%)
  Pallas kernels  9.83 us (16%)
  other arithmetic  7.04 us (11%)
  local copies, waits for them, and re-layouts  2.98 us (5%)
  matrix products  0.77 us (1%)
    ppermute x6, waiting for transfers between devices, shifted(): return lax.ppermute(x, axis, pairs)  17.1 us
    ppermute x6, starting transfers between devices, shifted(): return lax.ppermute(x, axis, pairs)  16 us
    pallas_call x1, Pallas kernels, attend_chunk(): pl.pallas_call(functools.partial(whole_kernel, sources) if final else fun...  9.83 us
    ppermute x5, waiting for transfers between devices, rotated(): lax.ppermute(x, axis, [(i, (i + step) % count) for i in range(count)])  6.03 us
    ppermute x5, starting transfers between devices, rotated(): lax.ppermute(x, axis, [(i, (i + step) % count) for i in range(count)])  2.19 us
    another operation x1, other arithmetic, body(): own = jnp.stack([key_rows, value_rows])  1.98 us
  transfers between devices with their start and end apart: 11, of which 6 were waited for; matrix products, arithmetic and copies ran while one was open for 11% of the time, Pallas kernels for 0%

profile of v6, /device:TPU:20, one launch (start us, length us, event | category | flops | bytes accessed | tf_op | source)
XLA Modules:
  0.0 62.3 jit_solution(2074893201055195788)
XLA Ops:
  0.0 0.0 copy-start
  0.0 0.0 copy-start.4
  0.0 2.0 %pad_maximum_fusion.2 = (bf16[2,192,512]{2,1,0:T(8,128)(2,1)S(1)}, bf16[1,2,192,512]{3,2,1,0:T(8,128)(2,1)}) fusion(bf16[1,192,512]{2,1,0:T(8,128)(2,1)} %bitcast.31, bf16[1,192,512]{2,1,0:T(8,128)(2,1)} %bitcast.32), kind=kLoop, calls=%fused_computation.15 | loop fusion | flops 196608 | bytes 1179648 | tf_op jit(solution)/shard_map/stack | solution.py:302
  2.0 3.5 %collective-permute-start = (bf16[2,192,512]{2,1,0:T(8,128)(2,1)S(1)}, bf16[2,192,512]{2,1,0:T(8,128)(2,1)}, u32[]{:S(2)}, u32[]{:S(2)}) collective-permute-start(bf16[2,192,512]{2,1,0:T(8,128)(2,1)S(1)} %get-tuple-element.14), channel_id=1, source_target_pairs={{0,4},{4,8},{8,12},{1,5},{5,9},{9,13},{2,6},{6,10},{10,14},{3,7},{... | collective-permute-start | bytes 1179656 | tf_op jit(solution)/shard_map/ppermute | solution.py:22
  5.5 2.4 %collective-permute-start.1 = (bf16[2,192,512]{2,1,0:T(8,128)(2,1)S(1)}, bf16[2,192,512]{2,1,0:T(8,128)(2,1)}, u32[]{:S(2)}, u32[]{:S(2)}) collective-permute-start(bf16[2,192,512]{2,1,0:T(8,128)(2,1)S(1)} %get-tuple-element.14), channel_id=1, source_target_pairs={{4,0},{8,4},{12,8},{5,1},{9,5},{13,9},{6,2},{10,6},{14,10},{7,3},{... | collective-permute-start | bytes 1179656 | tf_op jit(solution)/shard_map/ppermute | solution.py:22
  7.8 0.1 collective-permute-start.4
  8.1 0.1 slice.17
  8.2 0.1 reshape.151
  8.3 0.7 %constant_dynamic-slice_fusion = s32[3,24]{1,0:T(4,128)S(1)} fusion(s32[6,24]{1,0:T(8,128)} %param.11, s32[]{:T(128)S(6)} %select_n.86), kind=kLoop, calls=%fused_computation.59 | loop fusion | bytes 580 | tf_op jit(solution)/shard_map/dynamic_slice | solution.py:261
  9.0 0.1 le.32
  9.1 0.1 copy.19
  9.2 0.6 gather_fusion
  9.7 0.1 copy.16
  9.8 0.1 reshape.154
  9.9 0.8 %reduce-window.8 = s32[6,1]{0,1:T(1,128)S(1)} reduce-window(s32[6,1]{0,1:T(1,128)} %bitcast.36, s32[]{:T(128)} %constant.89.clone.1), window={size=6x1 pad=5_0x0_0}, to_apply=%region_0.0 | reduce-window | flops 30 | bytes 52 | tf_op jit(solution)/shard_map/reduce-window.3
  10.7 0.1 convert_reduce_fusion
  10.9 4.0 %collective-permute-done = bf16[2,192,512]{2,1,0:T(8,128)(2,1)} collective-permute-done((bf16[2,192,512]{2,1,0:T(8,128)(2,1)S(1)}, bf16[2,192,512]{2,1,0:T(8,128)(2,1)}, u32[]{:S(2)}, u32[]{:S(2)}) %collective-permute-start) | collective-permute-done | bytes 393248 | tf_op jit(solution)/shard_map/ppermute | solution.py:22
  14.8 3.5 %collective-permute-start.2 = (bf16[2,192,512]{2,1,0:T(8,128)(2,1)}, bf16[2,192,512]{2,1,0:T(8,128)(2,1)S(1)}, u32[]{:S(2)}, u32[]{:S(2)}) collective-permute-start(bf16[2,192,512]{2,1,0:T(8,128)(2,1)} %collective-permute-done), channel_id=1, source_target_pairs={{0,4},{4,8},{8,12},{1,5},{5,9},{9,13},{2,6},{6,10},{10,14},{3,7},{... | collective-permute-start | bytes 1179656 | tf_op jit(solution)/shard_map/ppermute | solution.py:22
  18.3 0.0 collective-permute-done.1
  18.3 2.4 %collective-permute-start.3 = (bf16[2,192,512]{2,1,0:T(8,128)(2,1)}, bf16[2,192,512]{2,1,0:T(8,128)(2,1)S(1)}, u32[]{:S(2)}, u32[]{:S(2)}) collective-permute-start(bf16[2,192,512]{2,1,0:T(8,128)(2,1)} %collective-permute-done.1), channel_id=1, source_target_pairs={{4,0},{8,4},{12,8},{5,1},{9,5},{13,9},{6,2},{10,6},{14,10},{7,3},{... | collective-permute-start | bytes 1179656 | tf_op jit(solution)/shard_map/ppermute | solution.py:22
  20.7 0.1 convert_reduce_fusion.2
  20.8 0.1 broadcast_in_dim.113
  20.9 0.1 reshape.148
  21.0 0.1 broadcast_in_dim.114
  21.1 0.1 eq.45
  21.2 0.0 copy-start.5
  21.2 0.5 compare_reduce_fusion
  21.7 0.1 collective-permute-start.5
  21.7 0.5 collective-permute-start.6
  22.2 4.7 %collective-permute-done.2 = bf16[2,192,512]{2,1,0:T(8,128)(2,1)S(1)} collective-permute-done((bf16[2,192,512]{2,1,0:T(8,128)(2,1)}, bf16[2,192,512]{2,1,0:T(8,128)(2,1)S(1)}, u32[]{:S(2)}, u32[]{:S(2)}) %collective-permute-start.2) | collective-permute-done | bytes 393248 | tf_op jit(solution)/shard_map/ppermute | solution.py:22
  26.9 0.0 copy-start.1
  26.9 3.2 %collective-permute-done.3 = bf16[2,192,512]{2,1,0:T(8,128)(2,1)S(1)} collective-permute-done((bf16[2,192,512]{2,1,0:T(8,128)(2,1)}, bf16[2,192,512]{2,1,0:T(8,128)(2,1)S(1)}, u32[]{:S(2)}, u32[]{:S(2)}) %collective-permute-start.3) | collective-permute-done | bytes 393248 | tf_op jit(solution)/shard_map/ppermute | solution.py:22
  30.1 0.0 copy-start.2
  30.1 0.8 %broadcast_select_fusion = bf16[2,192,512]{2,1,0:T(8,128)(2,1)} fusion(bf16[2,192,512]{2,1,0:T(8,128)(2,1)S(1)} %collective-permute-done.3, bf16[2,192,512]{2,1,0:T(8,128)(2,1)S(1)} %collective-permute-done.2, pred[]{:T(512)S(6)} %eq.47), kind=kLoop, calls=%fused_computation.17 | loop fusion | flops 196608 | bytes 1179649 | tf_op jit(solution)/shard_map/jit(_where)/select_n | solution.py:316
  31.0 0.0 collective-permute-start.7
  31.0 0.6 convert_element_type.33.flags_ref
  31.6 0.8 %copy.18.qclip_ref = s32[192,1]{1,0:T(8,128)} copy(s32[192,1]{0,1:T(1,128)S(1)} %bitcast.33) | data formatting | bytes 1536 | tf_op jit(solution)/shard_map/broadcast_in_dim | solution.py:241
  32.3 0.0 copy-done.4
  32.4 0.8 %multiply_convert_fusion.q_ref = bf16[2,192,512]{2,1,0:T(8,128)(2,1)} fusion(bf16[1,192,512]{2,1,0:T(8,128)(2,1)S(1)} %get-tuple-element.17, bf16[1,192,512]{2,1,0:T(8,128)(2,1)S(1)} %get-tuple-element.16), kind=kLoop, calls=%fused_computation.14 | loop fusion | flops 786432 | bytes 786432 | tf_op jit(solution)/shard_map/convert_element_type | solution.py:217
  33.2 0.0 collective-permute-done.4
  33.2 0.0 collective-permute-done.5
  33.2 0.0 collective-permute-done.6
  33.2 0.0 collective-permute-done.7
  33.2 0.0 copy-done.5
  33.2 0.0 copy-done.1
  33.2 0.0 copy-done.2
  33.2 9.8 %shard_map.73 = bf16[192,512]{1,0:T(8,128)(2,1)} custom-call(s32[9]{0:T(128)} %convert_element_type.33.flags_ref, bf16[2,192,512]{2,1,0:T(8,128)(2,1)} %multiply_convert_fusion.q_ref, s32[9,3,192]{2,1,0:T(4,128)} %copy-done.5, s32[192,1]{1,0:T(8,128)} %copy.18.qclip_ref, bf16[1,2,192,512]{3,2,1,0:T(8,128)(2,1)} %get-tuple-element.15.refs_0_, ...), custom_call_target="tpu_custom_call" | custom-call | flops 1358954496 | bytes 5111808 | tf_op jit(solution)/shard_map/pallas_call | solution.py:224
  43.1 0.0 copy-start.3
  43.1 1.6 %collective-permute-start.8 = (bf16[192,512]{1,0:T(8,128)(2,1)}, bf16[192,512]{1,0:T(8,128)(2,1)S(1)}, u32[]{:S(2)}, u32[]{:S(2)}) collective-permute-start(bf16[192,512]{1,0:T(8,128)(2,1)} %shard_map.73), channel_id=1, source_target_pairs={{0,2},{2,0},{1,3},{3,1},{4,6},{6,4},{5,7},{7,5},{8,10},{10,8},{9,1... | collective-permute-start | bytes 589832 | tf_op jit(solution)/shard_map/ppermute | solution.py:26
  44.6 6.0 %collective-permute-done.8 = bf16[192,512]{1,0:T(8,128)(2,1)S(1)} collective-permute-done((bf16[192,512]{1,0:T(8,128)(2,1)}, bf16[192,512]{1,0:T(8,128)(2,1)S(1)}, u32[]{:S(2)}, u32[]{:S(2)}) %collective-permute-start.8) | collective-permute-done | bytes 196640 | tf_op jit(solution)/shard_map/ppermute | solution.py:26
  50.7 0.0 copy-done
  50.7 0.4 fusion
  51.0 0.0 copy-done.3
  51.1 0.0 copy-start.6
  51.1 0.4 convolution_add_fusion
  51.5 1.9 %collective-permute-start.10 = (f32[64,1024]{1,0:T(8,128)S(1)}, f32[64,1024]{1,0:T(8,128)S(1)}, u32[]{:S(2)}, u32[]{:S(2)}) collective-permute-start(f32[64,1024]{1,0:T(8,128)S(1)} %get-tuple-element.13), channel_id=1, source_target_pairs={{1,0},{4,1},{5,4},{8,5},{9,8},{12,9},{13,12},{3,2},{6,3},{7,6},{10... | collective-permute-start | bytes 786440 | tf_op jit(solution)/shard_map/ppermute | solution.py:22
  53.4 2.4 %collective-permute-start.9 = (f32[64,1024]{1,0:T(8,128)S(1)}, f32[64,1024]{1,0:T(8,128)S(1)}, u32[]{:S(2)}, u32[]{:S(2)}) collective-permute-start(f32[64,1024]{1,0:T(8,128)S(1)} %get-tuple-element.12), channel_id=1, source_target_pairs={{0,1},{1,4},{4,5},{5,8},{8,9},{9,12},{12,13},{2,3},{3,6},{6,7},{7,... | collective-permute-start | bytes 786440 | tf_op jit(solution)/shard_map/ppermute | solution.py:22
  55.8 0.0 copy-done.6
  55.9 1.4 %collective-permute-done.10 = f32[64,1024]{1,0:T(8,128)S(1)} collective-permute-done((f32[64,1024]{1,0:T(8,128)S(1)}, f32[64,1024]{1,0:T(8,128)S(1)}, u32[]{:S(2)}, u32[]{:S(2)}) %collective-permute-start.10) | collective-permute-done | bytes 262176 | tf_op jit(solution)/shard_map/ppermute | solution.py:22
  57.3 3.8 %collective-permute-done.9 = f32[64,1024]{1,0:T(8,128)S(1)} collective-permute-done((f32[64,1024]{1,0:T(8,128)S(1)}, f32[64,1024]{1,0:T(8,128)S(1)}, u32[]{:S(2)}, u32[]{:S(2)}) %collective-permute-start.9) | collective-permute-done | bytes 262176 | tf_op jit(solution)/shard_map/ppermute | solution.py:22
  61.1 0.4 multiply_reduce_fusion
  61.5 0.8 %multiply_convert_fusion.1 = bf16[192,512]{1,0:T(8,128)(2,1)} fusion(f32[192,1024]{1,0:T(8,128)S(1)} %get-tuple-element.9, s32[]{:T(128)S(6)} %select_n.94, f32[512]{0:T(512)S(1)} %convert_element_type.38, f32[192]{0:T(256)S(1)} %add_rsqrt_fusion), kind=kLoop, calls=%fused_computation.16 | loop fusion | flops 294912 | bytes 592644 | tf_op jit(solution)/shard_map/convert_element_type | solution.py:376
  (19 shorter events, 0.3 us)
Async XLA Ops:
  0.0 50.7 %copy-start = (bf16[1024,1024]{1,0:T(8,128)(2,1)S(1)}, bf16[1024,1024]{1,0:T(8,128)(2,1)}, u32[]{:S(2)}) copy-start(bf16[1024,1024]{1,0:T(8,128)(2,1)} %param.12) | copy-start | bytes 6291460
  0.0 32.3 %copy-start.4 = (bf16[192,512]{1,0:T(8,128)(2,1)S(1)}, bf16[192,512]{1,0:T(8,128)(2,1)}, u32[]{:S(2)}) copy-start(bf16[192,512]{1,0:T(8,128)(2,1)} %param.7) | copy-start | bytes 589828
  2.0 12.8 %collective-permute-start = (bf16[2,192,512]{2,1,0:T(8,128)(2,1)S(1)}, bf16[2,192,512]{2,1,0:T(8,128)(2,1)}, u32[]{:S(2)}, u32[]{:S(2)}) collective-permute-start(bf16[2,192,512]{2,1,0:T(8,128)(2,1)S(1)} %get-tuple-element.14), channel_id=1, source_target_pairs={{0,4},{4,8},{8,12},{1,5},{5,9},{9,13},{2,6},{6,10},{10,14},{3,7},{... | collective-permute-start | bytes 1179656 | tf_op jit(solution)/shard_map/ppermute | solution.py:22
  5.5 12.8 %collective-permute-start.1 = (bf16[2,192,512]{2,1,0:T(8,128)(2,1)S(1)}, bf16[2,192,512]{2,1,0:T(8,128)(2,1)}, u32[]{:S(2)}, u32[]{:S(2)}) collective-permute-start(bf16[2,192,512]{2,1,0:T(8,128)(2,1)S(1)} %get-tuple-element.14), channel_id=1, source_target_pairs={{4,0},{8,4},{12,8},{5,1},{9,5},{13,9},{6,2},{10,6},{14,10},{7,3},{... | collective-permute-start | bytes 1179656 | tf_op jit(solution)/shard_map/ppermute | solution.py:22
  7.8 25.4 %collective-permute-start.4 = (bf16[2,192,512]{2,1,0:T(8,128)(2,1)S(1)}, bf16[2,192,512]{2,1,0:T(8,128)(2,1)}, u32[]{:S(2)}, u32[]{:S(2)}) collective-permute-start(bf16[2,192,512]{2,1,0:T(8,128)(2,1)S(1)} %get-tuple-element.14), channel_id=1, source_target_pairs={{0,1},{1,0},{2,3},{3,2},{4,5},{5,4},{6,7},{7,6},{8,9},{9,8},{10,11... | collective-permute-start | bytes 1179656 | tf_op jit(solution)/shard_map/ppermute | solution.py:26
  14.8 12.1 %collective-permute-start.2 = (bf16[2,192,512]{2,1,0:T(8,128)(2,1)}, bf16[2,192,512]{2,1,0:T(8,128)(2,1)S(1)}, u32[]{:S(2)}, u32[]{:S(2)}) collective-permute-start(bf16[2,192,512]{2,1,0:T(8,128)(2,1)} %collective-permute-done), channel_id=1, source_target_pairs={{0,4},{4,8},{8,12},{1,5},{5,9},{9,13},{2,6},{6,10},{10,14},{3,7},{... | collective-permute-start | bytes 1179656 | tf_op jit(solution)/shard_map/ppermute | solution.py:22
  18.3 11.8 %collective-permute-start.3 = (bf16[2,192,512]{2,1,0:T(8,128)(2,1)}, bf16[2,192,512]{2,1,0:T(8,128)(2,1)S(1)}, u32[]{:S(2)}, u32[]{:S(2)}) collective-permute-start(bf16[2,192,512]{2,1,0:T(8,128)(2,1)} %collective-permute-done.1), channel_id=1, source_target_pairs={{4,0},{8,4},{12,8},{5,1},{9,5},{13,9},{6,2},{10,6},{14,10},{7,3},{... | collective-permute-start | bytes 1179656 | tf_op jit(solution)/shard_map/ppermute | solution.py:22
  21.2 12.0 %copy-start.5 = (s32[9,3,192]{2,1,0:T(4,128)}, s32[9,3,192]{2,1,0:T(4,128)S(1)}, u32[]{:S(2)}) copy-start(s32[9,3,192]{2,1,0:T(4,128)S(1)} %select_bitcast_fusion.2.code_ref) | copy-start | bytes 62212
  21.7 11.5 %collective-permute-start.5 = (bf16[2,192,512]{2,1,0:T(8,128)(2,1)}, bf16[2,192,512]{2,1,0:T(8,128)(2,1)}, u32[]{:S(2)}, u32[]{:S(2)}) collective-permute-start(bf16[2,192,512]{2,1,0:T(8,128)(2,1)} %collective-permute-done), channel_id=1, source_target_pairs={{0,1},{1,0},{2,3},{3,2},{4,5},{5,4},{6,7},{7,6},{8,9},{9,8},{10,11... | collective-permute-start | bytes 1179656 | tf_op jit(solution)/shard_map/ppermute | solution.py:26
  21.7 11.5 %collective-permute-start.6 = (bf16[2,192,512]{2,1,0:T(8,128)(2,1)}, bf16[2,192,512]{2,1,0:T(8,128)(2,1)}, u32[]{:S(2)}, u32[]{:S(2)}) collective-permute-start(bf16[2,192,512]{2,1,0:T(8,128)(2,1)} %collective-permute-done.1), channel_id=1, source_target_pairs={{0,1},{1,0},{2,3},{3,2},{4,5},{5,4},{6,7},{7,6},{8,9},{9,8},{10,11... | collective-permute-start | bytes 1179656 | tf_op jit(solution)/shard_map/ppermute | solution.py:26
  26.9 6.3 %copy-start.1 = (bf16[2,192,512]{2,1,0:T(8,128)(2,1)}, bf16[2,192,512]{2,1,0:T(8,128)(2,1)S(1)}, u32[]{:S(2)}) copy-start(bf16[2,192,512]{2,1,0:T(8,128)(2,1)S(1)} %collective-permute-done.2) | copy-start | bytes 1179652
  30.1 3.1 %copy-start.2 = (bf16[2,192,512]{2,1,0:T(8,128)(2,1)}, bf16[2,192,512]{2,1,0:T(8,128)(2,1)S(1)}, u32[]{:S(2)}) copy-start(bf16[2,192,512]{2,1,0:T(8,128)(2,1)S(1)} %collective-permute-done.3) | copy-start | bytes 1179652
  31.0 2.2 %collective-permute-start.7 = (bf16[2,192,512]{2,1,0:T(8,128)(2,1)}, bf16[2,192,512]{2,1,0:T(8,128)(2,1)}, u32[]{:S(2)}, u32[]{:S(2)}) collective-permute-start(bf16[2,192,512]{2,1,0:T(8,128)(2,1)} %broadcast_select_fusion), channel_id=1, source_target_pairs={{0,1},{1,0},{2,3},{3,2},{4,5},{5,4},{6,7},{7,6},{8,9},{9,8},{10,11... | collective-permute-start | bytes 1179656 | tf_op jit(solution)/shard_map/ppermute | solution.py:26
  43.1 8.0 %copy-start.3 = (bf16[192,512]{1,0:T(8,128)(2,1)S(1)}, bf16[192,512]{1,0:T(8,128)(2,1)}, u32[]{:S(2)}) copy-start(bf16[192,512]{1,0:T(8,128)(2,1)} %shard_map.73) | copy-start | bytes 589828
  43.1 7.6 %collective-permute-start.8 = (bf16[192,512]{1,0:T(8,128)(2,1)}, bf16[192,512]{1,0:T(8,128)(2,1)S(1)}, u32[]{:S(2)}, u32[]{:S(2)}) collective-permute-start(bf16[192,512]{1,0:T(8,128)(2,1)} %shard_map.73), channel_id=1, source_target_pairs={{0,2},{2,0},{1,3},{3,1},{4,6},{6,4},{5,7},{7,5},{8,10},{10,8},{9,1... | collective-permute-start | bytes 589832 | tf_op jit(solution)/shard_map/ppermute | solution.py:26
  51.1 4.8 %copy-start.6 = (bf16[512]{0:T(512)(128)(2,1)S(1)}, bf16[512]{0:T(512)(128)(2,1)}, u32[]{:S(2)}) copy-start(bf16[512]{0:T(512)(128)(2,1)} %param.13) | copy-start | bytes 3076
  51.5 5.8 %collective-permute-start.10 = (f32[64,1024]{1,0:T(8,128)S(1)}, f32[64,1024]{1,0:T(8,128)S(1)}, u32[]{:S(2)}, u32[]{:S(2)}) collective-permute-start(f32[64,1024]{1,0:T(8,128)S(1)} %get-tuple-element.13), channel_id=1, source_target_pairs={{1,0},{4,1},{5,4},{8,5},{9,8},{12,9},{13,12},{3,2},{6,3},{7,6},{10... | collective-permute-start | bytes 786440 | tf_op jit(solution)/shard_map/ppermute | solution.py:22
  53.4 7.7 %collective-permute-start.9 = (f32[64,1024]{1,0:T(8,128)S(1)}, f32[64,1024]{1,0:T(8,128)S(1)}, u32[]{:S(2)}, u32[]{:S(2)}) collective-permute-start(f32[64,1024]{1,0:T(8,128)S(1)} %get-tuple-element.12), channel_id=1, source_target_pairs={{0,1},{1,4},{4,5},{5,8},{8,9},{9,12},{12,13},{2,3},{3,6},{6,7},{7,... | collective-permute-start | bytes 786440 | tf_op jit(solution)/shard_map/ppermute | solution.py:22

commit v7 on v5

--- a/solution.py
+++ b/solution.py
@@ -97,15 +97,14 @@
         out_ref[...] = (acc_ref[...] / l_ref[...]).astype(out_ref.dtype)
 
 
-def whole_kernel(sources, flags_ref, q_ref, code_ref, qclip_ref, *refs):
+def whole_kernel(sources, flags_ref, q_in, code_ref, meta_ref, *refs):
     n_in = max(src for src, _ in sources) + 1
     kv_hbm = refs[:n_in]
-    out_ref, bias_ref, m_ref, l_ref, acc_ref, kv_buf, sems = refs[n_in:]
+    out_ref, bias_ref, m_ref, l_ref, acc_ref, kv_buf, sems, q_ref = refs[n_in:]
     row_count, col_count = out_ref.shape
     sub_rows = code_ref.shape[1]
     piece = row_count // sub_rows
     pair = 2 * HD
-    qclip = qclip_ref[...]
     low = lax.broadcasted_iota(jnp.int32, (row_count, pair), 1) < HD
 
     def fetch(b):
@@ -117,6 +116,15 @@
         @pl.when(flags_ref[b] > 0)
         def _():
             fetch(b).start()
+
+    lane_low = lax.broadcasted_iota(jnp.int32, (row_count, col_count), 1) % pair < HD
+    q_scaled = q_in[...].astype(jnp.float32) * (1.0 / math.sqrt(HD))
+    q_ref[0] = jnp.where(lane_low, q_scaled, 0.0).astype(q_ref.dtype)
+    q_ref[1] = jnp.where(lane_low, 0.0, q_scaled).astype(q_ref.dtype)
+    q_pos = meta_ref[0] + lax.broadcasted_iota(jnp.int32, (row_count, 1), 0)
+    qclip = jnp.zeros((row_count, 1), jnp.int32)
+    for j in range(1, meta_ref.shape[0]):
+        qclip = qclip + (q_pos >= meta_ref[j]).astype(jnp.int32)
 
     for b in range(len(sources)):
 
@@ -180,7 +188,9 @@
         out_ref[:, cols] = (acc_ref[:, cols] / den).astype(out_ref.dtype)
 
 
-def attend_chunk(state_now, q_split, query_clip, mask_rows, clip_ends, total, inputs, blocks):
+def attend_chunk(
+    state_now, q_split, query_clip, mask_rows, clip_ends, total, inputs, blocks, q_raw, meta
+):
     block_total = mask_rows.shape[1]
     sub_rows = mask_rows.shape[0]
     key_pos = jnp.stack([pos for _, _, pos in blocks])
@@ -211,10 +221,10 @@
             pltpu.VMEM((row_count, col_count), jnp.float32),
             pltpu.VMEM((len(blocks),) + inputs[0].shape[1:], inputs[0].dtype),
             pltpu.SemaphoreType.DMA((len(blocks),)),
+            pltpu.VMEM((2, row_count, col_count), jnp.bfloat16),
         ]
         aliases = {}
         extra = ()
-        q_split = (q_split.astype(jnp.float32) * (1.0 / math.sqrt(HD))).astype(jnp.bfloat16)
     else:
         out_shape = (state_shape,) * 3
         out_specs = [pl.BlockSpec(memory_space=pltpu.VMEM)] * 3
@@ -227,7 +237,8 @@
         else functools.partial(chunk_kernel, sources, has_state, final),
         out_shape=out_shape,
         in_specs=[pl.BlockSpec(memory_space=pltpu.SMEM)]
-        + [pl.BlockSpec(memory_space=pltpu.VMEM)] * 3
+        + [pl.BlockSpec(memory_space=pltpu.VMEM)] * 2
+        + [pl.BlockSpec(memory_space=pltpu.SMEM if final else pltpu.VMEM)]
         + [pl.BlockSpec(memory_space=pl.ANY if final else pltpu.VMEM)] * n_in
         + [pl.BlockSpec(memory_space=pltpu.VMEM)] * len(extra),
         out_specs=out_specs,
@@ -238,7 +249,7 @@
             transcendentals=len(blocks) * 2 * row_count**2 * col_count // HD,
             bytes_accessed=sum(x.size * x.dtype.itemsize for x in inputs) + 8 * q_split.size,
         ),
-    )(flags, q_split, code, query_clip[:, None], *inputs, *extra)
+    )(flags, q_raw if final else q_split, code, meta if final else query_clip[:, None], *inputs, *extra)
 
 
 def body(query_rows, key_rows, value_rows, clip_lengths, block_mask, out_weight, norm_gain):
@@ -282,7 +293,8 @@
                 blocks += [(len(inputs), b, block_pos(off, src)) for b, off in enumerate(offs)]
                 inputs.append(got)
         return attend_chunk(
-            state_now, q_split, query_clip, mask_rows, clip_ends, total, inputs, blocks
+            state_now, q_split, query_clip, mask_rows, clip_ends, total, inputs, blocks,
+            query_rows, jnp.concatenate([token_first[None], clip_ends]).astype(jnp.int32),
         )
 
     def to_partner(mine):

time: 61.4 us -> 64.5 us (1.050)
  Pallas kernels: 7.27 us -> 11 us
  local copies, waits for them, and re-layouts: 2.99 us -> 5.25 us
  starting transfers between devices: 19.8 us -> 18.1 us
  waiting for transfers between devices: 23.2 us -> 22 us
    pallas_call x1, Pallas kernels: 7.27 us -> 11 us  [attend_chunk(): pl.pallas_call(functools.partial(whole_kernel, sources) if final else fun...]
    unnamed x13 -> x21, local copies, waits for them, and re-layouts: 0.11 us -> 3.13 us
    ppermute x6, starting transfers between devices: 17.6 us -> 16 us  [shifted(): return lax.ppermute(x, axis, pairs)]
    ppermute x6, waiting for transfers between devices: 5.69 us -> 4.42 us  [rotated(): lax.ppermute(x, axis, [(i, (i + step) % count) for i in range(count)])]
    convert_element_type x1 -> x0, other arithmetic: 0.81 us -> none  [attend_chunk(): (q_split.astype(jnp.float32) * (1.0 / math.sqrt(HD))).astype(jnp.bfloat16)]
    broadcast_in_dim x1 -> x0, local copies, waits for them, and re-layouts: 0.76 us -> none  [attend_chunk(): query_clip[:, None]]
    concatenate x0 -> x1, other arithmetic: none -> 0.66 us  [fold(): jnp.concatenate([token_first[None], clip_ends]).astype(jnp.int32)]
  transfers between devices with their start and end apart: 12 -> 12, of which waited for: 6 -> 6; matrix products, arithmetic and copies ran while one was open for 10% -> 8% of each run, Pallas kernels for 0% -> 0%
where the time goes in v7:
time: 64.5 us; the launch traced here: 63.5 us
  waiting for transfers between devices  22 us (34%)
  starting transfers between devices  18.1 us (28%)
  Pallas kernels  11 us (17%)
  other arithmetic  6.02 us (9%)
  local copies, waits for them, and re-layouts  5.25 us (8%)
  matrix products  0.77 us (1%)
    ppermute x6, waiting for transfers between devices, shifted(): return lax.ppermute(x, axis, pairs)  17.6 us
    ppermute x6, starting transfers between devices, shifted(): return lax.ppermute(x, axis, pairs)  16 us
    pallas_call x1, Pallas kernels, attend_chunk(): pl.pallas_call(functools.partial(whole_kernel, sources) if final else fun...  11 us
    ppermute x6, waiting for transfers between devices, rotated(): lax.ppermute(x, axis, [(i, (i + step) % count) for i in range(count)])  4.42 us
    unnamed x21, local copies, waits for them, and re-layouts  3.13 us
    ppermute x6, starting transfers between devices, rotated(): lax.ppermute(x, axis, [(i, (i + step) % count) for i in range(count)])  2.12 us
    another operation x1, other arithmetic, body(): own = jnp.stack([key_rows, value_rows])  1.96 us
  transfers between devices with their start and end apart: 12, of which 6 were waited for; matrix products, arithmetic and copies ran while one was open for 8% of the time, Pallas kernels for 0%

profile of v7, /device:TPU:20, one launch (start us, length us, event | category | flops | bytes accessed | tf_op | source)
XLA Modules:
  0.0 63.5 jit_solution(12529922790472129222)
XLA Ops:
  0.0 0.0 copy-start
  0.0 2.0 %pad_maximum_fusion.2 = (bf16[2,192,512]{2,1,0:T(8,128)(2,1)S(1)}, bf16[1,2,192,512]{3,2,1,0:T(8,128)(2,1)}) fusion(bf16[1,192,512]{2,1,0:T(8,128)(2,1)} %bitcast.26, bf16[1,192,512]{2,1,0:T(8,128)(2,1)} %bitcast.27), kind=kLoop, calls=%fused_computation.14 | loop fusion | flops 196608 | bytes 1179648 | tf_op jit(solution)/shard_map/stack | solution.py:314
  2.0 3.5 %collective-permute-start = (bf16[2,192,512]{2,1,0:T(8,128)(2,1)S(1)}, bf16[2,192,512]{2,1,0:T(8,128)(2,1)S(1)}, u32[]{:S(2)}, u32[]{:S(2)}) collective-permute-start(bf16[2,192,512]{2,1,0:T(8,128)(2,1)S(1)} %get-tuple-element.14), channel_id=1, source_target_pairs={{0,4},{4,8},{8,12},{1,5},{5,9},{9,13},{2,6},{6,10},{10,14},{3,7},{... | collective-permute-start | bytes 1179656 | tf_op jit(solution)/shard_map/ppermute | solution.py:22
  5.4 2.4 %collective-permute-start.1 = (bf16[2,192,512]{2,1,0:T(8,128)(2,1)S(1)}, bf16[2,192,512]{2,1,0:T(8,128)(2,1)S(1)}, u32[]{:S(2)}, u32[]{:S(2)}) collective-permute-start(bf16[2,192,512]{2,1,0:T(8,128)(2,1)S(1)} %get-tuple-element.14), channel_id=1, source_target_pairs={{4,0},{8,4},{12,8},{5,1},{9,5},{13,9},{6,2},{10,6},{14,10},{7,3},{... | collective-permute-start | bytes 1179656 | tf_op jit(solution)/shard_map/ppermute | solution.py:22
  7.8 0.1 collective-permute-start.4
  8.0 0.1 stack.8
  8.1 0.1 slice.17
  8.2 0.7 %constant_dynamic-slice_fusion = s32[3,24]{1,0:T(4,128)S(1)} fusion(s32[6,24]{1,0:T(8,128)} %param.11, s32[]{:T(128)S(6)} %select_n.52), kind=kLoop, calls=%fused_computation.49 | loop fusion | bytes 580 | tf_op jit(solution)/shard_map/dynamic_slice | solution.py:272
  8.9 0.1 le.32
  8.9 0.1 copy.17
  9.0 0.1 reshape.137
  9.1 0.6 gather_fusion
  9.7 0.1 copy.15
  9.8 0.1 reshape.140
  9.9 0.8 %reduce-window.8 = s32[6,1]{0,1:T(1,128)S(1)} reduce-window(s32[6,1]{0,1:T(1,128)} %bitcast.37, s32[]{:T(128)} %constant.75.clone.1), window={size=6x1 pad=5_0x0_0}, to_apply=%region_0.0 | reduce-window | flops 30 | bytes 52 | tf_op jit(solution)/shard_map/reduce-window.3
  10.7 4.0 %collective-permute-done = bf16[2,192,512]{2,1,0:T(8,128)(2,1)S(1)} collective-permute-done((bf16[2,192,512]{2,1,0:T(8,128)(2,1)S(1)}, bf16[2,192,512]{2,1,0:T(8,128)(2,1)S(1)}, u32[]{:S(2)}, u32[]{:S(2)}) %collective-permute-start) | collective-permute-done | bytes 393248 | tf_op jit(solution)/shard_map/ppermute | solution.py:22
  14.7 3.5 %collective-permute-start.2 = (bf16[2,192,512]{2,1,0:T(8,128)(2,1)S(1)}, bf16[2,192,512]{2,1,0:T(8,128)(2,1)}, u32[]{:S(2)}, u32[]{:S(2)}) collective-permute-start(bf16[2,192,512]{2,1,0:T(8,128)(2,1)S(1)} %collective-permute-done), channel_id=1, source_target_pairs={{0,4},{4,8},{8,12},{1,5},{5,9},{9,13},{2,6},{6,10},{10,14},{3,7},{... | collective-permute-start | bytes 1179656 | tf_op jit(solution)/shard_map/ppermute | solution.py:22
  18.2 0.0 collective-permute-done.1
  18.2 0.0 copy-start.5
  18.2 2.4 %collective-permute-start.3 = (bf16[2,192,512]{2,1,0:T(8,128)(2,1)S(1)}, bf16[2,192,512]{2,1,0:T(8,128)(2,1)}, u32[]{:S(2)}, u32[]{:S(2)}) collective-permute-start(bf16[2,192,512]{2,1,0:T(8,128)(2,1)S(1)} %collective-permute-done.1), channel_id=1, source_target_pairs={{4,0},{8,4},{12,8},{5,1},{9,5},{13,9},{6,2},{10,6},{14,10},{7,3},{... | collective-permute-start | bytes 1179656 | tf_op jit(solution)/shard_map/ppermute | solution.py:22
  20.6 0.1 convert_reduce_fusion
  20.7 0.1 broadcast_in_dim.98
  20.8 0.1 reshape.134
  20.9 0.1 broadcast_in_dim.99
  21.0 0.1 convert_reduce_fusion.2
  21.1 0.1 eq.40
  21.1 0.0 collective-permute-start.5
  21.2 0.5 collective-permute-start.6
  21.7 5.0 %collective-permute-done.2 = bf16[2,192,512]{2,1,0:T(8,128)(2,1)} collective-permute-done((bf16[2,192,512]{2,1,0:T(8,128)(2,1)S(1)}, bf16[2,192,512]{2,1,0:T(8,128)(2,1)}, u32[]{:S(2)}, u32[]{:S(2)}) %collective-permute-start.2) | collective-permute-done | bytes 393248 | tf_op jit(solution)/shard_map/ppermute | solution.py:22
  26.7 0.0 collective-permute-start.7
  26.7 3.2 %collective-permute-done.3 = bf16[2,192,512]{2,1,0:T(8,128)(2,1)} collective-permute-done((bf16[2,192,512]{2,1,0:T(8,128)(2,1)S(1)}, bf16[2,192,512]{2,1,0:T(8,128)(2,1)}, u32[]{:S(2)}, u32[]{:S(2)}) %collective-permute-start.3) | collective-permute-done | bytes 393248 | tf_op jit(solution)/shard_map/ppermute | solution.py:22
  29.9 0.0 collective-permute-start.8
  29.9 0.0 copy-start.2
  29.9 0.6 compare_reduce_fusion
  30.5 0.6 convert_element_type.24.flags_ref
  31.1 0.7 %pad_add_fusion.meta_ref = s32[7]{0:T(128)} fusion(s32[6]{0:T(128)S(1)} %bitcast.30, s32[1]{0:T(128)} %bitcast.4), kind=kLoop, calls=%fused_computation.52 | loop fusion | flops 7 | bytes 56 | tf_op jit(solution)/shard_map/concatenate | solution.py:297
  31.7 0.0 collective-permute-done.4
  31.7 0.0 collective-permute-done.5
  31.7 0.0 collective-permute-done.6
  31.7 0.7 %copy-done.6 = bf16[2,192,512]{2,1,0:T(8,128)(2,1)} copy-done((bf16[2,192,512]{2,1,0:T(8,128)(2,1)}, bf16[2,192,512]{2,1,0:T(8,128)(2,1)S(1)}, u32[]{:S(2)}) %copy-start.6) | copy-done | bytes 393240
  32.5 0.0 collective-permute-done.7
  32.5 0.8 %copy-done.7 = bf16[2,192,512]{2,1,0:T(8,128)(2,1)} copy-done((bf16[2,192,512]{2,1,0:T(8,128)(2,1)}, bf16[2,192,512]{2,1,0:T(8,128)(2,1)S(1)}, u32[]{:S(2)}) %copy-start.7) | copy-done | bytes 393240
  33.2 0.0 collective-permute-done.8
  33.3 0.8 %copy-done.8 = bf16[2,192,512]{2,1,0:T(8,128)(2,1)} copy-done((bf16[2,192,512]{2,1,0:T(8,128)(2,1)}, bf16[2,192,512]{2,1,0:T(8,128)(2,1)S(1)}, u32[]{:S(2)}) %copy-start.8) | copy-done | bytes 393240
  34.0 0.8 %copy-done.9 = bf16[2,192,512]{2,1,0:T(8,128)(2,1)} copy-done((bf16[2,192,512]{2,1,0:T(8,128)(2,1)}, bf16[2,192,512]{2,1,0:T(8,128)(2,1)S(1)}, u32[]{:S(2)}) %copy-start.9) | copy-done | bytes 393240
  34.8 0.0 copy-done.4
  34.8 0.0 copy-done.5
  34.8 0.0 copy-done.2
  34.8 11.0 %shard_map.73 = bf16[192,512]{1,0:T(8,128)(2,1)} custom-call(s32[10]{0:T(128)} %convert_element_type.24.flags_ref, bf16[192,512]{1,0:T(8,128)(2,1)} %q_in.1, s32[10,3,192]{2,1,0:T(4,128)} %copy-done.2, s32[7]{0:T(128)} %pad_add_fusion.meta_ref, bf16[1,2,192,512]{3,2,1,0:T(8,128)(2,1)} %get-tuple-element.15.refs_0_, bf16[1,2,192,512]{3,2,1,0:T(8,128)(2,1)} %bitcast.31, ...), custom_call_target="tpu_custom_call" | custom-call | flops 1509949440 | bytes 5505024 | tf_op jit(solution)/shard_map/pallas_call | solution.py:234
  45.8 0.0 copy-start.1
  45.8 1.5 %collective-permute-start.9 = (bf16[192,512]{1,0:T(8,128)(2,1)}, bf16[192,512]{1,0:T(8,128)(2,1)S(1)}, u32[]{:S(2)}, u32[]{:S(2)}) collective-permute-start(bf16[192,512]{1,0:T(8,128)(2,1)} %shard_map.73), channel_id=1, source_target_pairs={{0,2},{2,0},{1,3},{3,1},{4,6},{6,4},{5,7},{7,5},{8,10},{10,8},{9,1... | collective-permute-start | bytes 589832 | tf_op jit(solution)/shard_map/ppermute | solution.py:26
  47.4 4.4 %collective-permute-done.9 = bf16[192,512]{1,0:T(8,128)(2,1)S(1)} collective-permute-done((bf16[192,512]{1,0:T(8,128)(2,1)}, bf16[192,512]{1,0:T(8,128)(2,1)S(1)}, u32[]{:S(2)}, u32[]{:S(2)}) %collective-permute-start.9) | collective-permute-done | bytes 196640 | tf_op jit(solution)/shard_map/ppermute | solution.py:26
  51.8 0.0 copy-done
  51.8 0.4 fusion
  52.2 0.0 copy-done.1
  52.2 0.0 copy-start.3
  52.2 0.4 convolution_add_fusion
  52.6 2.0 %collective-permute-start.11 = (f32[64,1024]{1,0:T(8,128)S(1)}, f32[64,1024]{1,0:T(8,128)S(1)}, u32[]{:S(2)}, u32[]{:S(2)}) collective-permute-start(f32[64,1024]{1,0:T(8,128)S(1)} %get-tuple-element.13), channel_id=1, source_target_pairs={{1,0},{4,1},{5,4},{8,5},{9,8},{12,9},{13,12},{3,2},{6,3},{7,6},{10... | collective-permute-start | bytes 786440 | tf_op jit(solution)/shard_map/ppermute | solution.py:22
  54.7 2.3 %collective-permute-start.10 = (f32[64,1024]{1,0:T(8,128)S(1)}, f32[64,1024]{1,0:T(8,128)S(1)}, u32[]{:S(2)}, u32[]{:S(2)}) collective-permute-start(f32[64,1024]{1,0:T(8,128)S(1)} %get-tuple-element.12), channel_id=1, source_target_pairs={{0,1},{1,4},{4,5},{5,8},{8,9},{9,12},{12,13},{2,3},{3,6},{6,7},{7,... | collective-permute-start | bytes 786440 | tf_op jit(solution)/shard_map/ppermute | solution.py:22
  57.0 0.0 copy-done.3
  57.0 1.5 %collective-permute-done.11 = f32[64,1024]{1,0:T(8,128)S(1)} collective-permute-done((f32[64,1024]{1,0:T(8,128)S(1)}, f32[64,1024]{1,0:T(8,128)S(1)}, u32[]{:S(2)}, u32[]{:S(2)}) %collective-permute-start.11) | collective-permute-done | bytes 262176 | tf_op jit(solution)/shard_map/ppermute | solution.py:22
  58.5 3.8 %collective-permute-done.10 = f32[64,1024]{1,0:T(8,128)S(1)} collective-permute-done((f32[64,1024]{1,0:T(8,128)S(1)}, f32[64,1024]{1,0:T(8,128)S(1)}, u32[]{:S(2)}, u32[]{:S(2)}) %collective-permute-start.10) | collective-permute-done | bytes 262176 | tf_op jit(solution)/shard_map/ppermute | solution.py:22
  62.3 0.3 multiply_reduce_fusion
  62.7 0.8 %multiply_convert_fusion = bf16[192,512]{1,0:T(8,128)(2,1)} fusion(f32[192,1024]{1,0:T(8,128)S(1)} %get-tuple-element.9, s32[]{:T(128)S(6)} %select_n.55, f32[512]{0:T(512)S(1)} %convert_element_type.27, f32[192]{0:T(256)S(1)} %add_rsqrt_fusion), kind=kLoop, calls=%fused_computation.15 | loop fusion | flops 294912 | bytes 592644 | tf_op jit(solution)/shard_map/convert_element_type | solution.py:382
  (21 shorter events, 0.2 us)
Async XLA Ops:
  0.0 51.8 %copy-start = (bf16[1024,1024]{1,0:T(8,128)(2,1)S(1)}, bf16[1024,1024]{1,0:T(8,128)(2,1)}, u32[]{:S(2)}) copy-start(bf16[1024,1024]{1,0:T(8,128)(2,1)} %param.12) | copy-start | bytes 6291460
  2.0 12.7 %collective-permute-start = (bf16[2,192,512]{2,1,0:T(8,128)(2,1)S(1)}, bf16[2,192,512]{2,1,0:T(8,128)(2,1)S(1)}, u32[]{:S(2)}, u32[]{:S(2)}) collective-permute-start(bf16[2,192,512]{2,1,0:T(8,128)(2,1)S(1)} %get-tuple-element.14), channel_id=1, source_target_pairs={{0,4},{4,8},{8,12},{1,5},{5,9},{9,13},{2,6},{6,10},{10,14},{3,7},{... | collective-permute-start | bytes 1179656 | tf_op jit(solution)/shard_map/ppermute | solution.py:22
  5.4 12.7 %collective-permute-start.1 = (bf16[2,192,512]{2,1,0:T(8,128)(2,1)S(1)}, bf16[2,192,512]{2,1,0:T(8,128)(2,1)S(1)}, u32[]{:S(2)}, u32[]{:S(2)}) collective-permute-start(bf16[2,192,512]{2,1,0:T(8,128)(2,1)S(1)} %get-tuple-element.14), channel_id=1, source_target_pairs={{4,0},{8,4},{12,8},{5,1},{9,5},{13,9},{6,2},{10,6},{14,10},{7,3},{... | collective-permute-start | bytes 1179656 | tf_op jit(solution)/shard_map/ppermute | solution.py:22
  7.8 23.9 %collective-permute-start.4 = (bf16[2,192,512]{2,1,0:T(8,128)(2,1)S(1)}, bf16[2,192,512]{2,1,0:T(8,128)(2,1)}, u32[]{:S(2)}, u32[]{:S(2)}) collective-permute-start(bf16[2,192,512]{2,1,0:T(8,128)(2,1)S(1)} %get-tuple-element.14), channel_id=1, source_target_pairs={{0,1},{1,0},{2,3},{3,2},{4,5},{5,4},{6,7},{7,6},{8,9},{9,8},{10,11... | collective-permute-start | bytes 1179656 | tf_op jit(solution)/shard_map/ppermute | solution.py:26
  14.7 20.1 %copy-start.4 = (bf16[2,192,512]{2,1,0:T(8,128)(2,1)}, bf16[2,192,512]{2,1,0:T(8,128)(2,1)S(1)}, u32[]{:S(2)}) copy-start(bf16[2,192,512]{2,1,0:T(8,128)(2,1)S(1)} %collective-permute-done) | copy-start | bytes 1179652
  14.7 12.0 %collective-permute-start.2 = (bf16[2,192,512]{2,1,0:T(8,128)(2,1)S(1)}, bf16[2,192,512]{2,1,0:T(8,128)(2,1)}, u32[]{:S(2)}, u32[]{:S(2)}) collective-permute-start(bf16[2,192,512]{2,1,0:T(8,128)(2,1)S(1)} %collective-permute-done), channel_id=1, source_target_pairs={{0,4},{4,8},{8,12},{1,5},{5,9},{9,13},{2,6},{6,10},{10,14},{3,7},{... | collective-permute-start | bytes 1179656 | tf_op jit(solution)/shard_map/ppermute | solution.py:22
  18.2 16.6 %copy-start.5 = (bf16[2,192,512]{2,1,0:T(8,128)(2,1)}, bf16[2,192,512]{2,1,0:T(8,128)(2,1)S(1)}, u32[]{:S(2)}) copy-start(bf16[2,192,512]{2,1,0:T(8,128)(2,1)S(1)} %collective-permute-done.1) | copy-start | bytes 1179652
  18.2 11.7 %collective-permute-start.3 = (bf16[2,192,512]{2,1,0:T(8,128)(2,1)S(1)}, bf16[2,192,512]{2,1,0:T(8,128)(2,1)}, u32[]{:S(2)}, u32[]{:S(2)}) collective-permute-start(bf16[2,192,512]{2,1,0:T(8,128)(2,1)S(1)} %collective-permute-done.1), channel_id=1, source_target_pairs={{4,0},{8,4},{12,8},{5,1},{9,5},{13,9},{6,2},{10,6},{14,10},{7,3},{... | collective-permute-start | bytes 1179656 | tf_op jit(solution)/shard_map/ppermute | solution.py:22
  21.1 10.6 %collective-permute-start.5 = (bf16[2,192,512]{2,1,0:T(8,128)(2,1)S(1)}, bf16[2,192,512]{2,1,0:T(8,128)(2,1)S(1)}, u32[]{:S(2)}, u32[]{:S(2)}) collective-permute-start(bf16[2,192,512]{2,1,0:T(8,128)(2,1)S(1)} %collective-permute-done), channel_id=1, source_target_pairs={{0,1},{1,0},{2,3},{3,2},{4,5},{5,4},{6,7},{7,6},{8,9},{9,8},{10,11... | collective-permute-start | bytes 1179656 | tf_op jit(solution)/shard_map/ppermute | solution.py:26
  21.2 10.6 %collective-permute-start.6 = (bf16[2,192,512]{2,1,0:T(8,128)(2,1)S(1)}, bf16[2,192,512]{2,1,0:T(8,128)(2,1)S(1)}, u32[]{:S(2)}, u32[]{:S(2)}) collective-permute-start(bf16[2,192,512]{2,1,0:T(8,128)(2,1)S(1)} %collective-permute-done.1), channel_id=1, source_target_pairs={{0,1},{1,0},{2,3},{3,2},{4,5},{5,4},{6,7},{7,6},{8,9},{9,8},{10,11... | collective-permute-start | bytes 1179656 | tf_op jit(solution)/shard_map/ppermute | solution.py:26
  26.7 5.8 %collective-permute-start.7 = (bf16[2,192,512]{2,1,0:T(8,128)(2,1)}, bf16[2,192,512]{2,1,0:T(8,128)(2,1)S(1)}, u32[]{:S(2)}, u32[]{:S(2)}) collective-permute-start(bf16[2,192,512]{2,1,0:T(8,128)(2,1)} %collective-permute-done.2), channel_id=1, source_target_pairs={{0,1},{1,0},{2,3},{3,2},{4,5},{5,4},{6,7},{7,6},{8,9},{9,8},{10,11... | collective-permute-start | bytes 1179656 | tf_op jit(solution)/shard_map/ppermute | solution.py:26
  29.9 3.3 %collective-permute-start.8 = (bf16[2,192,512]{2,1,0:T(8,128)(2,1)}, bf16[2,192,512]{2,1,0:T(8,128)(2,1)S(1)}, u32[]{:S(2)}, u32[]{:S(2)}) collective-permute-start(bf16[2,192,512]{2,1,0:T(8,128)(2,1)} %collective-permute-done.3), channel_id=1, source_target_pairs={{0,1},{1,0},{2,3},{3,2},{4,5},{5,4},{6,7},{7,6},{8,9},{9,8},{10,11... | collective-permute-start | bytes 1179656 | tf_op jit(solution)/shard_map/ppermute | solution.py:26
  29.9 4.8 %copy-start.2 = (s32[10,3,192]{2,1,0:T(4,128)}, s32[10,3,192]{2,1,0:T(4,128)S(1)}, u32[]{:S(2)}) copy-start(s32[10,3,192]{2,1,0:T(4,128)S(1)} %select_bitcast_fusion.code_ref) | copy-start | bytes 69124
  31.7 0.8 %copy-start.6 = (bf16[2,192,512]{2,1,0:T(8,128)(2,1)}, bf16[2,192,512]{2,1,0:T(8,128)(2,1)S(1)}, u32[]{:S(2)}) copy-start(bf16[2,192,512]{2,1,0:T(8,128)(2,1)S(1)} %collective-permute-done.5) | copy-start | bytes 1179652
  32.5 0.8 %copy-start.7 = (bf16[2,192,512]{2,1,0:T(8,128)(2,1)}, bf16[2,192,512]{2,1,0:T(8,128)(2,1)S(1)}, u32[]{:S(2)}) copy-start(bf16[2,192,512]{2,1,0:T(8,128)(2,1)S(1)} %collective-permute-done.6) | copy-start | bytes 1179652
  33.2 0.8 %copy-start.8 = (bf16[2,192,512]{2,1,0:T(8,128)(2,1)}, bf16[2,192,512]{2,1,0:T(8,128)(2,1)S(1)}, u32[]{:S(2)}) copy-start(bf16[2,192,512]{2,1,0:T(8,128)(2,1)S(1)} %collective-permute-done.7) | copy-start | bytes 1179652
  34.0 0.8 %copy-start.9 = (bf16[2,192,512]{2,1,0:T(8,128)(2,1)}, bf16[2,192,512]{2,1,0:T(8,128)(2,1)S(1)}, u32[]{:S(2)}) copy-start(bf16[2,192,512]{2,1,0:T(8,128)(2,1)S(1)} %collective-permute-done.8) | copy-start | bytes 1179652
  45.8 6.3 %copy-start.1 = (bf16[192,512]{1,0:T(8,128)(2,1)S(1)}, bf16[192,512]{1,0:T(8,128)(2,1)}, u32[]{:S(2)}) copy-start(bf16[192,512]{1,0:T(8,128)(2,1)} %shard_map.73) | copy-start | bytes 589828
  45.8 5.9 %collective-permute-start.9 = (bf16[192,512]{1,0:T(8,128)(2,1)}, bf16[192,512]{1,0:T(8,128)(2,1)S(1)}, u32[]{:S(2)}, u32[]{:S(2)}) collective-permute-start(bf16[192,512]{1,0:T(8,128)(2,1)} %shard_map.73), channel_id=1, source_target_pairs={{0,2},{2,0},{1,3},{3,1},{4,6},{6,4},{5,7},{7,5},{8,10},{10,8},{9,1... | collective-permute-start | bytes 589832 | tf_op jit(solution)/shard_map/ppermute | solution.py:26
  52.2 4.8 %copy-start.3 = (bf16[512]{0:T(512)(128)(2,1)S(1)}, bf16[512]{0:T(512)(128)(2,1)}, u32[]{:S(2)}) copy-start(bf16[512]{0:T(512)(128)(2,1)} %param.13) | copy-start | bytes 3076
  52.6 5.9 %collective-permute-start.11 = (f32[64,1024]{1,0:T(8,128)S(1)}, f32[64,1024]{1,0:T(8,128)S(1)}, u32[]{:S(2)}, u32[]{:S(2)}) collective-permute-start(f32[64,1024]{1,0:T(8,128)S(1)} %get-tuple-element.13), channel_id=1, source_target_pairs={{1,0},{4,1},{5,4},{8,5},{9,8},{12,9},{13,12},{3,2},{6,3},{7,6},{10... | collective-permute-start | bytes 786440 | tf_op jit(solution)/shard_map/ppermute | solution.py:22
  54.7 7.7 %collective-permute-start.10 = (f32[64,1024]{1,0:T(8,128)S(1)}, f32[64,1024]{1,0:T(8,128)S(1)}, u32[]{:S(2)}, u32[]{:S(2)}) collective-permute-start(f32[64,1024]{1,0:T(8,128)S(1)} %get-tuple-element.12), channel_id=1, source_target_pairs={{0,1},{1,4},{4,5},{5,8},{8,9},{9,12},{12,13},{2,3},{3,6},{6,7},{7,... | collective-permute-start | bytes 786440 | tf_op jit(solution)/shard_map/ppermute | solution.py:22

commit v8 on v5

--- a/solution.py
+++ b/solution.py
@@ -100,7 +100,8 @@
 def whole_kernel(sources, flags_ref, q_ref, code_ref, qclip_ref, *refs):
     n_in = max(src for src, _ in sources) + 1
     kv_hbm = refs[:n_in]
-    out_ref, bias_ref, m_ref, l_ref, acc_ref, kv_buf, sems = refs[n_in:]
+    k_own, v_own = refs[n_in : n_in + 2]
+    out_ref, bias_ref, m_ref, l_ref, acc_ref, kv_buf, sems = refs[n_in + 2 :]
     row_count, col_count = out_ref.shape
     sub_rows = code_ref.shape[1]
     piece = row_count // sub_rows
@@ -110,13 +111,19 @@
 
     def fetch(b):
         src, idx = sources[b]
-        return pltpu.make_async_copy(kv_hbm[src].at[idx], kv_buf.at[b], sems.at[b])
+        if src < 0:
+            return [
+                pltpu.make_async_copy(k_own, kv_buf.at[b, 0], sems.at[b, 0]),
+                pltpu.make_async_copy(v_own, kv_buf.at[b, 1], sems.at[b, 1]),
+            ]
+        return [pltpu.make_async_copy(kv_hbm[src].at[idx], kv_buf.at[b], sems.at[b, 0])]
 
     for b in range(len(sources)):
 
         @pl.when(flags_ref[b] > 0)
         def _():
-            fetch(b).start()
+            for copy in fetch(b):
+                copy.start()
 
     for b in range(len(sources)):
 
@@ -151,7 +158,8 @@
 
         @pl.when(flags_ref[b] > 0)
         def _():
-            fetch(b).wait()
+            for copy in fetch(b):
+                copy.wait()
             for hp in range(col_count // pair):
                 for e in range(2):
                     h = 2 * hp + e
@@ -180,7 +188,9 @@
         out_ref[:, cols] = (acc_ref[:, cols] / den).astype(out_ref.dtype)
 
 
-def attend_chunk(state_now, q_split, query_clip, mask_rows, clip_ends, total, inputs, blocks):
+def attend_chunk(
+    state_now, q_split, query_clip, mask_rows, clip_ends, total, inputs, blocks, own_raw
+):
     block_total = mask_rows.shape[1]
     sub_rows = mask_rows.shape[0]
     key_pos = jnp.stack([pos for _, _, pos in blocks])
@@ -210,10 +220,10 @@
             pltpu.VMEM((head_count, row_count, 1), jnp.float32),
             pltpu.VMEM((row_count, col_count), jnp.float32),
             pltpu.VMEM((len(blocks),) + inputs[0].shape[1:], inputs[0].dtype),
-            pltpu.SemaphoreType.DMA((len(blocks),)),
+            pltpu.SemaphoreType.DMA((len(blocks), 2)),
         ]
         aliases = {}
-        extra = ()
+        extra = own_raw
         q_split = (q_split.astype(jnp.float32) * (1.0 / math.sqrt(HD))).astype(jnp.bfloat16)
     else:
         out_shape = (state_shape,) * 3
@@ -228,8 +238,7 @@
         out_shape=out_shape,
         in_specs=[pl.BlockSpec(memory_space=pltpu.SMEM)]
         + [pl.BlockSpec(memory_space=pltpu.VMEM)] * 3
-        + [pl.BlockSpec(memory_space=pl.ANY if final else pltpu.VMEM)] * n_in
-        + [pl.BlockSpec(memory_space=pltpu.VMEM)] * len(extra),
+        + [pl.BlockSpec(memory_space=pl.ANY if final else pltpu.VMEM)] * (n_in + len(extra)),
         out_specs=out_specs,
         scratch_shapes=scratch,
         input_output_aliases=aliases,
@@ -271,8 +280,13 @@
     ).astype(jnp.bfloat16)
 
     def fold(state_now, mine, theirs):
-        inputs = [kv[None] for kv, _ in mine]
-        blocks = [(n, 0, block_pos(off, sub_i)) for n, (_, off) in enumerate(mine)]
+        if state_now is None:
+            inputs = [kv[None] for kv, _ in mine[1:]]
+            blocks = [(-1, 0, block_pos(mine[0][1], sub_i))]
+            blocks += [(n, 0, block_pos(off, sub_i)) for n, (_, off) in enumerate(mine[1:])]
+        else:
+            inputs = [kv[None] for kv, _ in mine]
+            blocks = [(n, 0, block_pos(off, sub_i)) for n, (_, off) in enumerate(mine)]
         for got, offs, src in theirs:
             if isinstance(got, list):
                 for piece, off in zip(got, offs):
@@ -282,7 +296,8 @@
                 blocks += [(len(inputs), b, block_pos(off, src)) for b, off in enumerate(offs)]
                 inputs.append(got)
         return attend_chunk(
-            state_now, q_split, query_clip, mask_rows, clip_ends, total, inputs, blocks
+            state_now, q_split, query_clip, mask_rows, clip_ends, total, inputs, blocks,
+            (key_rows, value_rows),
         )
 
     def to_partner(mine):

time: 61.4 us -> 62.2 us (1.013)
  Pallas kernels: 7.27 us -> 9.95 us
  starting transfers between devices: 19.8 us -> 18.3 us
  waiting for transfers between devices: 23.2 us -> 22.5 us
    pallas_call x1, Pallas kernels: 7.27 us -> 9.95 us  [attend_chunk(): pl.pallas_call(functools.partial(whole_kernel, sources) if final else fun...]
    ppermute x6, starting transfers between devices: 17.6 us -> 16.1 us  [shifted(): return lax.ppermute(x, axis, pairs)]
    another operation x1, other arithmetic: 0.03 us -> 0.96 us  [body(): jnp.stack([jnp.where(lane < HD, query_rows, 0), jnp.where(lane >= HD, que...]
    another operation x1, other arithmetic: 1.98 us -> 1.21 us  [body(): own = jnp.stack([key_rows, value_rows])]
    ppermute x6, waiting for transfers between devices: 17.5 us -> 16.9 us  [shifted(): return lax.ppermute(x, axis, pairs)]
  transfers between devices with their start and end apart: 12 -> 12, of which waited for: 6 -> 6; matrix products, arithmetic and copies ran while one was open for 10% -> 11% of each run, Pallas kernels for 0% -> 0%
where the time goes in v8:
time: 62.2 us; the launch traced here: 61.3 us
  waiting for transfers between devices  22.5 us (36%)
  starting transfers between devices  18.3 us (29%)
  Pallas kernels  9.95 us (16%)
  other arithmetic  6.34 us (10%)
  local copies, waits for them, and re-layouts  2.98 us (5%)
  matrix products  0.77 us (1%)
    ppermute x6, waiting for transfers between devices, shifted(): return lax.ppermute(x, axis, pairs)  16.9 us
    ppermute x6, starting transfers between devices, shifted(): return lax.ppermute(x, axis, pairs)  16.1 us
    pallas_call x1, Pallas kernels, attend_chunk(): pl.pallas_call(functools.partial(whole_kernel, sources) if final else fun...  9.95 us
    ppermute x6, waiting for transfers between devices, rotated(): lax.ppermute(x, axis, [(i, (i + step) % count) for i in range(count)])  5.69 us
    ppermute x6, starting transfers between devices, rotated(): lax.ppermute(x, axis, [(i, (i + step) % count) for i in range(count)])  2.21 us
  transfers between devices with their start and end apart: 12, of which 6 were waited for; matrix products, arithmetic and copies ran while one was open for 11% of the time, Pallas kernels for 0%

profile of v8, /device:TPU:20, one launch (start us, length us, event | category | flops | bytes accessed | tf_op | source)
XLA Modules:
  0.0 61.3 jit_solution(11032431999741647107)
XLA Ops:
  0.0 0.0 copy-start
  0.0 1.2 %pad_maximum_fusion.2 = bf16[2,192,512]{2,1,0:T(8,128)(2,1)S(1)} fusion(bf16[1,192,512]{2,1,0:T(8,128)(2,1)} %bitcast.28, bf16[1,192,512]{2,1,0:T(8,128)(2,1)} %bitcast.29), kind=kLoop, calls=%fused_computation.15 | loop fusion | flops 196608 | bytes 786432 | tf_op jit(solution)/shard_map/stack | solution.py:317
  1.2 3.5 %collective-permute-start = (bf16[2,192,512]{2,1,0:T(8,128)(2,1)S(1)}, bf16[2,192,512]{2,1,0:T(8,128)(2,1)S(1)}, u32[]{:S(2)}, u32[]{:S(2)}) collective-permute-start(bf16[2,192,512]{2,1,0:T(8,128)(2,1)S(1)} %pad_maximum_fusion.2), channel_id=1, source_target_pairs={{0,4},{4,8},{8,12},{1,5},{5,9},{9,13},{2,6},{6,10},{10,14},{3,7},{... | collective-permute-start | bytes 1179656 | tf_op jit(solution)/shard_map/ppermute | solution.py:22
  4.7 2.4 %collective-permute-start.1 = (bf16[2,192,512]{2,1,0:T(8,128)(2,1)S(1)}, bf16[2,192,512]{2,1,0:T(8,128)(2,1)S(1)}, u32[]{:S(2)}, u32[]{:S(2)}) collective-permute-start(bf16[2,192,512]{2,1,0:T(8,128)(2,1)S(1)} %pad_maximum_fusion.2), channel_id=1, source_target_pairs={{4,0},{8,4},{12,8},{5,1},{9,5},{13,9},{6,2},{10,6},{14,10},{7,3},{... | collective-permute-start | bytes 1179656 | tf_op jit(solution)/shard_map/ppermute | solution.py:22
  7.1 0.1 collective-permute-start.4
  7.3 0.1 stack.14
  7.3 0.1 slice.17
  7.5 0.1 reshape.158
  7.5 0.7 %constant_dynamic-slice_fusion = s32[3,24]{1,0:T(4,128)S(1)} fusion(s32[6,24]{1,0:T(8,128)} %param.11, s32[]{:T(128)S(6)} %select_n.75), kind=kLoop, calls=%fused_computation.59 | loop fusion | bytes 580 | tf_op jit(solution)/shard_map/dynamic_slice | solution.py:270
  8.2 0.1 le.32
  8.3 0.1 copy.19
  8.4 0.6 gather_fusion
  9.0 0.1 copy.16
  9.1 0.1 reshape.161
  9.1 0.8 %reduce-window.8 = s32[6,1]{0,1:T(1,128)S(1)} reduce-window(s32[6,1]{0,1:T(1,128)} %bitcast.35, s32[]{:T(128)} %constant.91.clone.1), window={size=6x1 pad=5_0x0_0}, to_apply=%region_0.0 | reduce-window | flops 30 | bytes 52 | tf_op jit(solution)/shard_map/reduce-window.3
  10.0 0.1 convert_reduce_fusion
  10.1 3.9 %collective-permute-done = bf16[2,192,512]{2,1,0:T(8,128)(2,1)S(1)} collective-permute-done((bf16[2,192,512]{2,1,0:T(8,128)(2,1)S(1)}, bf16[2,192,512]{2,1,0:T(8,128)(2,1)S(1)}, u32[]{:S(2)}, u32[]{:S(2)}) %collective-permute-start) | collective-permute-done | bytes 393248 | tf_op jit(solution)/shard_map/ppermute | solution.py:22
  14.0 0.0 copy-start.4
  14.0 3.5 %collective-permute-start.2 = (bf16[2,192,512]{2,1,0:T(8,128)(2,1)S(1)}, bf16[2,192,512]{2,1,0:T(8,128)(2,1)}, u32[]{:S(2)}, u32[]{:S(2)}) collective-permute-start(bf16[2,192,512]{2,1,0:T(8,128)(2,1)S(1)} %collective-permute-done), channel_id=1, source_target_pairs={{0,4},{4,8},{8,12},{1,5},{5,9},{9,13},{2,6},{6,10},{10,14},{3,7},{... | collective-permute-start | bytes 1179656 | tf_op jit(solution)/shard_map/ppermute | solution.py:22
  17.4 0.0 collective-permute-done.1
  17.5 0.0 copy-start.5
  17.5 2.4 %collective-permute-start.3 = (bf16[2,192,512]{2,1,0:T(8,128)(2,1)S(1)}, bf16[2,192,512]{2,1,0:T(8,128)(2,1)}, u32[]{:S(2)}, u32[]{:S(2)}) collective-permute-start(bf16[2,192,512]{2,1,0:T(8,128)(2,1)S(1)} %collective-permute-done.1), channel_id=1, source_target_pairs={{4,0},{8,4},{12,8},{5,1},{9,5},{13,9},{6,2},{10,6},{14,10},{7,3},{... | collective-permute-start | bytes 1179656 | tf_op jit(solution)/shard_map/ppermute | solution.py:22
  19.8 0.1 convert_reduce_fusion.2
  19.9 0.1 broadcast_in_dim.113
  20.0 0.1 reshape.155
  20.1 0.1 broadcast_in_dim.114
  20.2 0.1 eq.42
  20.3 0.0 copy-start.2
  20.3 0.6 compare_reduce_fusion
  20.9 0.1 collective-permute-start.5
  21.0 0.5 collective-permute-start.6
  21.5 4.5 %collective-permute-done.2 = bf16[2,192,512]{2,1,0:T(8,128)(2,1)} collective-permute-done((bf16[2,192,512]{2,1,0:T(8,128)(2,1)S(1)}, bf16[2,192,512]{2,1,0:T(8,128)(2,1)}, u32[]{:S(2)}, u32[]{:S(2)}) %collective-permute-start.2) | collective-permute-done | bytes 393248 | tf_op jit(solution)/shard_map/ppermute | solution.py:22
  25.9 0.0 collective-permute-start.7
  25.9 3.2 %collective-permute-done.3 = bf16[2,192,512]{2,1,0:T(8,128)(2,1)} collective-permute-done((bf16[2,192,512]{2,1,0:T(8,128)(2,1)S(1)}, bf16[2,192,512]{2,1,0:T(8,128)(2,1)}, u32[]{:S(2)}, u32[]{:S(2)}) %collective-permute-start.3) | collective-permute-done | bytes 393248 | tf_op jit(solution)/shard_map/ppermute | solution.py:22
  29.2 0.0 collective-permute-start.8
  29.2 0.5 convert_element_type.33.flags_ref
  29.7 0.8 %copy.18.qclip_ref = s32[192,1]{1,0:T(8,128)} copy(s32[192,1]{0,1:T(1,128)S(1)} %bitcast.30) | data formatting | bytes 1536 | tf_op jit(solution)/shard_map/broadcast_in_dim | solution.py:250
  30.4 1.0 %select_bitcast_fusion.1 = (bf16[1,192,512]{2,1,0:T(8,128)(2,1)S(1)}, bf16[1,192,512]{2,1,0:T(8,128)(2,1)S(1)}) fusion(bf16[192,512]{1,0:T(8,128)(2,1)} %param.7, pred[512]{0:T(512)(128)(4,1)S(1)} %get-tuple-element.32, pred[512]{0:T(512)(128)(4,1)S(1)} %get-tuple-element.31), kind=kLoop, calls=%fused_computation.18 | loop fusion | flops 196608 | bytes 590848 | tf_op jit(solution)/shard_map/stack | solution.py:278
  31.4 0.8 %multiply_convert_fusion.q_ref = bf16[2,192,512]{2,1,0:T(8,128)(2,1)} fusion(bf16[1,192,512]{2,1,0:T(8,128)(2,1)S(1)} %get-tuple-element.15, bf16[1,192,512]{2,1,0:T(8,128)(2,1)S(1)} %get-tuple-element.14), kind=kLoop, calls=%fused_computation.14 | loop fusion | flops 786432 | bytes 786432 | tf_op jit(solution)/shard_map/convert_element_type | solution.py:227
  32.2 0.0 collective-permute-done.4
  32.2 0.0 collective-permute-done.5
  32.2 0.0 collective-permute-done.6
  32.2 0.0 collective-permute-done.7
  32.2 0.0 collective-permute-done.8
  32.3 0.0 copy-done.4
  32.3 0.0 copy-done.5
  32.3 0.0 copy-done.2
  32.3 10.0 %shard_map.73 = bf16[192,512]{1,0:T(8,128)(2,1)} custom-call(s32[10]{0:T(128)} %convert_element_type.33.flags_ref, bf16[2,192,512]{2,1,0:T(8,128)(2,1)} %multiply_convert_fusion.q_ref, s32[10,3,192]{2,1,0:T(4,128)} %copy-done.2, s32[192,1]{1,0:T(8,128)} %copy.18.qclip_ref, bf16[1,2,192,512]{3,2,1,0:T(8,128)(2,1)} %bitcast.33, ...), custom_call_target="tpu_custom_call" | custom-call | flops 1509949440 | bytes 5111808 | tf_op jit(solution)/shard_map/pallas_call | solution.py:234
  42.2 0.0 copy-start.1
  42.3 1.6 %collective-permute-start.9 = (bf16[192,512]{1,0:T(8,128)(2,1)}, bf16[192,512]{1,0:T(8,128)(2,1)S(1)}, u32[]{:S(2)}, u32[]{:S(2)}) collective-permute-start(bf16[192,512]{1,0:T(8,128)(2,1)} %shard_map.73), channel_id=1, source_target_pairs={{0,2},{2,0},{1,3},{3,1},{4,6},{6,4},{5,7},{7,5},{8,10},{10,8},{9,1... | collective-permute-start | bytes 589832 | tf_op jit(solution)/shard_map/ppermute | solution.py:26
  43.8 5.7 %collective-permute-done.9 = bf16[192,512]{1,0:T(8,128)(2,1)S(1)} collective-permute-done((bf16[192,512]{1,0:T(8,128)(2,1)}, bf16[192,512]{1,0:T(8,128)(2,1)S(1)}, u32[]{:S(2)}, u32[]{:S(2)}) %collective-permute-start.9) | collective-permute-done | bytes 196640 | tf_op jit(solution)/shard_map/ppermute | solution.py:26
  49.5 0.0 copy-done
  49.5 0.4 fusion
  49.9 0.0 copy-done.1
  49.9 0.0 copy-start.3
  49.9 0.4 convolution_add_fusion
  50.3 2.1 %collective-permute-start.11 = (f32[64,1024]{1,0:T(8,128)S(1)}, f32[64,1024]{1,0:T(8,128)S(1)}, u32[]{:S(2)}, u32[]{:S(2)}) collective-permute-start(f32[64,1024]{1,0:T(8,128)S(1)} %get-tuple-element.13), channel_id=1, source_target_pairs={{1,0},{4,1},{5,4},{8,5},{9,8},{12,9},{13,12},{3,2},{6,3},{7,6},{10... | collective-permute-start | bytes 786440 | tf_op jit(solution)/shard_map/ppermute | solution.py:22
  52.4 2.4 %collective-permute-start.10 = (f32[64,1024]{1,0:T(8,128)S(1)}, f32[64,1024]{1,0:T(8,128)S(1)}, u32[]{:S(2)}, u32[]{:S(2)}) collective-permute-start(f32[64,1024]{1,0:T(8,128)S(1)} %get-tuple-element.12), channel_id=1, source_target_pairs={{0,1},{1,4},{4,5},{5,8},{8,9},{9,12},{12,13},{2,3},{3,6},{6,7},{7,... | collective-permute-start | bytes 786440 | tf_op jit(solution)/shard_map/ppermute | solution.py:22
  54.8 0.0 copy-done.3
  54.9 1.5 %collective-permute-done.11 = f32[64,1024]{1,0:T(8,128)S(1)} collective-permute-done((f32[64,1024]{1,0:T(8,128)S(1)}, f32[64,1024]{1,0:T(8,128)S(1)}, u32[]{:S(2)}, u32[]{:S(2)}) %collective-permute-start.11) | collective-permute-done | bytes 262176 | tf_op jit(solution)/shard_map/ppermute | solution.py:22
  56.3 3.8 %collective-permute-done.10 = f32[64,1024]{1,0:T(8,128)S(1)} collective-permute-done((f32[64,1024]{1,0:T(8,128)S(1)}, f32[64,1024]{1,0:T(8,128)S(1)}, u32[]{:S(2)}, u32[]{:S(2)}) %collective-permute-start.10) | collective-permute-done | bytes 262176 | tf_op jit(solution)/shard_map/ppermute | solution.py:22
  60.1 0.4 multiply_reduce_fusion
  60.5 0.8 %multiply_convert_fusion.1 = bf16[192,512]{1,0:T(8,128)(2,1)} fusion(f32[192,1024]{1,0:T(8,128)S(1)} %get-tuple-element.9, s32[]{:T(128)S(6)} %select_n.81, f32[512]{0:T(512)S(1)} %convert_element_type.38, f32[192]{0:T(256)S(1)} %add_rsqrt_fusion), kind=kLoop, calls=%fused_computation.16 | loop fusion | flops 294912 | bytes 592644 | tf_op jit(solution)/shard_map/convert_element_type | solution.py:385
  (17 shorter events, 0.2 us)
Async XLA Ops:
  0.0 49.5 %copy-start = (bf16[1024,1024]{1,0:T(8,128)(2,1)S(1)}, bf16[1024,1024]{1,0:T(8,128)(2,1)}, u32[]{:S(2)}) copy-start(bf16[1024,1024]{1,0:T(8,128)(2,1)} %param.12) | copy-start | bytes 6291460
  1.2 12.7 %collective-permute-start = (bf16[2,192,512]{2,1,0:T(8,128)(2,1)S(1)}, bf16[2,192,512]{2,1,0:T(8,128)(2,1)S(1)}, u32[]{:S(2)}, u32[]{:S(2)}) collective-permute-start(bf16[2,192,512]{2,1,0:T(8,128)(2,1)S(1)} %pad_maximum_fusion.2), channel_id=1, source_target_pairs={{0,4},{4,8},{8,12},{1,5},{5,9},{9,13},{2,6},{6,10},{10,14},{3,7},{... | collective-permute-start | bytes 1179656 | tf_op jit(solution)/shard_map/ppermute | solution.py:22
  4.7 12.7 %collective-permute-start.1 = (bf16[2,192,512]{2,1,0:T(8,128)(2,1)S(1)}, bf16[2,192,512]{2,1,0:T(8,128)(2,1)S(1)}, u32[]{:S(2)}, u32[]{:S(2)}) collective-permute-start(bf16[2,192,512]{2,1,0:T(8,128)(2,1)S(1)} %pad_maximum_fusion.2), channel_id=1, source_target_pairs={{4,0},{8,4},{12,8},{5,1},{9,5},{13,9},{6,2},{10,6},{14,10},{7,3},{... | collective-permute-start | bytes 1179656 | tf_op jit(solution)/shard_map/ppermute | solution.py:22
  7.1 25.2 %collective-permute-start.4 = (bf16[2,192,512]{2,1,0:T(8,128)(2,1)S(1)}, bf16[2,192,512]{2,1,0:T(8,128)(2,1)}, u32[]{:S(2)}, u32[]{:S(2)}) collective-permute-start(bf16[2,192,512]{2,1,0:T(8,128)(2,1)S(1)} %pad_maximum_fusion.2), channel_id=1, source_target_pairs={{0,1},{1,0},{2,3},{3,2},{4,5},{5,4},{6,7},{7,6},{8,9},{9,8},{10,11... | collective-permute-start | bytes 1179656 | tf_op jit(solution)/shard_map/ppermute | solution.py:26
  14.0 18.3 %copy-start.4 = (bf16[2,192,512]{2,1,0:T(8,128)(2,1)}, bf16[2,192,512]{2,1,0:T(8,128)(2,1)S(1)}, u32[]{:S(2)}) copy-start(bf16[2,192,512]{2,1,0:T(8,128)(2,1)S(1)} %collective-permute-done) | copy-start | bytes 1179652
  14.0 12.0 %collective-permute-start.2 = (bf16[2,192,512]{2,1,0:T(8,128)(2,1)S(1)}, bf16[2,192,512]{2,1,0:T(8,128)(2,1)}, u32[]{:S(2)}, u32[]{:S(2)}) collective-permute-start(bf16[2,192,512]{2,1,0:T(8,128)(2,1)S(1)} %collective-permute-done), channel_id=1, source_target_pairs={{0,4},{4,8},{8,12},{1,5},{5,9},{9,13},{2,6},{6,10},{10,14},{3,7},{... | collective-permute-start | bytes 1179656 | tf_op jit(solution)/shard_map/ppermute | solution.py:22
  17.5 14.8 %copy-start.5 = (bf16[2,192,512]{2,1,0:T(8,128)(2,1)}, bf16[2,192,512]{2,1,0:T(8,128)(2,1)S(1)}, u32[]{:S(2)}) copy-start(bf16[2,192,512]{2,1,0:T(8,128)(2,1)S(1)} %collective-permute-done.1) | copy-start | bytes 1179652
  17.5 11.7 %collective-permute-start.3 = (bf16[2,192,512]{2,1,0:T(8,128)(2,1)S(1)}, bf16[2,192,512]{2,1,0:T(8,128)(2,1)}, u32[]{:S(2)}, u32[]{:S(2)}) collective-permute-start(bf16[2,192,512]{2,1,0:T(8,128)(2,1)S(1)} %collective-permute-done.1), channel_id=1, source_target_pairs={{4,0},{8,4},{12,8},{5,1},{9,5},{13,9},{6,2},{10,6},{14,10},{7,3},{... | collective-permute-start | bytes 1179656 | tf_op jit(solution)/shard_map/ppermute | solution.py:22
  20.3 12.0 %copy-start.2 = (s32[10,3,192]{2,1,0:T(4,128)}, s32[10,3,192]{2,1,0:T(4,128)S(1)}, u32[]{:S(2)}) copy-start(s32[10,3,192]{2,1,0:T(4,128)S(1)} %select_bitcast_fusion.2.code_ref) | copy-start | bytes 69124
  20.9 11.3 %collective-permute-start.5 = (bf16[2,192,512]{2,1,0:T(8,128)(2,1)S(1)}, bf16[2,192,512]{2,1,0:T(8,128)(2,1)}, u32[]{:S(2)}, u32[]{:S(2)}) collective-permute-start(bf16[2,192,512]{2,1,0:T(8,128)(2,1)S(1)} %collective-permute-done), channel_id=1, source_target_pairs={{0,1},{1,0},{2,3},{3,2},{4,5},{5,4},{6,7},{7,6},{8,9},{9,8},{10,11... | collective-permute-start | bytes 1179656 | tf_op jit(solution)/shard_map/ppermute | solution.py:26
  21.0 11.3 %collective-permute-start.6 = (bf16[2,192,512]{2,1,0:T(8,128)(2,1)S(1)}, bf16[2,192,512]{2,1,0:T(8,128)(2,1)}, u32[]{:S(2)}, u32[]{:S(2)}) collective-permute-start(bf16[2,192,512]{2,1,0:T(8,128)(2,1)S(1)} %collective-permute-done.1), channel_id=1, source_target_pairs={{0,1},{1,0},{2,3},{3,2},{4,5},{5,4},{6,7},{7,6},{8,9},{9,8},{10,11... | collective-permute-start | bytes 1179656 | tf_op jit(solution)/shard_map/ppermute | solution.py:26
  25.9 6.3 %collective-permute-start.7 = (bf16[2,192,512]{2,1,0:T(8,128)(2,1)}, bf16[2,192,512]{2,1,0:T(8,128)(2,1)}, u32[]{:S(2)}, u32[]{:S(2)}) collective-permute-start(bf16[2,192,512]{2,1,0:T(8,128)(2,1)} %collective-permute-done.2), channel_id=1, source_target_pairs={{0,1},{1,0},{2,3},{3,2},{4,5},{5,4},{6,7},{7,6},{8,9},{9,8},{10,11... | collective-permute-start | bytes 1179656 | tf_op jit(solution)/shard_map/ppermute | solution.py:26
  29.2 3.1 %collective-permute-start.8 = (bf16[2,192,512]{2,1,0:T(8,128)(2,1)}, bf16[2,192,512]{2,1,0:T(8,128)(2,1)}, u32[]{:S(2)}, u32[]{:S(2)}) collective-permute-start(bf16[2,192,512]{2,1,0:T(8,128)(2,1)} %collective-permute-done.3), channel_id=1, source_target_pairs={{0,1},{1,0},{2,3},{3,2},{4,5},{5,4},{6,7},{7,6},{8,9},{9,8},{10,11... | collective-permute-start | bytes 1179656 | tf_op jit(solution)/shard_map/ppermute | solution.py:26
  42.2 7.6 %copy-start.1 = (bf16[192,512]{1,0:T(8,128)(2,1)S(1)}, bf16[192,512]{1,0:T(8,128)(2,1)}, u32[]{:S(2)}) copy-start(bf16[192,512]{1,0:T(8,128)(2,1)} %shard_map.73) | copy-start | bytes 589828
  42.3 7.2 %collective-permute-start.9 = (bf16[192,512]{1,0:T(8,128)(2,1)}, bf16[192,512]{1,0:T(8,128)(2,1)S(1)}, u32[]{:S(2)}, u32[]{:S(2)}) collective-permute-start(bf16[192,512]{1,0:T(8,128)(2,1)} %shard_map.73), channel_id=1, source_target_pairs={{0,2},{2,0},{1,3},{3,1},{4,6},{6,4},{5,7},{7,5},{8,10},{10,8},{9,1... | collective-permute-start | bytes 589832 | tf_op jit(solution)/shard_map/ppermute | solution.py:26
  49.9 4.9 %copy-start.3 = (bf16[512]{0:T(512)(128)(2,1)S(1)}, bf16[512]{0:T(512)(128)(2,1)}, u32[]{:S(2)}) copy-start(bf16[512]{0:T(512)(128)(2,1)} %param.13) | copy-start | bytes 3076
  50.3 6.0 %collective-permute-start.11 = (f32[64,1024]{1,0:T(8,128)S(1)}, f32[64,1024]{1,0:T(8,128)S(1)}, u32[]{:S(2)}, u32[]{:S(2)}) collective-permute-start(f32[64,1024]{1,0:T(8,128)S(1)} %get-tuple-element.13), channel_id=1, source_target_pairs={{1,0},{4,1},{5,4},{8,5},{9,8},{12,9},{13,12},{3,2},{6,3},{7,6},{10... | collective-permute-start | bytes 786440 | tf_op jit(solution)/shard_map/ppermute | solution.py:22
  52.4 7.7 %collective-permute-start.10 = (f32[64,1024]{1,0:T(8,128)S(1)}, f32[64,1024]{1,0:T(8,128)S(1)}, u32[]{:S(2)}, u32[]{:S(2)}) collective-permute-start(f32[64,1024]{1,0:T(8,128)S(1)} %get-tuple-element.12), channel_id=1, source_target_pairs={{0,1},{1,4},{4,5},{5,8},{8,9},{9,12},{12,13},{2,3},{3,6},{6,7},{7,... | collective-permute-start | bytes 786440 | tf_op jit(solution)/shard_map/ppermute | solution.py:22

commit v9 on v5

--- a/solution.py
+++ b/solution.py
@@ -351,8 +351,12 @@
             lax.dynamic_slice_in_dim(out_weight, src * col_count, col_count, 0),
             preferred_element_type=jnp.float32,
         )
-    prev_tail = shifted(projected[row_count - F :], ("seq", "sub"), n_dev, -1)
-    next_head = shifted(projected[:F], ("seq", "sub"), n_dev, 1)
+    prev_tail = shifted(
+        projected[row_count - F :].astype(jnp.bfloat16), ("seq", "sub"), n_dev, -1
+    ).astype(jnp.float32)
+    next_head = shifted(projected[:F].astype(jnp.bfloat16), ("seq", "sub"), n_dev, 1).astype(
+        jnp.float32
+    )
     projected = jnp.concatenate([prev_tail, projected, next_head], axis=0)
 
     positions = token_first + jnp.arange(row_count, dtype=jnp.int32)

time: 61.4 us -> 61.1 us (level)
  waiting for transfers between devices: 23.2 us -> 20.9 us
  Pallas kernels: 7.27 us -> 8.57 us
    ppermute x6, waiting for transfers between devices: 17.5 us -> 16.1 us  [shifted(): return lax.ppermute(x, axis, pairs)]
    pallas_call x1, Pallas kernels: 7.27 us -> 8.57 us  [attend_chunk(): pl.pallas_call(functools.partial(whole_kernel, sources) if final else fun...]
    ppermute x6, waiting for transfers between devices: 5.69 us -> 4.76 us  [rotated(): lax.ppermute(x, axis, [(i, (i + step) % count) for i in range(count)])]
where the time goes in v9:
time: 61.1 us; the launch traced here: 59.9 us
  waiting for transfers between devices  20.9 us (34%)
  starting transfers between devices  20.1 us (33%)
  Pallas kernels  8.57 us (14%)
  other arithmetic  6.29 us (10%)
  local copies, waits for them, and re-layouts  2.98 us (5%)
  matrix products  0.77 us (1%)
    ppermute x6, starting transfers between devices, shifted(): return lax.ppermute(x, axis, pairs)  17.9 us
    ppermute x6, waiting for transfers between devices, shifted(): return lax.ppermute(x, axis, pairs)  16.1 us
    pallas_call x1, Pallas kernels, attend_chunk(): pl.pallas_call(functools.partial(whole_kernel, sources) if final else fun...  8.57 us
    ppermute x6, waiting for transfers between devices, rotated(): lax.ppermute(x, axis, [(i, (i + step) % count) for i in range(count)])  4.76 us
    ppermute x6, starting transfers between devices, rotated(): lax.ppermute(x, axis, [(i, (i + step) % count) for i in range(count)])  2.19 us
    another operation x1, other arithmetic, body(): own = jnp.stack([key_rows, value_rows])  1.97 us
  transfers between devices with their start and end apart: 12, of which 6 were waited for; matrix products, arithmetic and copies ran while one was open for 10% of the time, Pallas kernels for 0%

profile of v9, /device:TPU:20, one launch (start us, length us, event | category | flops | bytes accessed | tf_op | source)
XLA Modules:
  0.0 59.9 jit_solution(11701193578625188675)
XLA Ops:
  0.0 0.0 copy-start
  0.0 0.0 copy-start.1
  0.0 2.0 %pad_maximum_fusion.2 = (bf16[2,192,512]{2,1,0:T(8,128)(2,1)S(1)}, bf16[1,2,192,512]{3,2,1,0:T(8,128)(2,1)}) fusion(bf16[1,192,512]{2,1,0:T(8,128)(2,1)} %bitcast.30, bf16[1,192,512]{2,1,0:T(8,128)(2,1)} %bitcast.31), kind=kLoop, calls=%fused_computation.15 | loop fusion | flops 196608 | bytes 1179648 | tf_op jit(solution)/shard_map/stack | solution.py:302
  2.0 3.5 %collective-permute-start = (bf16[2,192,512]{2,1,0:T(8,128)(2,1)S(1)}, bf16[2,192,512]{2,1,0:T(8,128)(2,1)S(1)}, u32[]{:S(2)}, u32[]{:S(2)}) collective-permute-start(bf16[2,192,512]{2,1,0:T(8,128)(2,1)S(1)} %get-tuple-element.14), channel_id=1, source_target_pairs={{0,4},{4,8},{8,12},{1,5},{5,9},{9,13},{2,6},{6,10},{10,14},{3,7},{... | collective-permute-start | bytes 1179656 | tf_op jit(solution)/shard_map/ppermute | solution.py:22
  5.5 2.4 %collective-permute-start.1 = (bf16[2,192,512]{2,1,0:T(8,128)(2,1)S(1)}, bf16[2,192,512]{2,1,0:T(8,128)(2,1)}, u32[]{:S(2)}, u32[]{:S(2)}) collective-permute-start(bf16[2,192,512]{2,1,0:T(8,128)(2,1)S(1)} %get-tuple-element.14), channel_id=1, source_target_pairs={{4,0},{8,4},{12,8},{5,1},{9,5},{13,9},{6,2},{10,6},{14,10},{7,3},{... | collective-permute-start | bytes 1179656 | tf_op jit(solution)/shard_map/ppermute | solution.py:22
  7.8 0.1 collective-permute-start.4
  8.0 0.1 stack.14
  8.1 0.1 slice.19
  8.2 0.1 reshape.158
  8.3 0.7 %constant_dynamic-slice_fusion = s32[3,24]{1,0:T(4,128)S(1)} fusion(s32[6,24]{1,0:T(8,128)} %param.11, s32[]{:T(128)S(6)} %select_n.75), kind=kLoop, calls=%fused_computation.59 | loop fusion | bytes 580 | tf_op jit(solution)/shard_map/dynamic_slice | solution.py:261
  9.0 0.1 le.32
  9.1 0.1 copy.19
  9.2 0.6 gather_fusion
  9.7 0.1 copy.16
  9.8 0.1 reshape.161
  9.9 0.8 %reduce-window.8 = s32[6,1]{0,1:T(1,128)S(1)} reduce-window(s32[6,1]{0,1:T(1,128)} %bitcast.36, s32[]{:T(128)} %constant.91.clone.1), window={size=6x1 pad=5_0x0_0}, to_apply=%region_0.0 | reduce-window | flops 30 | bytes 52 | tf_op jit(solution)/shard_map/reduce-window.3
  10.7 0.1 convert_reduce_fusion
  10.8 3.9 %collective-permute-done = bf16[2,192,512]{2,1,0:T(8,128)(2,1)S(1)} collective-permute-done((bf16[2,192,512]{2,1,0:T(8,128)(2,1)S(1)}, bf16[2,192,512]{2,1,0:T(8,128)(2,1)S(1)}, u32[]{:S(2)}, u32[]{:S(2)}) %collective-permute-start) | collective-permute-done | bytes 393248 | tf_op jit(solution)/shard_map/ppermute | solution.py:22
  14.7 0.0 copy-start.5
  14.7 3.5 %collective-permute-start.2 = (bf16[2,192,512]{2,1,0:T(8,128)(2,1)S(1)}, bf16[2,192,512]{2,1,0:T(8,128)(2,1)}, u32[]{:S(2)}, u32[]{:S(2)}) collective-permute-start(bf16[2,192,512]{2,1,0:T(8,128)(2,1)S(1)} %collective-permute-done), channel_id=1, source_target_pairs={{0,4},{4,8},{8,12},{1,5},{5,9},{9,13},{2,6},{6,10},{10,14},{3,7},{... | collective-permute-start | bytes 1179656 | tf_op jit(solution)/shard_map/ppermute | solution.py:22
  18.2 0.0 collective-permute-done.1
  18.2 2.4 %collective-permute-start.3 = (bf16[2,192,512]{2,1,0:T(8,128)(2,1)}, bf16[2,192,512]{2,1,0:T(8,128)(2,1)}, u32[]{:S(2)}, u32[]{:S(2)}) collective-permute-start(bf16[2,192,512]{2,1,0:T(8,128)(2,1)} %collective-permute-done.1), channel_id=1, source_target_pairs={{4,0},{8,4},{12,8},{5,1},{9,5},{13,9},{6,2},{10,6},{14,10},{7,3},{... | collective-permute-start | bytes 1179656 | tf_op jit(solution)/shard_map/ppermute | solution.py:22
  20.6 0.1 convert_reduce_fusion.2
  20.7 0.1 broadcast_in_dim.116
  20.8 0.1 reshape.155
  20.9 0.1 broadcast_in_dim.117
  21.0 0.1 eq.42
  21.1 0.0 copy-start.3
  21.1 0.6 compare_reduce_fusion
  21.6 0.1 collective-permute-start.5
  21.7 0.5 collective-permute-start.6
  22.2 4.6 %collective-permute-done.2 = bf16[2,192,512]{2,1,0:T(8,128)(2,1)} collective-permute-done((bf16[2,192,512]{2,1,0:T(8,128)(2,1)S(1)}, bf16[2,192,512]{2,1,0:T(8,128)(2,1)}, u32[]{:S(2)}, u32[]{:S(2)}) %collective-permute-start.2) | collective-permute-done | bytes 393248 | tf_op jit(solution)/shard_map/ppermute | solution.py:22
  26.8 0.0 collective-permute-start.7
  26.8 3.3 %collective-permute-done.3 = bf16[2,192,512]{2,1,0:T(8,128)(2,1)} collective-permute-done((bf16[2,192,512]{2,1,0:T(8,128)(2,1)}, bf16[2,192,512]{2,1,0:T(8,128)(2,1)}, u32[]{:S(2)}, u32[]{:S(2)}) %collective-permute-start.3) | collective-permute-done | bytes 393248 | tf_op jit(solution)/shard_map/ppermute | solution.py:22
  30.1 0.0 collective-permute-start.8
  30.1 0.6 convert_element_type.41.flags_ref
  30.7 0.8 %copy.18.qclip_ref = s32[192,1]{1,0:T(8,128)} copy(s32[192,1]{0,1:T(1,128)S(1)} %bitcast.32) | data formatting | bytes 1536 | tf_op jit(solution)/shard_map/broadcast_in_dim | solution.py:241
  31.5 0.0 copy-done.1
  31.5 0.8 %multiply_convert_fusion.q_ref = bf16[2,192,512]{2,1,0:T(8,128)(2,1)} fusion(bf16[1,192,512]{2,1,0:T(8,128)(2,1)S(1)} %get-tuple-element.17, bf16[1,192,512]{2,1,0:T(8,128)(2,1)S(1)} %get-tuple-element.16), kind=kLoop, calls=%fused_computation.14 | loop fusion | flops 786432 | bytes 786432 | tf_op jit(solution)/shard_map/convert_element_type | solution.py:217
  32.3 0.0 collective-permute-done.4
  32.3 0.0 collective-permute-done.5
  32.3 0.0 collective-permute-done.6
  32.3 0.0 collective-permute-done.7
  32.4 0.0 collective-permute-done.8
  32.4 0.0 copy-done.5
  32.4 0.0 copy-done.3
  32.4 0.0 copy-start.4
  32.4 8.6 %shard_map.73 = bf16[192,512]{1,0:T(8,128)(2,1)} custom-call(s32[10]{0:T(128)} %convert_element_type.41.flags_ref, bf16[2,192,512]{2,1,0:T(8,128)(2,1)} %multiply_convert_fusion.q_ref, s32[10,3,192]{2,1,0:T(4,128)} %copy-done.3, s32[192,1]{1,0:T(8,128)} %copy.18.qclip_ref, bf16[1,2,192,512]{3,2,1,0:T(8,128)(2,1)} %get-tuple-element.15.refs_0_, ...), custom_call_target="tpu_custom_call" | custom-call | flops 1509949440 | bytes 5505024 | tf_op jit(solution)/shard_map/pallas_call | solution.py:224
  41.0 0.0 copy-start.2
  41.0 1.5 %collective-permute-start.9 = (bf16[192,512]{1,0:T(8,128)(2,1)}, bf16[192,512]{1,0:T(8,128)(2,1)S(1)}, u32[]{:S(2)}, u32[]{:S(2)}) collective-permute-start(bf16[192,512]{1,0:T(8,128)(2,1)} %shard_map.73), channel_id=1, source_target_pairs={{0,2},{2,0},{1,3},{3,1},{4,6},{6,4},{5,7},{7,5},{8,10},{10,8},{9,1... | collective-permute-start | bytes 589832 | tf_op jit(solution)/shard_map/ppermute | solution.py:26
  42.5 0.0 copy-done.4
  42.5 4.8 %collective-permute-done.9 = bf16[192,512]{1,0:T(8,128)(2,1)S(1)} collective-permute-done((bf16[192,512]{1,0:T(8,128)(2,1)}, bf16[192,512]{1,0:T(8,128)(2,1)S(1)}, u32[]{:S(2)}, u32[]{:S(2)}) %collective-permute-start.9) | collective-permute-done | bytes 196640 | tf_op jit(solution)/shard_map/ppermute | solution.py:26
  47.3 0.0 copy-done
  47.3 0.4 fusion
  47.7 0.0 copy-done.2
  47.7 0.4 fusion.25
  48.1 4.4 %collective-permute-start.11 = (bf16[64,1024]{1,0:T(8,128)(2,1)S(1)}, bf16[64,1024]{1,0:T(8,128)(2,1)S(1)}, u32[]{:S(2)}, u32[]{:S(2)}) collective-permute-start(bf16[64,1024]{1,0:T(8,128)(2,1)S(1)} %get-tuple-element.13), channel_id=1, source_target_pairs={{1,0},{4,1},{5,4},{8,5},{9,8},{12,9},{13,12},{3,2},{6,3},{7,6},{10... | collective-permute-start | bytes 393224 | tf_op jit(solution)/shard_map/ppermute | solution.py:22
  52.5 1.9 %collective-permute-start.10 = (bf16[64,1024]{1,0:T(8,128)(2,1)S(1)}, bf16[64,1024]{1,0:T(8,128)(2,1)S(1)}, u32[]{:S(2)}, u32[]{:S(2)}) collective-permute-start(bf16[64,1024]{1,0:T(8,128)(2,1)S(1)} %get-tuple-element.12), channel_id=1, source_target_pairs={{0,1},{1,4},{4,5},{5,8},{8,9},{9,12},{12,13},{2,3},{3,6},{6,7},{7,... | collective-permute-start | bytes 393224 | tf_op jit(solution)/shard_map/ppermute | solution.py:22
  54.4 0.6 collective-permute-done.11
  55.0 3.8 %collective-permute-done.10 = bf16[64,1024]{1,0:T(8,128)(2,1)S(1)} collective-permute-done((bf16[64,1024]{1,0:T(8,128)(2,1)S(1)}, bf16[64,1024]{1,0:T(8,128)(2,1)S(1)}, u32[]{:S(2)}, u32[]{:S(2)}) %collective-permute-start.10) | collective-permute-done | bytes 131104 | tf_op jit(solution)/shard_map/ppermute | solution.py:22
  58.8 0.4 multiply_reduce_fusion
  59.1 0.8 %multiply_convert_fusion.1 = bf16[192,512]{1,0:T(8,128)(2,1)} fusion(f32[192,1024]{1,0:T(8,128)S(1)} %get-tuple-element.9, s32[]{:T(128)S(6)} %select_n.81, f32[512]{0:T(512)S(1)} %convert_element_type.48, f32[192]{0:T(256)S(1)} %add_rsqrt_fusion), kind=kLoop, calls=%fused_computation.16 | loop fusion | flops 294912 | bytes 592644 | tf_op jit(solution)/shard_map/convert_element_type | solution.py:374
  (20 shorter events, 0.2 us)
Async XLA Ops:
  0.0 47.3 %copy-start = (bf16[1024,1024]{1,0:T(8,128)(2,1)S(1)}, bf16[1024,1024]{1,0:T(8,128)(2,1)}, u32[]{:S(2)}) copy-start(bf16[1024,1024]{1,0:T(8,128)(2,1)} %param.12) | copy-start | bytes 6291460
  0.0 31.5 %copy-start.1 = (bf16[192,512]{1,0:T(8,128)(2,1)S(1)}, bf16[192,512]{1,0:T(8,128)(2,1)}, u32[]{:S(2)}) copy-start(bf16[192,512]{1,0:T(8,128)(2,1)} %param.7) | copy-start | bytes 589828
  2.0 12.7 %collective-permute-start = (bf16[2,192,512]{2,1,0:T(8,128)(2,1)S(1)}, bf16[2,192,512]{2,1,0:T(8,128)(2,1)S(1)}, u32[]{:S(2)}, u32[]{:S(2)}) collective-permute-start(bf16[2,192,512]{2,1,0:T(8,128)(2,1)S(1)} %get-tuple-element.14), channel_id=1, source_target_pairs={{0,4},{4,8},{8,12},{1,5},{5,9},{9,13},{2,6},{6,10},{10,14},{3,7},{... | collective-permute-start | bytes 1179656 | tf_op jit(solution)/shard_map/ppermute | solution.py:22
  5.5 12.7 %collective-permute-start.1 = (bf16[2,192,512]{2,1,0:T(8,128)(2,1)S(1)}, bf16[2,192,512]{2,1,0:T(8,128)(2,1)}, u32[]{:S(2)}, u32[]{:S(2)}) collective-permute-start(bf16[2,192,512]{2,1,0:T(8,128)(2,1)S(1)} %get-tuple-element.14), channel_id=1, source_target_pairs={{4,0},{8,4},{12,8},{5,1},{9,5},{13,9},{6,2},{10,6},{14,10},{7,3},{... | collective-permute-start | bytes 1179656 | tf_op jit(solution)/shard_map/ppermute | solution.py:22
  7.8 24.5 %collective-permute-start.4 = (bf16[2,192,512]{2,1,0:T(8,128)(2,1)S(1)}, bf16[2,192,512]{2,1,0:T(8,128)(2,1)}, u32[]{:S(2)}, u32[]{:S(2)}) collective-permute-start(bf16[2,192,512]{2,1,0:T(8,128)(2,1)S(1)} %get-tuple-element.14), channel_id=1, source_target_pairs={{0,1},{1,0},{2,3},{3,2},{4,5},{5,4},{6,7},{7,6},{8,9},{9,8},{10,11... | collective-permute-start | bytes 1179656 | tf_op jit(solution)/shard_map/ppermute | solution.py:26
  14.7 17.7 %copy-start.5 = (bf16[2,192,512]{2,1,0:T(8,128)(2,1)}, bf16[2,192,512]{2,1,0:T(8,128)(2,1)S(1)}, u32[]{:S(2)}) copy-start(bf16[2,192,512]{2,1,0:T(8,128)(2,1)S(1)} %collective-permute-done) | copy-start | bytes 1179652
  14.7 12.1 %collective-permute-start.2 = (bf16[2,192,512]{2,1,0:T(8,128)(2,1)S(1)}, bf16[2,192,512]{2,1,0:T(8,128)(2,1)}, u32[]{:S(2)}, u32[]{:S(2)}) collective-permute-start(bf16[2,192,512]{2,1,0:T(8,128)(2,1)S(1)} %collective-permute-done), channel_id=1, source_target_pairs={{0,4},{4,8},{8,12},{1,5},{5,9},{9,13},{2,6},{6,10},{10,14},{3,7},{... | collective-permute-start | bytes 1179656 | tf_op jit(solution)/shard_map/ppermute | solution.py:22
  18.2 11.9 %collective-permute-start.3 = (bf16[2,192,512]{2,1,0:T(8,128)(2,1)}, bf16[2,192,512]{2,1,0:T(8,128)(2,1)}, u32[]{:S(2)}, u32[]{:S(2)}) collective-permute-start(bf16[2,192,512]{2,1,0:T(8,128)(2,1)} %collective-permute-done.1), channel_id=1, source_target_pairs={{4,0},{8,4},{12,8},{5,1},{9,5},{13,9},{6,2},{10,6},{14,10},{7,3},{... | collective-permute-start | bytes 1179656 | tf_op jit(solution)/shard_map/ppermute | solution.py:22
  21.1 11.3 %copy-start.3 = (s32[10,3,192]{2,1,0:T(4,128)}, s32[10,3,192]{2,1,0:T(4,128)S(1)}, u32[]{:S(2)}) copy-start(s32[10,3,192]{2,1,0:T(4,128)S(1)} %select_bitcast_fusion.2.code_ref) | copy-start | bytes 69124
  21.6 10.7 %collective-permute-start.5 = (bf16[2,192,512]{2,1,0:T(8,128)(2,1)S(1)}, bf16[2,192,512]{2,1,0:T(8,128)(2,1)}, u32[]{:S(2)}, u32[]{:S(2)}) collective-permute-start(bf16[2,192,512]{2,1,0:T(8,128)(2,1)S(1)} %collective-permute-done), channel_id=1, source_target_pairs={{0,1},{1,0},{2,3},{3,2},{4,5},{5,4},{6,7},{7,6},{8,9},{9,8},{10,11... | collective-permute-start | bytes 1179656 | tf_op jit(solution)/shard_map/ppermute | solution.py:26
  21.7 10.6 %collective-permute-start.6 = (bf16[2,192,512]{2,1,0:T(8,128)(2,1)}, bf16[2,192,512]{2,1,0:T(8,128)(2,1)}, u32[]{:S(2)}, u32[]{:S(2)}) collective-permute-start(bf16[2,192,512]{2,1,0:T(8,128)(2,1)} %collective-permute-done.1), channel_id=1, source_target_pairs={{0,1},{1,0},{2,3},{3,2},{4,5},{5,4},{6,7},{7,6},{8,9},{9,8},{10,11... | collective-permute-start | bytes 1179656 | tf_op jit(solution)/shard_map/ppermute | solution.py:26
  26.8 5.6 %collective-permute-start.7 = (bf16[2,192,512]{2,1,0:T(8,128)(2,1)}, bf16[2,192,512]{2,1,0:T(8,128)(2,1)}, u32[]{:S(2)}, u32[]{:S(2)}) collective-permute-start(bf16[2,192,512]{2,1,0:T(8,128)(2,1)} %collective-permute-done.2), channel_id=1, source_target_pairs={{0,1},{1,0},{2,3},{3,2},{4,5},{5,4},{6,7},{7,6},{8,9},{9,8},{10,11... | collective-permute-start | bytes 1179656 | tf_op jit(solution)/shard_map/ppermute | solution.py:26
  30.1 2.2 %collective-permute-start.8 = (bf16[2,192,512]{2,1,0:T(8,128)(2,1)}, bf16[2,192,512]{2,1,0:T(8,128)(2,1)}, u32[]{:S(2)}, u32[]{:S(2)}) collective-permute-start(bf16[2,192,512]{2,1,0:T(8,128)(2,1)} %collective-permute-done.3), channel_id=1, source_target_pairs={{0,1},{1,0},{2,3},{3,2},{4,5},{5,4},{6,7},{7,6},{8,9},{9,8},{10,11... | collective-permute-start | bytes 1179656 | tf_op jit(solution)/shard_map/ppermute | solution.py:26
  32.4 10.1 %copy-start.4 = (bf16[512]{0:T(512)(128)(2,1)S(1)}, bf16[512]{0:T(512)(128)(2,1)}, u32[]{:S(2)}) copy-start(bf16[512]{0:T(512)(128)(2,1)} %param.13) | copy-start | bytes 3076
  41.0 6.7 %copy-start.2 = (bf16[192,512]{1,0:T(8,128)(2,1)S(1)}, bf16[192,512]{1,0:T(8,128)(2,1)}, u32[]{:S(2)}) copy-start(bf16[192,512]{1,0:T(8,128)(2,1)} %shard_map.73) | copy-start | bytes 589828
  41.0 6.3 %collective-permute-start.9 = (bf16[192,512]{1,0:T(8,128)(2,1)}, bf16[192,512]{1,0:T(8,128)(2,1)S(1)}, u32[]{:S(2)}, u32[]{:S(2)}) collective-permute-start(bf16[192,512]{1,0:T(8,128)(2,1)} %shard_map.73), channel_id=1, source_target_pairs={{0,2},{2,0},{1,3},{3,1},{4,6},{6,4},{5,7},{7,5},{8,10},{10,8},{9,1... | collective-permute-start | bytes 589832 | tf_op jit(solution)/shard_map/ppermute | solution.py:26
  48.1 6.9 %collective-permute-start.11 = (bf16[64,1024]{1,0:T(8,128)(2,1)S(1)}, bf16[64,1024]{1,0:T(8,128)(2,1)S(1)}, u32[]{:S(2)}, u32[]{:S(2)}) collective-permute-start(bf16[64,1024]{1,0:T(8,128)(2,1)S(1)} %get-tuple-element.13), channel_id=1, source_target_pairs={{1,0},{4,1},{5,4},{8,5},{9,8},{12,9},{13,12},{3,2},{6,3},{7,6},{10... | collective-permute-start | bytes 393224 | tf_op jit(solution)/shard_map/ppermute | solution.py:22
  52.5 6.3 %collective-permute-start.10 = (bf16[64,1024]{1,0:T(8,128)(2,1)S(1)}, bf16[64,1024]{1,0:T(8,128)(2,1)S(1)}, u32[]{:S(2)}, u32[]{:S(2)}) collective-permute-start(bf16[64,1024]{1,0:T(8,128)(2,1)S(1)} %get-tuple-element.12), channel_id=1, source_target_pairs={{0,1},{1,4},{4,5},{5,8},{8,9},{9,12},{12,13},{2,3},{3,6},{6,7},{7,... | collective-permute-start | bytes 393224 | tf_op jit(solution)/shard_map/ppermute | solution.py:22

commit v10 on v8

--- a/solution.py
+++ b/solution.py
@@ -366,8 +366,12 @@
             lax.dynamic_slice_in_dim(out_weight, src * col_count, col_count, 0),
             preferred_element_type=jnp.float32,
         )
-    prev_tail = shifted(projected[row_count - F :], ("seq", "sub"), n_dev, -1)
-    next_head = shifted(projected[:F], ("seq", "sub"), n_dev, 1)
+    prev_tail = shifted(
+        projected[row_count - F :].astype(jnp.bfloat16), ("seq", "sub"), n_dev, -1
+    ).astype(jnp.float32)
+    next_head = shifted(projected[:F].astype(jnp.bfloat16), ("seq", "sub"), n_dev, 1).astype(
+        jnp.float32
+    )
     projected = jnp.concatenate([prev_tail, projected, next_head], axis=0)
 
     positions = token_first + jnp.arange(row_count, dtype=jnp.int32)

time: 62.2 us -> 60.5 us (0.973)
  waiting for transfers between devices: 22.5 us -> 19.9 us
  Pallas kernels: 9.95 us -> 11.3 us
    ppermute x6, waiting for transfers between devices: 16.9 us -> 15.5 us  [shifted(): return lax.ppermute(x, axis, pairs)]
    ppermute x6, waiting for transfers between devices: 5.69 us -> 4.39 us  [rotated(): lax.ppermute(x, axis, [(i, (i + step) % count) for i in range(count)])]
    pallas_call x1, Pallas kernels: 9.95 us -> 11.3 us  [attend_chunk(): pl.pallas_call(functools.partial(whole_kernel, sources) if final else fun...]
  transfers between devices with their start and end apart: 12 -> 12, of which waited for: 6 -> 6; matrix products, arithmetic and copies ran while one was open for 11% -> 12% of each run, Pallas kernels for 0% -> 0%
where the time goes in v10:
time: 60.5 us; the launch traced here: 59.9 us
  waiting for transfers between devices  19.9 us (33%)
  starting transfers between devices  18.2 us (30%)
  Pallas kernels  11.3 us (19%)
  other arithmetic  6.45 us (11%)
  local copies, waits for them, and re-layouts  2.96 us (5%)
  matrix products  0.77 us (1%)
    ppermute x6, starting transfers between devices, shifted(): return lax.ppermute(x, axis, pairs)  16 us
    ppermute x6, waiting for transfers between devices, shifted(): return lax.ppermute(x, axis, pairs)  15.5 us
    pallas_call x1, Pallas kernels, attend_chunk(): pl.pallas_call(functools.partial(whole_kernel, sources) if final else fun...  11.3 us
    ppermute x6, waiting for transfers between devices, rotated(): lax.ppermute(x, axis, [(i, (i + step) % count) for i in range(count)])  4.39 us
    ppermute x6, starting transfers between devices, rotated(): lax.ppermute(x, axis, [(i, (i + step) % count) for i in range(count)])  2.2 us
  transfers between devices with their start and end apart: 12, of which 6 were waited for; matrix products, arithmetic and copies ran while one was open for 12% of the time, Pallas kernels for 0%

profile of v10, /device:TPU:20, one launch (start us, length us, event | category | flops | bytes accessed | tf_op | source)
XLA Modules:
  0.0 59.9 jit_solution(3067198098501302876)
XLA Ops:
  0.0 0.0 copy-start
  0.0 1.2 %pad_maximum_fusion.2 = bf16[2,192,512]{2,1,0:T(8,128)(2,1)S(1)} fusion(bf16[1,192,512]{2,1,0:T(8,128)(2,1)} %bitcast.28, bf16[1,192,512]{2,1,0:T(8,128)(2,1)} %bitcast.29), kind=kLoop, calls=%fused_computation.15 | loop fusion | flops 196608 | bytes 786432 | tf_op jit(solution)/shard_map/stack | solution.py:317
  1.2 3.5 %collective-permute-start = (bf16[2,192,512]{2,1,0:T(8,128)(2,1)S(1)}, bf16[2,192,512]{2,1,0:T(8,128)(2,1)S(1)}, u32[]{:S(2)}, u32[]{:S(2)}) collective-permute-start(bf16[2,192,512]{2,1,0:T(8,128)(2,1)S(1)} %pad_maximum_fusion.2), channel_id=1, source_target_pairs={{0,4},{4,8},{8,12},{1,5},{5,9},{9,13},{2,6},{6,10},{10,14},{3,7},{... | collective-permute-start | bytes 1179656 | tf_op jit(solution)/shard_map/ppermute | solution.py:22
  4.7 2.4 %collective-permute-start.1 = (bf16[2,192,512]{2,1,0:T(8,128)(2,1)S(1)}, bf16[2,192,512]{2,1,0:T(8,128)(2,1)S(1)}, u32[]{:S(2)}, u32[]{:S(2)}) collective-permute-start(bf16[2,192,512]{2,1,0:T(8,128)(2,1)S(1)} %pad_maximum_fusion.2), channel_id=1, source_target_pairs={{4,0},{8,4},{12,8},{5,1},{9,5},{13,9},{6,2},{10,6},{14,10},{7,3},{... | collective-permute-start | bytes 1179656 | tf_op jit(solution)/shard_map/ppermute | solution.py:22
  7.1 0.1 collective-permute-start.4
  7.3 0.1 stack.14
  7.3 0.1 slice.19
  7.5 0.1 reshape.158
  7.5 0.7 %constant_dynamic-slice_fusion = s32[3,24]{1,0:T(4,128)S(1)} fusion(s32[6,24]{1,0:T(8,128)} %param.11, s32[]{:T(128)S(6)} %select_n.75), kind=kLoop, calls=%fused_computation.59 | loop fusion | bytes 580 | tf_op jit(solution)/shard_map/dynamic_slice | solution.py:270
  8.2 0.1 le.32
  8.3 0.1 copy.19
  8.4 0.6 gather_fusion
  9.0 0.1 copy.16
  9.1 0.1 reshape.161
  9.1 0.8 %reduce-window.8 = s32[6,1]{0,1:T(1,128)S(1)} reduce-window(s32[6,1]{0,1:T(1,128)} %bitcast.35, s32[]{:T(128)} %constant.91.clone.1), window={size=6x1 pad=5_0x0_0}, to_apply=%region_0.0 | reduce-window | flops 30 | bytes 52 | tf_op jit(solution)/shard_map/reduce-window.3
  10.0 0.1 convert_reduce_fusion
  10.1 3.9 %collective-permute-done = bf16[2,192,512]{2,1,0:T(8,128)(2,1)S(1)} collective-permute-done((bf16[2,192,512]{2,1,0:T(8,128)(2,1)S(1)}, bf16[2,192,512]{2,1,0:T(8,128)(2,1)S(1)}, u32[]{:S(2)}, u32[]{:S(2)}) %collective-permute-start) | collective-permute-done | bytes 393248 | tf_op jit(solution)/shard_map/ppermute | solution.py:22
  14.0 0.0 copy-start.4
  14.0 3.5 %collective-permute-start.2 = (bf16[2,192,512]{2,1,0:T(8,128)(2,1)S(1)}, bf16[2,192,512]{2,1,0:T(8,128)(2,1)}, u32[]{:S(2)}, u32[]{:S(2)}) collective-permute-start(bf16[2,192,512]{2,1,0:T(8,128)(2,1)S(1)} %collective-permute-done), channel_id=1, source_target_pairs={{0,4},{4,8},{8,12},{1,5},{5,9},{9,13},{2,6},{6,10},{10,14},{3,7},{... | collective-permute-start | bytes 1179656 | tf_op jit(solution)/shard_map/ppermute | solution.py:22
  17.4 0.0 collective-permute-done.1
  17.5 0.0 copy-start.5
  17.5 2.4 %collective-permute-start.3 = (bf16[2,192,512]{2,1,0:T(8,128)(2,1)S(1)}, bf16[2,192,512]{2,1,0:T(8,128)(2,1)}, u32[]{:S(2)}, u32[]{:S(2)}) collective-permute-start(bf16[2,192,512]{2,1,0:T(8,128)(2,1)S(1)} %collective-permute-done.1), channel_id=1, source_target_pairs={{4,0},{8,4},{12,8},{5,1},{9,5},{13,9},{6,2},{10,6},{14,10},{7,3},{... | collective-permute-start | bytes 1179656 | tf_op jit(solution)/shard_map/ppermute | solution.py:22
  19.8 0.1 convert_reduce_fusion.2
  19.9 0.1 broadcast_in_dim.113
  20.0 0.1 reshape.155
  20.1 0.1 broadcast_in_dim.114
  20.2 0.1 eq.42
  20.3 0.0 copy-start.2
  20.3 0.6 compare_reduce_fusion
  20.9 0.1 collective-permute-start.5
  21.0 0.5 collective-permute-start.6
  21.5 4.5 %collective-permute-done.2 = bf16[2,192,512]{2,1,0:T(8,128)(2,1)} collective-permute-done((bf16[2,192,512]{2,1,0:T(8,128)(2,1)S(1)}, bf16[2,192,512]{2,1,0:T(8,128)(2,1)}, u32[]{:S(2)}, u32[]{:S(2)}) %collective-permute-start.2) | collective-permute-done | bytes 393248 | tf_op jit(solution)/shard_map/ppermute | solution.py:22
  25.9 0.0 collective-permute-start.7
  25.9 3.2 %collective-permute-done.3 = bf16[2,192,512]{2,1,0:T(8,128)(2,1)} collective-permute-done((bf16[2,192,512]{2,1,0:T(8,128)(2,1)S(1)}, bf16[2,192,512]{2,1,0:T(8,128)(2,1)}, u32[]{:S(2)}, u32[]{:S(2)}) %collective-permute-start.3) | collective-permute-done | bytes 393248 | tf_op jit(solution)/shard_map/ppermute | solution.py:22
  29.2 0.0 collective-permute-start.8
  29.2 0.6 convert_element_type.41.flags_ref
  29.8 0.8 %copy.18.qclip_ref = s32[192,1]{1,0:T(8,128)} copy(s32[192,1]{0,1:T(1,128)S(1)} %bitcast.30) | data formatting | bytes 1536 | tf_op jit(solution)/shard_map/broadcast_in_dim | solution.py:250
  30.5 1.0 %select_bitcast_fusion.1 = (bf16[1,192,512]{2,1,0:T(8,128)(2,1)S(1)}, bf16[1,192,512]{2,1,0:T(8,128)(2,1)S(1)}) fusion(bf16[192,512]{1,0:T(8,128)(2,1)} %param.7, pred[512]{0:T(512)(128)(4,1)S(1)} %get-tuple-element.34, pred[512]{0:T(512)(128)(4,1)S(1)} %get-tuple-element.33), kind=kLoop, calls=%fused_computation.18 | loop fusion | flops 196608 | bytes 590848 | tf_op jit(solution)/shard_map/stack | solution.py:278
  31.5 0.8 %multiply_convert_fusion.q_ref = bf16[2,192,512]{2,1,0:T(8,128)(2,1)} fusion(bf16[1,192,512]{2,1,0:T(8,128)(2,1)S(1)} %get-tuple-element.15, bf16[1,192,512]{2,1,0:T(8,128)(2,1)S(1)} %get-tuple-element.14), kind=kLoop, calls=%fused_computation.14 | loop fusion | flops 786432 | bytes 786432 | tf_op jit(solution)/shard_map/convert_element_type | solution.py:227
  32.3 0.0 collective-permute-done.4
  32.3 0.0 collective-permute-done.5
  32.3 0.0 collective-permute-done.6
  32.3 0.0 collective-permute-done.7
  32.3 0.0 collective-permute-done.8
  32.3 0.0 copy-done.4
  32.3 0.0 copy-done.5
  32.3 0.0 copy-done.2
  32.4 0.0 copy-start.3
  32.4 11.3 %shard_map.73 = bf16[192,512]{1,0:T(8,128)(2,1)} custom-call(s32[10]{0:T(128)} %convert_element_type.41.flags_ref, bf16[2,192,512]{2,1,0:T(8,128)(2,1)} %multiply_convert_fusion.q_ref, s32[10,3,192]{2,1,0:T(4,128)} %copy-done.2, s32[192,1]{1,0:T(8,128)} %copy.18.qclip_ref, bf16[1,2,192,512]{3,2,1,0:T(8,128)(2,1)} %bitcast.33, ...), custom_call_target="tpu_custom_call" | custom-call | flops 1509949440 | bytes 5111808 | tf_op jit(solution)/shard_map/pallas_call | solution.py:234
  43.6 0.0 copy-start.1
  43.6 1.6 %collective-permute-start.9 = (bf16[192,512]{1,0:T(8,128)(2,1)}, bf16[192,512]{1,0:T(8,128)(2,1)S(1)}, u32[]{:S(2)}, u32[]{:S(2)}) collective-permute-start(bf16[192,512]{1,0:T(8,128)(2,1)} %shard_map.73), channel_id=1, source_target_pairs={{0,2},{2,0},{1,3},{3,1},{4,6},{6,4},{5,7},{7,5},{8,10},{10,8},{9,1... | collective-permute-start | bytes 589832 | tf_op jit(solution)/shard_map/ppermute | solution.py:26
  45.2 0.0 copy-done.3
  45.2 4.4 %collective-permute-done.9 = bf16[192,512]{1,0:T(8,128)(2,1)S(1)} collective-permute-done((bf16[192,512]{1,0:T(8,128)(2,1)}, bf16[192,512]{1,0:T(8,128)(2,1)S(1)}, u32[]{:S(2)}, u32[]{:S(2)}) %collective-permute-start.9) | collective-permute-done | bytes 196640 | tf_op jit(solution)/shard_map/ppermute | solution.py:26
  49.6 0.0 copy-done
  49.6 0.4 fusion
  50.0 0.0 copy-done.1
  50.0 0.4 fusion.24
  50.4 2.0 %collective-permute-start.11 = (bf16[64,1024]{1,0:T(8,128)(2,1)S(1)}, bf16[64,1024]{1,0:T(8,128)(2,1)S(1)}, u32[]{:S(2)}, u32[]{:S(2)}) collective-permute-start(bf16[64,1024]{1,0:T(8,128)(2,1)S(1)} %get-tuple-element.13), channel_id=1, source_target_pairs={{1,0},{4,1},{5,4},{8,5},{9,8},{12,9},{13,12},{3,2},{6,3},{7,6},{10... | collective-permute-start | bytes 393224 | tf_op jit(solution)/shard_map/ppermute | solution.py:22
  52.5 2.3 %collective-permute-start.10 = (bf16[64,1024]{1,0:T(8,128)(2,1)S(1)}, bf16[64,1024]{1,0:T(8,128)(2,1)S(1)}, u32[]{:S(2)}, u32[]{:S(2)}) collective-permute-start(bf16[64,1024]{1,0:T(8,128)(2,1)S(1)} %get-tuple-element.12), channel_id=1, source_target_pairs={{0,1},{1,4},{4,5},{5,8},{8,9},{9,12},{12,13},{2,3},{3,6},{6,7},{7,... | collective-permute-start | bytes 393224 | tf_op jit(solution)/shard_map/ppermute | solution.py:22
  54.8 0.2 collective-permute-done.11
  55.0 3.8 %collective-permute-done.10 = bf16[64,1024]{1,0:T(8,128)(2,1)S(1)} collective-permute-done((bf16[64,1024]{1,0:T(8,128)(2,1)S(1)}, bf16[64,1024]{1,0:T(8,128)(2,1)S(1)}, u32[]{:S(2)}, u32[]{:S(2)}) %collective-permute-start.10) | collective-permute-done | bytes 131104 | tf_op jit(solution)/shard_map/ppermute | solution.py:22
  58.8 0.4 multiply_reduce_fusion
  59.1 0.8 %multiply_convert_fusion.1 = bf16[192,512]{1,0:T(8,128)(2,1)} fusion(f32[192,1024]{1,0:T(8,128)S(1)} %get-tuple-element.9, s32[]{:T(128)S(6)} %select_n.81, f32[512]{0:T(512)S(1)} %convert_element_type.48, f32[192]{0:T(256)S(1)} %add_rsqrt_fusion), kind=kLoop, calls=%fused_computation.16 | loop fusion | flops 294912 | bytes 592644 | tf_op jit(solution)/shard_map/convert_element_type | solution.py:389
  (19 shorter events, 0.2 us)
Async XLA Ops:
  0.0 49.6 %copy-start = (bf16[1024,1024]{1,0:T(8,128)(2,1)S(1)}, bf16[1024,1024]{1,0:T(8,128)(2,1)}, u32[]{:S(2)}) copy-start(bf16[1024,1024]{1,0:T(8,128)(2,1)} %param.12) | copy-start | bytes 6291460
  1.2 12.7 %collective-permute-start = (bf16[2,192,512]{2,1,0:T(8,128)(2,1)S(1)}, bf16[2,192,512]{2,1,0:T(8,128)(2,1)S(1)}, u32[]{:S(2)}, u32[]{:S(2)}) collective-permute-start(bf16[2,192,512]{2,1,0:T(8,128)(2,1)S(1)} %pad_maximum_fusion.2), channel_id=1, source_target_pairs={{0,4},{4,8},{8,12},{1,5},{5,9},{9,13},{2,6},{6,10},{10,14},{3,7},{... | collective-permute-start | bytes 1179656 | tf_op jit(solution)/shard_map/ppermute | solution.py:22
  4.7 12.7 %collective-permute-start.1 = (bf16[2,192,512]{2,1,0:T(8,128)(2,1)S(1)}, bf16[2,192,512]{2,1,0:T(8,128)(2,1)S(1)}, u32[]{:S(2)}, u32[]{:S(2)}) collective-permute-start(bf16[2,192,512]{2,1,0:T(8,128)(2,1)S(1)} %pad_maximum_fusion.2), channel_id=1, source_target_pairs={{4,0},{8,4},{12,8},{5,1},{9,5},{13,9},{6,2},{10,6},{14,10},{7,3},{... | collective-permute-start | bytes 1179656 | tf_op jit(solution)/shard_map/ppermute | solution.py:22
  7.1 25.2 %collective-permute-start.4 = (bf16[2,192,512]{2,1,0:T(8,128)(2,1)S(1)}, bf16[2,192,512]{2,1,0:T(8,128)(2,1)}, u32[]{:S(2)}, u32[]{:S(2)}) collective-permute-start(bf16[2,192,512]{2,1,0:T(8,128)(2,1)S(1)} %pad_maximum_fusion.2), channel_id=1, source_target_pairs={{0,1},{1,0},{2,3},{3,2},{4,5},{5,4},{6,7},{7,6},{8,9},{9,8},{10,11... | collective-permute-start | bytes 1179656 | tf_op jit(solution)/shard_map/ppermute | solution.py:26
  14.0 18.4 %copy-start.4 = (bf16[2,192,512]{2,1,0:T(8,128)(2,1)}, bf16[2,192,512]{2,1,0:T(8,128)(2,1)S(1)}, u32[]{:S(2)}) copy-start(bf16[2,192,512]{2,1,0:T(8,128)(2,1)S(1)} %collective-permute-done) | copy-start | bytes 1179652
  14.0 12.0 %collective-permute-start.2 = (bf16[2,192,512]{2,1,0:T(8,128)(2,1)S(1)}, bf16[2,192,512]{2,1,0:T(8,128)(2,1)}, u32[]{:S(2)}, u32[]{:S(2)}) collective-permute-start(bf16[2,192,512]{2,1,0:T(8,128)(2,1)S(1)} %collective-permute-done), channel_id=1, source_target_pairs={{0,4},{4,8},{8,12},{1,5},{5,9},{9,13},{2,6},{6,10},{10,14},{3,7},{... | collective-permute-start | bytes 1179656 | tf_op jit(solution)/shard_map/ppermute | solution.py:22
  17.5 14.9 %copy-start.5 = (bf16[2,192,512]{2,1,0:T(8,128)(2,1)}, bf16[2,192,512]{2,1,0:T(8,128)(2,1)S(1)}, u32[]{:S(2)}) copy-start(bf16[2,192,512]{2,1,0:T(8,128)(2,1)S(1)} %collective-permute-done.1) | copy-start | bytes 1179652
  17.5 11.7 %collective-permute-start.3 = (bf16[2,192,512]{2,1,0:T(8,128)(2,1)S(1)}, bf16[2,192,512]{2,1,0:T(8,128)(2,1)}, u32[]{:S(2)}, u32[]{:S(2)}) collective-permute-start(bf16[2,192,512]{2,1,0:T(8,128)(2,1)S(1)} %collective-permute-done.1), channel_id=1, source_target_pairs={{4,0},{8,4},{12,8},{5,1},{9,5},{13,9},{6,2},{10,6},{14,10},{7,3},{... | collective-permute-start | bytes 1179656 | tf_op jit(solution)/shard_map/ppermute | solution.py:22
  20.3 12.0 %copy-start.2 = (s32[10,3,192]{2,1,0:T(4,128)}, s32[10,3,192]{2,1,0:T(4,128)S(1)}, u32[]{:S(2)}) copy-start(s32[10,3,192]{2,1,0:T(4,128)S(1)} %select_bitcast_fusion.2.code_ref) | copy-start | bytes 69124
  20.9 11.4 %collective-permute-start.5 = (bf16[2,192,512]{2,1,0:T(8,128)(2,1)S(1)}, bf16[2,192,512]{2,1,0:T(8,128)(2,1)}, u32[]{:S(2)}, u32[]{:S(2)}) collective-permute-start(bf16[2,192,512]{2,1,0:T(8,128)(2,1)S(1)} %collective-permute-done), channel_id=1, source_target_pairs={{0,1},{1,0},{2,3},{3,2},{4,5},{5,4},{6,7},{7,6},{8,9},{9,8},{10,11... | collective-permute-start | bytes 1179656 | tf_op jit(solution)/shard_map/ppermute | solution.py:26
  21.0 11.3 %collective-permute-start.6 = (bf16[2,192,512]{2,1,0:T(8,128)(2,1)S(1)}, bf16[2,192,512]{2,1,0:T(8,128)(2,1)}, u32[]{:S(2)}, u32[]{:S(2)}) collective-permute-start(bf16[2,192,512]{2,1,0:T(8,128)(2,1)S(1)} %collective-permute-done.1), channel_id=1, source_target_pairs={{0,1},{1,0},{2,3},{3,2},{4,5},{5,4},{6,7},{7,6},{8,9},{9,8},{10,11... | collective-permute-start | bytes 1179656 | tf_op jit(solution)/shard_map/ppermute | solution.py:26
  25.9 6.4 %collective-permute-start.7 = (bf16[2,192,512]{2,1,0:T(8,128)(2,1)}, bf16[2,192,512]{2,1,0:T(8,128)(2,1)}, u32[]{:S(2)}, u32[]{:S(2)}) collective-permute-start(bf16[2,192,512]{2,1,0:T(8,128)(2,1)} %collective-permute-done.2), channel_id=1, source_target_pairs={{0,1},{1,0},{2,3},{3,2},{4,5},{5,4},{6,7},{7,6},{8,9},{9,8},{10,11... | collective-permute-start | bytes 1179656 | tf_op jit(solution)/shard_map/ppermute | solution.py:26
  29.2 3.1 %collective-permute-start.8 = (bf16[2,192,512]{2,1,0:T(8,128)(2,1)}, bf16[2,192,512]{2,1,0:T(8,128)(2,1)}, u32[]{:S(2)}, u32[]{:S(2)}) collective-permute-start(bf16[2,192,512]{2,1,0:T(8,128)(2,1)} %collective-permute-done.3), channel_id=1, source_target_pairs={{0,1},{1,0},{2,3},{3,2},{4,5},{5,4},{6,7},{7,6},{8,9},{9,8},{10,11... | collective-permute-start | bytes 1179656 | tf_op jit(solution)/shard_map/ppermute | solution.py:26
  32.4 12.8 %copy-start.3 = (bf16[512]{0:T(512)(128)(2,1)S(1)}, bf16[512]{0:T(512)(128)(2,1)}, u32[]{:S(2)}) copy-start(bf16[512]{0:T(512)(128)(2,1)} %param.13) | copy-start | bytes 3076
  43.6 6.3 %copy-start.1 = (bf16[192,512]{1,0:T(8,128)(2,1)S(1)}, bf16[192,512]{1,0:T(8,128)(2,1)}, u32[]{:S(2)}) copy-start(bf16[192,512]{1,0:T(8,128)(2,1)} %shard_map.73) | copy-start | bytes 589828
  43.6 5.9 %collective-permute-start.9 = (bf16[192,512]{1,0:T(8,128)(2,1)}, bf16[192,512]{1,0:T(8,128)(2,1)S(1)}, u32[]{:S(2)}, u32[]{:S(2)}) collective-permute-start(bf16[192,512]{1,0:T(8,128)(2,1)} %shard_map.73), channel_id=1, source_target_pairs={{0,2},{2,0},{1,3},{3,1},{4,6},{6,4},{5,7},{7,5},{8,10},{10,8},{9,1... | collective-permute-start | bytes 589832 | tf_op jit(solution)/shard_map/ppermute | solution.py:26
  50.4 4.6 %collective-permute-start.11 = (bf16[64,1024]{1,0:T(8,128)(2,1)S(1)}, bf16[64,1024]{1,0:T(8,128)(2,1)S(1)}, u32[]{:S(2)}, u32[]{:S(2)}) collective-permute-start(bf16[64,1024]{1,0:T(8,128)(2,1)S(1)} %get-tuple-element.13), channel_id=1, source_target_pairs={{1,0},{4,1},{5,4},{8,5},{9,8},{12,9},{13,12},{3,2},{6,3},{7,6},{10... | collective-permute-start | bytes 393224 | tf_op jit(solution)/shard_map/ppermute | solution.py:22
  52.5 6.3 %collective-permute-start.10 = (bf16[64,1024]{1,0:T(8,128)(2,1)S(1)}, bf16[64,1024]{1,0:T(8,128)(2,1)S(1)}, u32[]{:S(2)}, u32[]{:S(2)}) collective-permute-start(bf16[64,1024]{1,0:T(8,128)(2,1)S(1)} %get-tuple-element.12), channel_id=1, source_target_pairs={{0,1},{1,4},{4,5},{5,8},{8,9},{9,12},{12,13},{2,3},{3,6},{6,7},{7,... | collective-permute-start | bytes 393224 | tf_op jit(solution)/shard_map/ppermute | solution.py:22
